TPU v7x, 1024 devices: a whole 4x4x32 slice. The times are simulated.
1024 devices in a mesh: row: 8 (over y, core), col: 128 (over x, z).
Axes of the slice: x: 4, y: 4, z: 32, core: 2. Of those that a mesh axis runs over, the one named last changes fastest.
Arguments:
- trailing: float32 [12288, 32768], P('row', 'col'), may hold values from -6 to 6
- leaf_v: float32 [12288, 256], P(('row', 'col')), may hold values from -0.15625 to 0.15625
- leaf_t: float32 [2048, 256], P(('row', 'col')), may hold values from -0.375 to 0.375
- tree_y: float32 [4096, 256], P(('row', 'col')), may hold values from -0.375 to 0.375
- tree_t: float32 [4096, 256], P(('row', 'col')), may hold values from -0.375 to 0.375
Outputs:
- updated: float32 [12288, 32768], P('row', 'col')
All inputs are finite; a program needn't handle non-finite values.
Results may differ from a plain program's by a relative error of at most 0.00011.
Values sent between devices are 32-bit elements; how exact they have to be, the bound alone decides.
No kernel may reach another device: no remote copies, remote signals or barrier semaphores. Data moves between devices by JAX's collectives and lax.ppermute only.
A program may use at most 32 MiB of HBM per device.

v0:
```python
import jax
import jax.numpy as jnp
from jax import lax
from jax.sharding import PartitionSpec as P


def swapped(shard, axis, stride):
    return lax.ppermute(shard, axis, [(i, i ^ 1 << stride) for i in range(lax.axis_size(axis))])


def unit_lower(piece):
    rows = lax.broadcasted_iota(jnp.int32, piece.shape, 0)
    cols = lax.broadcasted_iota(jnp.int32, piece.shape, 1)
    return jnp.where(
        rows < cols, jnp.float32(0.0), jnp.where(rows == cols, jnp.float32(1.0), piece)
    )


def inner(left, right):
    return lax.dot_general(
        left,
        right,
        (((0,), (0,)), ((), ())),
        precision=lax.Precision.HIGHEST,
        preferred_element_type=jnp.float32,
    )


def matmul(left, right):
    return jnp.dot(left, right, precision=lax.Precision.HIGHEST, preferred_element_type=jnp.float32)


def combine(top_rows, y_mine, t_mine, level):
    lower_side = lax.axis_index("row") // 2**level % 2 == 0
    outgoing_refl = jnp.where(lower_side, y_mine, t_mine)
    half = top_rows.shape[1] // 2
    first = top_rows[:, :half]
    second = top_rows[:, half:]
    kept = jnp.where(lower_side, first, second)
    outgoing = jnp.where(lower_side, second, first)
    incoming, partner_refl = swapped((outgoing, outgoing_refl), "row", level)
    refl_y = jnp.where(lower_side, y_mine, partner_refl)
    refl_t = jnp.triu(jnp.where(lower_side, partner_refl, t_mine))
    lower_top = jnp.where(lower_side, kept, incoming)
    upper_top = jnp.where(lower_side, incoming, kept)
    coeffs = inner(refl_t, lower_top + inner(refl_y, upper_top))
    new_lower = lower_top - coeffs
    new_upper = upper_top - matmul(refl_y, coeffs)
    mine = jnp.where(lower_side, new_lower, new_upper)
    theirs = jnp.where(lower_side, new_upper, new_lower)
    returned = swapped(theirs, "row", level)
    return jnp.where(
        lower_side,
        jnp.concatenate([mine, returned], axis=1),
        jnp.concatenate([returned, mine], axis=1),
    )


def local(trailing, leaf_v, leaf_t, tree_y, tree_t):
    width = leaf_v.shape[1]
    v_rows, t_leaf, y_tree, t_tree = (
        lax.all_gather(leaf_v, "col", axis=0, tiled=True),
        lax.all_gather(leaf_t, "col", axis=0, tiled=True),
        lax.all_gather(tree_y, "col", axis=0, tiled=True),
        lax.all_gather(tree_t, "col", axis=0, tiled=True),
    )
    v_rows = unit_lower(v_rows)
    coeffs = inner(jnp.triu(t_leaf), inner(v_rows, trailing))
    updated = trailing - matmul(v_rows, coeffs)
    top_rows = updated[:width]
    rest_rows = updated[width:]
    tree_depth = y_tree.shape[0] // width
    for level in range(tree_depth):
        low = level * width
        high = (level + 1) * width
        y_mine = y_tree[low:high]
        t_mine = t_tree[low:high]
        top_rows = combine(top_rows, y_mine, t_mine, level)
    return jnp.concatenate([top_rows, rest_rows], axis=0)


def solution(mesh):
    in_specs = (
        P("row", "col"),
        P(("row", "col"), None),
        P(("row", "col"), None),
        P(("row", "col"), None),
        P(("row", "col"), None),
    )
    out_specs = P("row", "col")
    return jax.shard_map(local, mesh=mesh, in_specs=in_specs, out_specs=out_specs, check_vma=False)
```

profile of v0, /device:TPU:1, one launch (start us, length us, event | category | flops | bytes accessed | tf_op | source)
XLA Modules:
  0.0 589.5 jit_solution(10583844672807343434)
XLA Ops:
  6.5 0.0 copy-start.6
  6.5 0.0 all-gather.6.cloned.1.call-start
  6.5 0.7 all-gather.6.cloned.1.call-update
  7.3 141.2 %all-gather.2 = f32[128,4,256]{2,1,0:T(4,128)S(1)} all-gather(f32[1,4,256]{2,1,0:T(4,128)} %bitcast.12), channel_id=1, replica_groups=mesh['row'=8,'col'=128] {'col'}, dimensions={0}, use_global_device_ids=true | all-gather | bytes 528384 | tf_op jit(solution)/shard_map/all_gather | solution.py:64
  148.5 0.7 fusion.31
  149.2 0.1 reshape.8
  149.3 0.1 copy.26
  149.4 0.0 copy-done.6
  149.5 136.5 %all-gather.3 = f32[128,4,256]{2,1,0:T(4,128)S(1)} all-gather(f32[1,4,256]{2,1,0:T(4,128)S(1)} %bitcast.13), channel_id=1, replica_groups=mesh['row'=8,'col'=128] {'col'}, dimensions={0}, use_global_device_ids=true | all-gather | bytes 528384 | tf_op jit(solution)/shard_map/all_gather | solution.py:65
  285.9 0.0 copy-start.7
  285.9 0.8 fusion.30
  286.7 0.0 copy-start.1
  286.7 0.1 reshape.9
  286.8 0.1 copy.27
  286.9 0.0 copy-start.2
  286.9 0.7 broadcast_select_fusion.1
  287.6 57.8 %collective-permute-start.1 = (f32[256,256]{0,1:T(8,128)}, f32[256,256]{0,1:T(8,128)}, u32[]{:S(2)}, u32[]{:S(2)}) collective-permute-start(f32[256,256]{0,1:T(8,128)} %broadcast_select_fusion.1), channel_id=1, source_target_pairs={{0,128},{128,0},{256,384},{384,256},{512,640},{640,512},{768,896},... | collective-permute-start | bytes 786440 | tf_op jit(solution)/shard_map/ppermute | solution.py:8
  345.5 0.0 copy-done.7
  345.5 145.0 %all-gather.1 = f32[128,2,256]{2,1,0:T(2,128)S(1)} all-gather(f32[1,2,256]{2,1,0:T(2,128)S(1)} %bitcast.14), channel_id=1, replica_groups=mesh['row'=8,'col'=128] {'col'}, dimensions={0}, use_global_device_ids=true | all-gather | bytes 264192 | tf_op jit(solution)/shard_map/all_gather | solution.py:63
  490.5 0.2 reshape.3
  490.7 0.8 copy.24
  491.6 0.0 copy-done.1
  491.6 1.6 copy.25
  493.2 0.0 copy-done.2
  493.2 0.0 all-gather.6.cloned.1.call-done
  493.2 1.6 reshape.1
  494.8 0.0 copy-start.4
  494.8 0.0 copy-start
  494.8 2.5 fusion
  497.4 0.0 copy-done.4
  497.4 0.4 fusion.11
  497.8 0.0 copy-done
  497.8 1.6 convolution_subtract_fusion
  499.5 0.0 copy-start.5
  499.5 0.0 copy-start.3
  499.5 55.8 %collective-permute-start = (f32[256,128]{0,1:T(8,128)S(1)}, f32[256,128]{0,1:T(8,128)S(1)}, u32[]{:S(2)}, u32[]{:S(2)}) collective-permute-start(f32[256,128]{0,1:T(8,128)S(1)} %get-tuple-element.6), channel_id=1, source_target_pairs={{0,128},{128,0},{256,384},{384,256},{512,640},{640,512},{768,896},... | collective-permute-start | bytes 393224 | tf_op jit(solution)/shard_map/ppermute | solution.py:8
  555.4 1.0 reshape.10
  556.4 0.1 copy.31
  556.6 0.0 copy-done.5
  556.6 0.1 reshape.11
  556.7 0.1 copy.32
  556.8 0.0 collective-permute-done.1
  556.8 0.0 collective-permute-done
  556.8 1.4 convolution_add_fusion.1
  558.2 0.0 copy-done.3
  558.2 0.4 fusion.8
  558.7 1.3 broadcast_select_fusion.9
  559.9 1.9 collective-permute-start.2
  561.9 3.2 collective-permute-start.4
  565.1 0.0 collective-permute-done.2
  565.2 2.1 collective-permute-start.3
  567.3 3.9 collective-permute-done.4
  571.2 2.8 collective-permute-done.3
  574.0 0.4 convolution_add_fusion
  574.4 0.4 fusion.5
  574.8 0.3 broadcast_select_fusion.13
  575.1 3.2 collective-permute-start.5
  578.3 0.1 slice.51
  578.4 2.4 collective-permute-done.5
  580.9 0.2 pad_maximum_fusion
  581.1 1.6 copy.36
  (6 shorter events, 0.1 us)
Async XLA Ops:
  6.5 142.9 %copy-start.6 = (f32[4,256]{1,0:T(4,128)S(1)}, f32[4,256]{1,0:T(4,128)}, u32[]{:S(2)}) copy-start(f32[4,256]{1,0:T(4,128)} %param.9) | copy-start | bytes 12292
  6.5 486.6 %all-gather.6.cloned.1.call-start = ((), (), s32[]{:S(2)}) async-start(), calls=%async_computation | async-start | bytes 2113536 | tf_op jit(solution)/shard_map/all_gather | solution.py:62
  285.9 59.6 %copy-start.7 = (f32[2,256]{1,0:T(2,128)S(1)}, f32[2,256]{1,0:T(2,128)}, u32[]{:S(2)}) copy-start(f32[2,256]{1,0:T(2,128)} %param.7) | copy-start | bytes 6148
  286.7 204.9 %copy-start.1 = (f32[1536,256]{1,0:T(8,128)S(1)}, f32[1536,256]{1,0:T(8,128)}, u32[]{:S(2)}) copy-start(f32[1536,256]{1,0:T(8,128)} %param.5) | copy-start | bytes 4718596
  286.9 206.3 %copy-start.2 = (f32[256,256]{0,1:T(8,128)}, f32[256,256]{0,1:T(8,128)S(1)}, u32[]{:S(2)}) copy-start(f32[256,256]{0,1:T(8,128)S(1)} %copy.27) | copy-start | bytes 786436
  287.6 269.2 %collective-permute-start.1 = (f32[256,256]{0,1:T(8,128)}, f32[256,256]{0,1:T(8,128)}, u32[]{:S(2)}, u32[]{:S(2)}) collective-permute-start(f32[256,256]{0,1:T(8,128)} %broadcast_select_fusion.1), channel_id=1, source_target_pairs={{0,128},{128,0},{256,384},{384,256},{512,640},{640,512},{768,896},... | collective-permute-start | bytes 786440 | tf_op jit(solution)/shard_map/ppermute | solution.py:8
  494.8 2.6 copy-start.4
  494.8 3.0 copy-start
  499.5 57.1 %copy-start.5 = (f32[64,4,256]{2,1,0:T(4,128)S(1)}, f32[64,4,256]{2,1,0:T(4,128)}, u32[]{:S(2)}) copy-start(f32[64,4,256]{2,1,0:T(4,128)} %get-tuple-element.12) | copy-start | bytes 786436
  499.5 58.7 %copy-start.3 = (f32[256,256]{0,1:T(8,128)S(1)}, f32[256,256]{0,1:T(8,128)}, u32[]{:S(2)}) copy-start(f32[256,256]{0,1:T(8,128)} %copy-done.2) | copy-start | bytes 786436
  499.5 57.3 %collective-permute-start = (f32[256,128]{0,1:T(8,128)S(1)}, f32[256,128]{0,1:T(8,128)S(1)}, u32[]{:S(2)}, u32[]{:S(2)}) collective-permute-start(f32[256,128]{0,1:T(8,128)S(1)} %get-tuple-element.6), channel_id=1, source_target_pairs={{0,128},{128,0},{256,384},{384,256},{512,640},{640,512},{768,896},... | collective-permute-start | bytes 393224 | tf_op jit(solution)/shard_map/ppermute | solution.py:8
  559.9 5.2 collective-permute-start.2
  561.9 9.3 %collective-permute-start.4 = (f32[256,256]{0,1:T(8,128)S(1)}, f32[256,256]{0,1:T(8,128)S(1)}, u32[]{:S(2)}, u32[]{:S(2)}) collective-permute-start(f32[256,256]{0,1:T(8,128)S(1)} %broadcast_select_fusion.3), channel_id=1, source_target_pairs={{0,256},{128,384},{256,0},{384,128},{512,768},{640,896},{768,512},... | collective-permute-start | bytes 786440 | tf_op jit(solution)/shard_map/ppermute | solution.py:8
  565.2 8.8 %collective-permute-start.3 = (f32[256,128]{0,1:T(8,128)S(1)}, f32[256,128]{0,1:T(8,128)S(1)}, u32[]{:S(2)}, u32[]{:S(2)}) collective-permute-start(f32[256,128]{0,1:T(8,128)S(1)} %get-tuple-element.16), channel_id=1, source_target_pairs={{0,256},{128,384},{256,0},{384,128},{512,768},{640,896},{768,512},... | collective-permute-start | bytes 393224 | tf_op jit(solution)/shard_map/ppermute | solution.py:8
  575.1 5.7 collective-permute-start.5
Sparse Core Ops, SparseCore 0:
  11.4 257.3 all-gather.5
where the time goes:
time: 591 us; the launch traced here: 590 us
  blocking collectives  423 us (72%)
  starting transfers between devices  124 us (21%)
  between operations  13.8 us (2%)
  waiting for transfers between devices  9.84 us (2%)
  local copies, waits for them, and re-layouts  9.32 us (2%)
  matrix products  8.78 us (1%)
    all_gather x1, blocking collectives, local(): lax.all_gather(leaf_t, 'col', axis=0, tiled=True)  145 us
    all_gather x1, blocking collectives, local(): lax.all_gather(tree_y, 'col', axis=0, tiled=True)  141 us
    all_gather x1, blocking collectives, local(): lax.all_gather(tree_t, 'col', axis=0, tiled=True)  136 us
    ppermute x6, starting transfers between devices, swapped(): lax.ppermute(shard, axis, [(i, i ^ 1 << stride) for i in range(lax.axis_s...  124 us
  transfers between devices with their start and end apart: 7, of which 3 were waited for; matrix products, arithmetic and copies ran while one was open for 2% of the time, Pallas kernels for 0%

commit v1 on v0

--- a/solution.py
+++ b/solution.py
@@ -30,17 +30,41 @@
     return jnp.dot(left, right, precision=lax.Precision.HIGHEST, preferred_element_type=jnp.float32)
 
 
-def combine(top_rows, y_mine, t_mine, level):
+def doubling_gather(shard, axis, orders):
+    n = lax.axis_size(axis)
+    bits = n.bit_length() - 1
+    me = lax.axis_index(axis)
+    width = shard.shape[1] // len(orders)
+    bufs = [shard[None, :, j * width:(j + 1) * width] for j in range(len(orders))]
+    for step in range(bits):
+        received = [
+            lax.ppermute(buf, axis, [(i, i ^ 1 << order[step]) for i in range(n)])
+            for buf, order in zip(bufs, orders)
+        ]
+        new = []
+        for buf, got, order in zip(bufs, received, orders):
+            low = (me >> order[step]) & 1 == 0
+            new.append(jnp.stack([jnp.where(low, buf, got), jnp.where(low, got, buf)], axis=0))
+        bufs = new
+    pieces = []
+    for buf, order in zip(bufs, orders):
+        held = list(reversed(order))
+        buf = buf.reshape((2,) * bits + (shard.shape[0], width))
+        buf = jnp.transpose(buf, [held.index(b) for b in range(bits - 1, -1, -1)] + [bits, bits + 1])
+        pieces.append(buf.reshape(n, shard.shape[0], width))
+    return jnp.concatenate(pieces, axis=2)
+
+
+def combine(top_rows, refl_mine, level):
     lower_side = lax.axis_index("row") // 2**level % 2 == 0
-    outgoing_refl = jnp.where(lower_side, y_mine, t_mine)
     half = top_rows.shape[1] // 2
     first = top_rows[:, :half]
     second = top_rows[:, half:]
     kept = jnp.where(lower_side, first, second)
     outgoing = jnp.where(lower_side, second, first)
-    incoming, partner_refl = swapped((outgoing, outgoing_refl), "row", level)
-    refl_y = jnp.where(lower_side, y_mine, partner_refl)
-    refl_t = jnp.triu(jnp.where(lower_side, partner_refl, t_mine))
+    incoming, partner_refl = swapped((outgoing, refl_mine), "row", level)
+    refl_y = jnp.where(lower_side, refl_mine, partner_refl)
+    refl_t = jnp.triu(jnp.where(lower_side, partner_refl, refl_mine))
     lower_top = jnp.where(lower_side, kept, incoming)
     upper_top = jnp.where(lower_side, incoming, kept)
     coeffs = inner(refl_t, lower_top + inner(refl_y, upper_top))
@@ -58,24 +82,28 @@
 
 def local(trailing, leaf_v, leaf_t, tree_y, tree_t):
     width = leaf_v.shape[1]
-    v_rows, t_leaf, y_tree, t_tree = (
-        lax.all_gather(leaf_v, "col", axis=0, tiled=True),
-        lax.all_gather(leaf_t, "col", axis=0, tiled=True),
-        lax.all_gather(tree_y, "col", axis=0, tiled=True),
-        lax.all_gather(tree_t, "col", axis=0, tiled=True),
-    )
+    n_col = lax.axis_size("col")
+    col = lax.axis_index("col")
+    row = lax.axis_index("row")
+    tree_depth = tree_y.shape[0] * n_col // width
+    shard_level = col * tree_y.shape[0] // width
+    tree_mine = jnp.where((row >> shard_level) & 1 == 0, tree_y, tree_t)
+    packed = jnp.concatenate([leaf_v, leaf_t, tree_mine], axis=0)
+    bits = n_col.bit_length() - 1
+    high = list(range(bits - 3, -1, -1))
+    orders = (high + [bits - 1, bits - 2], high[:3] + [bits - 1, bits - 2] + high[3:])
+    gathered = doubling_gather(packed, "col", orders)
+    nv, nt = leaf_v.shape[0], leaf_t.shape[0]
+    v_rows = gathered[:, :nv].reshape(-1, width)
+    t_leaf = gathered[:, nv:nv + nt].reshape(-1, width)
+    tree_rows = gathered[:, nv + nt:].reshape(-1, width)
     v_rows = unit_lower(v_rows)
     coeffs = inner(jnp.triu(t_leaf), inner(v_rows, trailing))
     updated = trailing - matmul(v_rows, coeffs)
     top_rows = updated[:width]
     rest_rows = updated[width:]
-    tree_depth = y_tree.shape[0] // width
     for level in range(tree_depth):
-        low = level * width
-        high = (level + 1) * width
-        y_mine = y_tree[low:high]
-        t_mine = t_tree[low:high]
-        top_rows = combine(top_rows, y_mine, t_mine, level)
+        top_rows = combine(top_rows, tree_rows[level * width:(level + 1) * width], level)
     return jnp.concatenate([top_rows, rest_rows], axis=0)
 
 

time: 591 us -> 176 us (0.30)
  blocking collectives: 423 us -> 0 us
  waiting for transfers between devices: 9.84 us -> 34.5 us
  starting transfers between devices: 124 us -> 101 us
  between operations: 13.8 us -> 0.78 us
  other arithmetic: 1.02 us -> 11.4 us
  local copies, waits for them, and re-layouts: 9.32 us -> 17 us
    all_gather x3 -> x0, blocking collectives: 423 us -> none  [the longest x1 145 us: local(): lax.all_gather(leaf_t, 'col', axis=0, tiled=True)]
    ppermute x6, starting transfers between devices: 124 us -> 21.6 us  [swapped(): lax.ppermute(shard, axis, [(i, i ^ 1 << stride) for i in range(lax.axis_s...]
    ppermute x0 -> x14, starting transfers between devices: none -> 79.4 us  [doubling_gather(): lax.ppermute(buf, axis, [(i, i ^ 1 << order[step]) for i in range(n)])]
    ppermute x0 -> x14, waiting for transfers between devices: none -> 24.1 us  [doubling_gather(): lax.ppermute(buf, axis, [(i, i ^ 1 << order[step]) for i in range(n)])]
    another operation x0 -> x31, other arithmetic: none -> 6.98 us  [doubling_gather(): jnp.stack([jnp.where(low, buf, got), jnp.where(low, got, buf)], axis=0)]
  transfers between devices with their start and end apart: 7 -> 20, of which waited for: 3 -> 11; matrix products, arithmetic and copies ran while one was open for 2% -> 14% of each run, Pallas kernels for 0% -> 0%
where the time goes in v1:
time: 176 us; the launch traced here: 173 us
  starting transfers between devices  101 us (57%)
  waiting for transfers between devices  34.5 us (20%)
  local copies, waits for them, and re-layouts  17 us (10%)
  other arithmetic  11.4 us (6%)
  matrix products  8.77 us (5%)
    ppermute x14, starting transfers between devices, doubling_gather(): lax.ppermute(buf, axis, [(i, i ^ 1 << order[step]) for i in range(n)])  79.4 us
    ppermute x14, waiting for transfers between devices, doubling_gather(): lax.ppermute(buf, axis, [(i, i ^ 1 << order[step]) for i in range(n)])  24.1 us
    ppermute x6, starting transfers between devices, swapped(): lax.ppermute(shard, axis, [(i, i ^ 1 << stride) for i in range(lax.axis_s...  21.6 us
    ppermute x6, waiting for transfers between devices, swapped(): lax.ppermute(shard, axis, [(i, i ^ 1 << stride) for i in range(lax.axis_s...  10.4 us
    another operation x31, other arithmetic, doubling_gather(): jnp.stack([jnp.where(low, buf, got), jnp.where(low, got, buf)], axis=0)  6.98 us
    dot_general x6, matrix products, inner(): lax.dot_general(left, right, (((0,), (0,)), ((), ())), precision=lax.Prec...  5.55 us
    reshape x2, local copies, waits for them, and re-layouts, local(): t_leaf = gathered[:, nv:nv + nt].reshape(-1, width)  3.61 us
  transfers between devices with their start and end apart: 20, of which 11 were waited for; matrix products, arithmetic and copies ran while one was open for 14% of the time, Pallas kernels for 0%

profile of v1, /device:TPU:1, one launch (start us, length us, event | category | flops | bytes accessed | tf_op | source)
XLA Modules:
  0.0 173.4 jit_solution(3873506219901837710)
XLA Ops:
  0.0 0.7 broadcast_select_fusion.20
  0.7 0.7 pad_maximum_fusion.12
  1.5 29.5 %collective-permute-start.7 = (f32[1,18,128]{2,0,1:T(1,128)S(1)}, f32[1,18,128]{2,0,1:T(1,128)S(1)}, u32[]{:S(2)}, u32[]{:S(2)}) collective-permute-start(f32[1,18,128]{2,0,1:T(1,128)S(1)} %broadcast_in_dim.22), channel_id=1, source_target_pairs={{0,16},{1,17},{2,18},{3,19},{4,20},{5,21},{6,22},{7,23},{8,24},{9,... | collective-permute-start | bytes 27656 | tf_op jit(solution)/shard_map/ppermute | solution.py:41
  31.0 1.9 %collective-permute-start = (f32[1,18,128]{2,0,1:T(1,128)S(1)}, f32[1,18,128]{2,0,1:T(1,128)S(1)}, u32[]{:S(2)}, u32[]{:S(2)}) collective-permute-start(f32[1,18,128]{2,0,1:T(1,128)S(1)} %broadcast_in_dim.21), channel_id=1, source_target_pairs={{0,16},{1,17},{2,18},{3,19},{4,20},{5,21},{6,22},{7,23},{8,24},{9,... | collective-permute-start | bytes 27656 | tf_op jit(solution)/shard_map/ppermute | solution.py:41
  33.0 8.4 %collective-permute-start.8 = (f32[2,1,18,128]{3,0,2,1:T(2,128)S(1)}, f32[2,1,18,128]{3,0,2,1:T(2,128)S(1)}, u32[]{:S(2)}, u32[]{:S(2)}) collective-permute-start(f32[2,1,18,128]{3,0,2,1:T(2,128)S(1)} %pad_maximum_fusion.14), channel_id=1, source_target_pairs={{0,8},{1,9},{2,10},{3,11},{4,12},{5,13},{6,14},{7,15},{8,0},{9,1},... | collective-permute-start | bytes 55304 | tf_op jit(solution)/shard_map/ppermute | solution.py:41
  41.5 12.3 %collective-permute-done = f32[1,18,128]{2,0,1:T(1,128)S(1)} collective-permute-done((f32[1,18,128]{2,0,1:T(1,128)S(1)}, f32[1,18,128]{2,0,1:T(1,128)S(1)}, u32[]{:S(2)}, u32[]{:S(2)}) %collective-permute-start) | collective-permute-done | bytes 9248 | tf_op jit(solution)/shard_map/ppermute | solution.py:41
  53.9 5.8 %collective-permute-start.1 = (f32[2,1,18,128]{3,0,2,1:T(2,128)S(1)}, f32[2,1,18,128]{3,0,2,1:T(2,128)S(1)}, u32[]{:S(2)}, u32[]{:S(2)}) collective-permute-start(f32[2,1,18,128]{3,0,2,1:T(2,128)S(1)} %pad_maximum_fusion.13), channel_id=1, source_target_pairs={{0,8},{1,9},{2,10},{3,11},{4,12},{5,13},{6,14},{7,15},{8,0},{9,1},... | collective-permute-start | bytes 55304 | tf_op jit(solution)/shard_map/ppermute | solution.py:41
  59.7 4.0 %collective-permute-start.9 = (f32[2,2,1,18,128]{4,1,3,0,2:T(2,128)S(1)}, f32[2,2,1,18,128]{4,1,3,0,2:T(2,128)S(1)}, u32[]{:S(2)}, u32[]{:S(2)}) collective-permute-start(f32[2,2,1,18,128]{4,1,3,0,2:T(2,128)S(1)} %pad_maximum_fusion.11), channel_id=1, source_target_pairs={{0,4},{1,5},{2,6},{3,7},{4,0},{5,1},{6,2},{7,3},{8,12},{9,13},{10,... | collective-permute-start | bytes 110600 | tf_op jit(solution)/shard_map/ppermute | solution.py:41
  63.7 3.4 %collective-permute-done.1 = f32[2,1,18,128]{3,0,2,1:T(2,128)S(1)} collective-permute-done((f32[2,1,18,128]{3,0,2,1:T(2,128)S(1)}, f32[2,1,18,128]{3,0,2,1:T(2,128)S(1)}, u32[]{:S(2)}, u32[]{:S(2)}) %collective-permute-start.1) | collective-permute-done | bytes 18464 | tf_op jit(solution)/shard_map/ppermute | solution.py:41
  67.1 4.0 %collective-permute-start.2 = (f32[2,2,1,18,128]{4,1,3,0,2:T(2,128)S(1)}, f32[2,2,1,18,128]{4,1,3,0,2:T(2,128)S(1)}, u32[]{:S(2)}, u32[]{:S(2)}) collective-permute-start(f32[2,2,1,18,128]{4,1,3,0,2:T(2,128)S(1)} %pad_maximum_fusion.10), channel_id=1, source_target_pairs={{0,4},{1,5},{2,6},{3,7},{4,0},{5,1},{6,2},{7,3},{8,12},{9,13},{10,... | collective-permute-start | bytes 110600 | tf_op jit(solution)/shard_map/ppermute | solution.py:41
  71.2 4.7 %collective-permute-start.10 = (f32[2,2,2,1,18,128]{5,2,4,1,0,3:T(2,128)S(1)}, f32[2,2,2,1,18,128]{5,2,4,1,0,3:T(2,128)S(1)}, u32[]{:S(2)}, u32[]{:S(2)}) collective-permute-start(f32[2,2,2,1,18,128]{5,2,4,1,0,3:T(2,128)S(1)} %fusion.35), channel_id=1, source_target_pairs={{0,64},{1,65},{2,66},{3,67},{4,68},{5,69},{6,70},{7,71},{8,72},{9,... | collective-permute-start | bytes 221192 | tf_op jit(solution)/shard_map/ppermute | solution.py:41
  75.9 3.2 %collective-permute-start.3 = (f32[2,2,2,1,18,128]{5,2,4,1,0,3:T(2,128)S(1)}, f32[2,2,2,1,18,128]{5,2,4,1,0,3:T(2,128)S(1)}, u32[]{:S(2)}, u32[]{:S(2)}) collective-permute-start(f32[2,2,2,1,18,128]{5,2,4,1,0,3:T(2,128)S(1)} %pad_maximum_fusion.8), channel_id=1, source_target_pairs={{0,2},{1,3},{2,0},{3,1},{4,6},{5,7},{6,4},{7,5},{8,10},{9,11},{10,... | collective-permute-start | bytes 221192 | tf_op jit(solution)/shard_map/ppermute | solution.py:41
  79.3 2.9 %collective-permute-start.11 = (f32[2,2,2,2,1,18,128]{6,3,5,2,1,0,4:T(2,128)S(1)}, f32[2,2,2,2,1,18,128]{6,3,5,2,1,0,4:T(2,128)S(1)}, u32[]{:S(2)}, u32[]{:S(2)}) collective-permute-start(f32[2,2,2,2,1,18,128]{6,3,5,2,1,0,4:T(2,128)S(1)} %fusion.34), channel_id=1, source_target_pairs={{0,32},{1,33},{2,34},{3,35},{4,36},{5,37},{6,38},{7,39},{8,40},{9,... | collective-permute-start | bytes 442376 | tf_op jit(solution)/shard_map/ppermute | solution.py:41
  82.3 0.5 collective-permute-done.3
  82.9 2.2 %collective-permute-start.4 = (f32[2,2,2,2,1,18,128]{6,3,5,2,1,0,4:T(2,128)S(1)}, f32[2,2,2,2,1,18,128]{6,3,5,2,1,0,4:T(2,128)S(1)}, u32[]{:S(2)}, u32[]{:S(2)}) collective-permute-start(f32[2,2,2,2,1,18,128]{6,3,5,2,1,0,4:T(2,128)S(1)} %pad_maximum_fusion.6), channel_id=1, source_target_pairs={{0,1},{1,0},{2,3},{3,2},{4,5},{5,4},{6,7},{7,6},{8,9},{9,8},{10,11... | collective-permute-start | bytes 442376 | tf_op jit(solution)/shard_map/ppermute | solution.py:41
  85.6 3.5 %collective-permute-start.12 = (f32[2,2,2,2,2,1,18,128]{7,4,6,3,2,1,0,5:T(2,128)S(1)}, f32[2,2,2,2,2,1,18,128]{7,4,6,3,2,1,0,5:T(2,128)S(1)}, u32[]{:S(2)}, u32[]{:S(2)}) collective-permute-start(f32[2,2,2,2,2,1,18,128]{7,4,6,3,2,1,0,5:T(2,128)S(1)} %fusion.30), channel_id=1, source_target_pairs={{0,2},{1,3},{2,0},{3,1},{4,6},{5,7},{6,4},{7,5},{8,10},{9,11},{10,... | collective-permute-start | bytes 884744 | tf_op jit(solution)/shard_map/ppermute | solution.py:41
  89.0 0.3 collective-permute-done.4
  89.6 4.7 %collective-permute-start.5 = (f32[2,2,2,2,2,1,18,128]{7,4,6,3,2,1,0,5:T(2,128)S(1)}, f32[2,2,2,2,2,1,18,128]{7,4,6,3,2,1,0,5:T(2,128)}, u32[]{:S(2)}, u32[]{:S(2)}) collective-permute-start(f32[2,2,2,2,2,1,18,128]{7,4,6,3,2,1,0,5:T(2,128)S(1)} %pad_maximum_fusion.3), channel_id=1, source_target_pairs={{0,64},{1,65},{2,66},{3,67},{4,68},{5,69},{6,70},{7,71},{8,72},{9,... | collective-permute-start | bytes 884744 | tf_op jit(solution)/shard_map/ppermute | solution.py:41
  94.3 3.3 %collective-permute-done.12 = f32[2,2,2,2,2,1,18,128]{7,4,6,3,2,1,0,5:T(2,128)S(1)} collective-permute-done((f32[2,2,2,2,2,1,18,128]{7,4,6,3,2,1,0,5:T(2,128)S(1)}, f32[2,2,2,2,2,1,18,128]{7,4,6,3,2,1,0,5:T(2,128)S(1)}, u32[]{:S(2)}, u32[]{:S(2)}) %collective-permute-start.12) | collective-permute-done | bytes 294944 | tf_op jit(solution)/shard_map/ppermute | solution.py:41
  97.8 0.2 fusion.10
  98.0 0.3 fusion.47
  98.3 1.9 %collective-permute-start.13 = (f32[2,2,2,2,2,2,1,18,128]{8,5,7,6,4,3,2,1,0:T(2,128)S(1)}, f32[2,2,2,2,2,2,1,18,128]{8,5,7,6,4,3,2,1,0:T(2,128)}, u32[]{:S(2)}, u32[]{:S(2)}) collective-permute-start(f32[2,2,2,2,2,2,1,18,128]{8,5,7,6,4,3,2,1,0:T(2,128)S(1)} %fusion.47), channel_id=1, source_target_pairs={{0,1},{1,0},{2,3},{3,2},{4,5},{5,4},{6,7},{7,6},{8,9},{9,8},{10,11... | collective-permute-start | bytes 1769480 | tf_op jit(solution)/shard_map/ppermute | solution.py:41
  100.2 1.6 copy.139
  101.8 1.2 select_bitcast_fusion.2
  103.0 0.3 pad_maximum_fusion.1
  103.3 2.8 %collective-permute-start.6 = (f32[2,2,2,2,2,2,1,18,128]{8,5,7,6,4,3,2,1,0:T(2,128)S(1)}, f32[2,2,2,2,2,2,1,18,128]{8,5,7,6,4,3,2,1,0:T(2,128)S(1)}, u32[]{:S(2)}, u32[]{:S(2)}) collective-permute-start(f32[2,2,2,2,2,2,1,18,128]{8,5,7,6,4,3,2,1,0:T(2,128)S(1)} %pad_maximum_fusion.1), channel_id=1, source_target_pairs={{0,32},{1,33},{2,34},{3,35},{4,36},{5,37},{6,38},{7,39},{8,40},{9,... | collective-permute-start | bytes 1769480 | tf_op jit(solution)/shard_map/ppermute | solution.py:41
  106.1 4.1 %collective-permute-done.13 = f32[2,2,2,2,2,2,1,18,128]{8,5,7,6,4,3,2,1,0:T(2,128)} collective-permute-done((f32[2,2,2,2,2,2,1,18,128]{8,5,7,6,4,3,2,1,0:T(2,128)S(1)}, f32[2,2,2,2,2,2,1,18,128]{8,5,7,6,4,3,2,1,0:T(2,128)}, u32[]{:S(2)}, u32[]{:S(2)}) %collective-permute-start.13) | collective-permute-done | bytes 589856 | tf_op jit(solution)/shard_map/ppermute | solution.py:41
  110.2 1.4 fusion.8
  111.7 1.4 fusion.7
  113.1 0.6 maximum_bitcast_fusion.1
  113.7 0.9 copy.135
  114.7 0.4 fusion.9
  115.1 0.4 fusion.6
  115.5 0.6 maximum_bitcast_fusion
  116.1 0.9 copy.116
  117.0 0.7 fusion.11
  117.7 0.7 fusion.12
  118.7 0.8 slice.52
  119.5 1.1 copy.141
  120.6 9.1 %collective-permute-start.15 = (f32[256,256]{0,1:T(8,128)S(1)}, f32[256,256]{0,1:T(8,128)}, u32[]{:S(2)}, u32[]{:S(2)}) collective-permute-start(f32[256,256]{0,1:T(8,128)S(1)} %copy.141), channel_id=1, source_target_pairs={{0,128},{128,0},{256,384},{384,256},{512,640},{640,512},{768,896},... | collective-permute-start | bytes 786440 | tf_op jit(solution)/shard_map/ppermute | solution.py:8
  129.7 1.9 %copy.137 = f32[128,2,256]{2,1,0:T(2,128)} copy(f32[128,2,256]{2,0,1:T(8,128)} %fusion.12) | data formatting | bytes 524288 | tf_op jit(solution)/shard_map/slice | solution.py:98
  131.6 1.8 %reshape.26 = f32[256,256]{1,0:T(8,128)} reshape(f32[128,2,256]{2,1,0:T(2,128)} %copy.137) | data formatting | bytes 524288 | tf_op jit(solution)/shard_map/reshape | solution.py:98
  133.4 1.8 %copy.138 = f32[256,256]{0,1:T(8,128)} copy(f32[256,256]{1,0:T(8,128)} %reshape.26) | data formatting | bytes 524288 | tf_op jit(solution)/shard_map/reshape | solution.py:98
  135.2 2.3 %copy.136 = f32[128,12,256]{2,1,0:T(8,128)} copy(f32[128,12,256]{2,0,1:T(8,128)S(1)} %fusion) | data formatting | bytes 3145728 | tf_op jit(solution)/shard_map/slice | solution.py:97
  137.5 1.6 reshape.25
  139.1 2.5 %fusion.1 = f32[256,256]{1,0:T(8,128)S(1)} fusion(f32[1536,256]{1,0:T(8,128)S(1)} %copy-done.1, f32[1536,256]{1,0:T(8,128)S(1)} %reshape.25), kind=kOutput, calls=%fused_computation.12 | convolution fusion | flops 1209532416 | bytes 3407872 | tf_op jit(solution)/shard_map/dot_general | solution.py:20
  141.7 0.4 fusion.19
  142.1 1.6 convolution_subtract_fusion
  143.8 2.1 %collective-permute-start.14 = (f32[256,128]{0,1:T(8,128)S(1)}, f32[256,128]{0,1:T(8,128)S(1)}, u32[]{:S(2)}, u32[]{:S(2)}) collective-permute-start(f32[256,128]{0,1:T(8,128)S(1)} %get-tuple-element.8), channel_id=1, source_target_pairs={{0,128},{128,0},{256,384},{384,256},{512,640},{640,512},{768,896},... | collective-permute-start | bytes 393224 | tf_op jit(solution)/shard_map/ppermute | solution.py:8
  145.9 1.3 collective-permute-done.14
  147.2 1.4 convolution_add_fusion.1
  148.5 0.4 fusion.16
  149.0 1.3 broadcast_select_fusion.7
  150.3 1.9 %collective-permute-start.16 = (f32[256,128]{0,1:T(8,128)S(1)}, f32[256,128]{0,1:T(8,128)S(1)}, u32[]{:S(2)}, u32[]{:S(2)}) collective-permute-start(f32[256,128]{0,1:T(8,128)S(1)} %get-tuple-element.14), channel_id=1, source_target_pairs={{0,128},{128,0},{256,384},{384,256},{512,640},{640,512},{768,896},... | collective-permute-start | bytes 393224 | tf_op jit(solution)/shard_map/ppermute | solution.py:8
  152.6 3.2 %collective-permute-start.18 = (f32[256,256]{0,1:T(8,128)S(1)}, f32[256,256]{0,1:T(8,128)S(1)}, u32[]{:S(2)}, u32[]{:S(2)}) collective-permute-start(f32[256,256]{0,1:T(8,128)S(1)} %copy.146), channel_id=1, source_target_pairs={{0,256},{128,384},{256,0},{384,128},{512,768},{640,896},{768,512},... | collective-permute-start | bytes 786440 | tf_op jit(solution)/shard_map/ppermute | solution.py:8
  155.9 2.1 %collective-permute-start.17 = (f32[256,128]{0,1:T(8,128)S(1)}, f32[256,128]{0,1:T(8,128)S(1)}, u32[]{:S(2)}, u32[]{:S(2)}) collective-permute-start(f32[256,128]{0,1:T(8,128)S(1)} %get-tuple-element.18), channel_id=1, source_target_pairs={{0,256},{128,384},{256,0},{384,128},{512,768},{640,896},{768,512},... | collective-permute-start | bytes 393224 | tf_op jit(solution)/shard_map/ppermute | solution.py:8
  158.0 3.9 %collective-permute-done.18 = f32[256,256]{0,1:T(8,128)S(1)} collective-permute-done((f32[256,256]{0,1:T(8,128)S(1)}, f32[256,256]{0,1:T(8,128)S(1)}, u32[]{:S(2)}, u32[]{:S(2)}) %collective-permute-start.18) | collective-permute-done | bytes 262176 | tf_op jit(solution)/shard_map/ppermute | solution.py:8
  161.9 2.8 %collective-permute-done.17 = f32[256,128]{0,1:T(8,128)S(1)} collective-permute-done((f32[256,128]{0,1:T(8,128)S(1)}, f32[256,128]{0,1:T(8,128)S(1)}, u32[]{:S(2)}, u32[]{:S(2)}) %collective-permute-start.17) | collective-permute-done | bytes 131104 | tf_op jit(solution)/shard_map/ppermute | solution.py:8
  164.7 0.4 convolution_add_fusion
  165.1 0.4 fusion.13
  165.6 0.3 broadcast_select_fusion.11
  165.9 3.2 %collective-permute-start.19 = (f32[256,128]{0,1:T(8,128)S(1)}, f32[256,128]{0,1:T(8,128)S(1)}, u32[]{:S(2)}, u32[]{:S(2)}) collective-permute-start(f32[256,128]{0,1:T(8,128)S(1)} %get-tuple-element.12), channel_id=1, source_target_pairs={{0,256},{128,384},{256,0},{384,128},{512,768},{640,896},{768,512},... | collective-permute-start | bytes 393224 | tf_op jit(solution)/shard_map/ppermute | solution.py:8
  169.2 2.4 %collective-permute-done.19 = f32[256,128]{0,1:T(8,128)S(1)} collective-permute-done((f32[256,128]{0,1:T(8,128)S(1)}, f32[256,128]{0,1:T(8,128)S(1)}, u32[]{:S(2)}, u32[]{:S(2)}) %collective-permute-start.19) | collective-permute-done | bytes 131104 | tf_op jit(solution)/shard_map/ppermute | solution.py:8
  171.8 1.6 copy.150
  (56 shorter events, 2.6 us)
Async XLA Ops:
  1.5 31.5 %collective-permute-start.7 = (f32[1,18,128]{2,0,1:T(1,128)S(1)}, f32[1,18,128]{2,0,1:T(1,128)S(1)}, u32[]{:S(2)}, u32[]{:S(2)}) collective-permute-start(f32[1,18,128]{2,0,1:T(1,128)S(1)} %broadcast_in_dim.22), channel_id=1, source_target_pairs={{0,16},{1,17},{2,18},{3,19},{4,20},{5,21},{6,22},{7,23},{8,24},{9,... | collective-permute-start | bytes 27656 | tf_op jit(solution)/shard_map/ppermute | solution.py:41
  31.0 22.8 %collective-permute-start = (f32[1,18,128]{2,0,1:T(1,128)S(1)}, f32[1,18,128]{2,0,1:T(1,128)S(1)}, u32[]{:S(2)}, u32[]{:S(2)}) collective-permute-start(f32[1,18,128]{2,0,1:T(1,128)S(1)} %broadcast_in_dim.21), channel_id=1, source_target_pairs={{0,16},{1,17},{2,18},{3,19},{4,20},{5,21},{6,22},{7,23},{8,24},{9,... | collective-permute-start | bytes 27656 | tf_op jit(solution)/shard_map/ppermute | solution.py:41
  33.0 26.6 %collective-permute-start.8 = (f32[2,1,18,128]{3,0,2,1:T(2,128)S(1)}, f32[2,1,18,128]{3,0,2,1:T(2,128)S(1)}, u32[]{:S(2)}, u32[]{:S(2)}) collective-permute-start(f32[2,1,18,128]{3,0,2,1:T(2,128)S(1)} %pad_maximum_fusion.14), channel_id=1, source_target_pairs={{0,8},{1,9},{2,10},{3,11},{4,12},{5,13},{6,14},{7,15},{8,0},{9,1},... | collective-permute-start | bytes 55304 | tf_op jit(solution)/shard_map/ppermute | solution.py:41
  53.9 13.2 %collective-permute-start.1 = (f32[2,1,18,128]{3,0,2,1:T(2,128)S(1)}, f32[2,1,18,128]{3,0,2,1:T(2,128)S(1)}, u32[]{:S(2)}, u32[]{:S(2)}) collective-permute-start(f32[2,1,18,128]{3,0,2,1:T(2,128)S(1)} %pad_maximum_fusion.13), channel_id=1, source_target_pairs={{0,8},{1,9},{2,10},{3,11},{4,12},{5,13},{6,14},{7,15},{8,0},{9,1},... | collective-permute-start | bytes 55304 | tf_op jit(solution)/shard_map/ppermute | solution.py:41
  59.7 11.4 %collective-permute-start.9 = (f32[2,2,1,18,128]{4,1,3,0,2:T(2,128)S(1)}, f32[2,2,1,18,128]{4,1,3,0,2:T(2,128)S(1)}, u32[]{:S(2)}, u32[]{:S(2)}) collective-permute-start(f32[2,2,1,18,128]{4,1,3,0,2:T(2,128)S(1)} %pad_maximum_fusion.11), channel_id=1, source_target_pairs={{0,4},{1,5},{2,6},{3,7},{4,0},{5,1},{6,2},{7,3},{8,12},{9,13},{10,... | collective-permute-start | bytes 110600 | tf_op jit(solution)/shard_map/ppermute | solution.py:41
  67.1 8.7 %collective-permute-start.2 = (f32[2,2,1,18,128]{4,1,3,0,2:T(2,128)S(1)}, f32[2,2,1,18,128]{4,1,3,0,2:T(2,128)S(1)}, u32[]{:S(2)}, u32[]{:S(2)}) collective-permute-start(f32[2,2,1,18,128]{4,1,3,0,2:T(2,128)S(1)} %pad_maximum_fusion.10), channel_id=1, source_target_pairs={{0,4},{1,5},{2,6},{3,7},{4,0},{5,1},{6,2},{7,3},{8,12},{9,13},{10,... | collective-permute-start | bytes 110600 | tf_op jit(solution)/shard_map/ppermute | solution.py:41
  71.2 7.9 %collective-permute-start.10 = (f32[2,2,2,1,18,128]{5,2,4,1,0,3:T(2,128)S(1)}, f32[2,2,2,1,18,128]{5,2,4,1,0,3:T(2,128)S(1)}, u32[]{:S(2)}, u32[]{:S(2)}) collective-permute-start(f32[2,2,2,1,18,128]{5,2,4,1,0,3:T(2,128)S(1)} %fusion.35), channel_id=1, source_target_pairs={{0,64},{1,65},{2,66},{3,67},{4,68},{5,69},{6,70},{7,71},{8,72},{9,... | collective-permute-start | bytes 221192 | tf_op jit(solution)/shard_map/ppermute | solution.py:41
  75.9 6.8 %collective-permute-start.3 = (f32[2,2,2,1,18,128]{5,2,4,1,0,3:T(2,128)S(1)}, f32[2,2,2,1,18,128]{5,2,4,1,0,3:T(2,128)S(1)}, u32[]{:S(2)}, u32[]{:S(2)}) collective-permute-start(f32[2,2,2,1,18,128]{5,2,4,1,0,3:T(2,128)S(1)} %pad_maximum_fusion.8), channel_id=1, source_target_pairs={{0,2},{1,3},{2,0},{3,1},{4,6},{5,7},{6,4},{7,5},{8,10},{9,11},{10,... | collective-permute-start | bytes 221192 | tf_op jit(solution)/shard_map/ppermute | solution.py:41
  79.3 5.9 %collective-permute-start.11 = (f32[2,2,2,2,1,18,128]{6,3,5,2,1,0,4:T(2,128)S(1)}, f32[2,2,2,2,1,18,128]{6,3,5,2,1,0,4:T(2,128)S(1)}, u32[]{:S(2)}, u32[]{:S(2)}) collective-permute-start(f32[2,2,2,2,1,18,128]{6,3,5,2,1,0,4:T(2,128)S(1)} %fusion.34), channel_id=1, source_target_pairs={{0,32},{1,33},{2,34},{3,35},{4,36},{5,37},{6,38},{7,39},{8,40},{9,... | collective-permute-start | bytes 442376 | tf_op jit(solution)/shard_map/ppermute | solution.py:41
  82.9 6.4 %collective-permute-start.4 = (f32[2,2,2,2,1,18,128]{6,3,5,2,1,0,4:T(2,128)S(1)}, f32[2,2,2,2,1,18,128]{6,3,5,2,1,0,4:T(2,128)S(1)}, u32[]{:S(2)}, u32[]{:S(2)}) collective-permute-start(f32[2,2,2,2,1,18,128]{6,3,5,2,1,0,4:T(2,128)S(1)} %pad_maximum_fusion.6), channel_id=1, source_target_pairs={{0,1},{1,0},{2,3},{3,2},{4,5},{5,4},{6,7},{7,6},{8,9},{9,8},{10,11... | collective-permute-start | bytes 442376 | tf_op jit(solution)/shard_map/ppermute | solution.py:41
  85.6 12.0 %collective-permute-start.12 = (f32[2,2,2,2,2,1,18,128]{7,4,6,3,2,1,0,5:T(2,128)S(1)}, f32[2,2,2,2,2,1,18,128]{7,4,6,3,2,1,0,5:T(2,128)S(1)}, u32[]{:S(2)}, u32[]{:S(2)}) collective-permute-start(f32[2,2,2,2,2,1,18,128]{7,4,6,3,2,1,0,5:T(2,128)S(1)} %fusion.30), channel_id=1, source_target_pairs={{0,2},{1,3},{2,0},{3,1},{4,6},{5,7},{6,4},{7,5},{8,10},{9,11},{10,... | collective-permute-start | bytes 884744 | tf_op jit(solution)/shard_map/ppermute | solution.py:41
  89.6 10.6 %copy-start.1 = (f32[1536,256]{1,0:T(8,128)S(1)}, f32[1536,256]{1,0:T(8,128)}, u32[]{:S(2)}) copy-start(f32[1536,256]{1,0:T(8,128)} %param.5) | copy-start | bytes 4718596
  89.6 12.2 %collective-permute-start.5 = (f32[2,2,2,2,2,1,18,128]{7,4,6,3,2,1,0,5:T(2,128)S(1)}, f32[2,2,2,2,2,1,18,128]{7,4,6,3,2,1,0,5:T(2,128)}, u32[]{:S(2)}, u32[]{:S(2)}) collective-permute-start(f32[2,2,2,2,2,1,18,128]{7,4,6,3,2,1,0,5:T(2,128)S(1)} %pad_maximum_fusion.3), channel_id=1, source_target_pairs={{0,64},{1,65},{2,66},{3,67},{4,68},{5,69},{6,70},{7,71},{8,72},{9,... | collective-permute-start | bytes 884744 | tf_op jit(solution)/shard_map/ppermute | solution.py:41
  98.3 12.0 %collective-permute-start.13 = (f32[2,2,2,2,2,2,1,18,128]{8,5,7,6,4,3,2,1,0:T(2,128)S(1)}, f32[2,2,2,2,2,2,1,18,128]{8,5,7,6,4,3,2,1,0:T(2,128)}, u32[]{:S(2)}, u32[]{:S(2)}) collective-permute-start(f32[2,2,2,2,2,2,1,18,128]{8,5,7,6,4,3,2,1,0:T(2,128)S(1)} %fusion.47), channel_id=1, source_target_pairs={{0,1},{1,0},{2,3},{3,2},{4,5},{5,4},{6,7},{7,6},{8,9},{9,8},{10,11... | collective-permute-start | bytes 1769480 | tf_op jit(solution)/shard_map/ppermute | solution.py:41
  103.3 11.4 %collective-permute-start.6 = (f32[2,2,2,2,2,2,1,18,128]{8,5,7,6,4,3,2,1,0:T(2,128)S(1)}, f32[2,2,2,2,2,2,1,18,128]{8,5,7,6,4,3,2,1,0:T(2,128)S(1)}, u32[]{:S(2)}, u32[]{:S(2)}) collective-permute-start(f32[2,2,2,2,2,2,1,18,128]{8,5,7,6,4,3,2,1,0:T(2,128)S(1)} %pad_maximum_fusion.1), channel_id=1, source_target_pairs={{0,32},{1,33},{2,34},{3,35},{4,36},{5,37},{6,38},{7,39},{8,40},{9,... | collective-permute-start | bytes 1769480 | tf_op jit(solution)/shard_map/ppermute | solution.py:41
  120.6 26.6 %collective-permute-start.15 = (f32[256,256]{0,1:T(8,128)S(1)}, f32[256,256]{0,1:T(8,128)}, u32[]{:S(2)}, u32[]{:S(2)}) collective-permute-start(f32[256,256]{0,1:T(8,128)S(1)} %copy.141), channel_id=1, source_target_pairs={{0,128},{128,0},{256,384},{384,256},{512,640},{640,512},{768,896},... | collective-permute-start | bytes 786440 | tf_op jit(solution)/shard_map/ppermute | solution.py:8
  139.1 2.6 %copy-start.2 = (f32[256,256]{0,1:T(8,128)S(1)}, f32[256,256]{0,1:T(8,128)}, u32[]{:S(2)}) copy-start(f32[256,256]{0,1:T(8,128)} %copy.138) | copy-start | bytes 786436
  139.1 3.0 %copy-start = (f32[1536,256]{0,1:T(8,128)S(1)}, f32[1536,256]{0,1:T(8,128)}, u32[]{:S(2)}) copy-start(f32[1536,256]{0,1:T(8,128)} %copy.139) | copy-start | bytes 4718596
  143.8 8.4 %copy-start.3 = (f32[64,4,256]{2,0,1:T(8,128)S(1)}, f32[64,4,256]{2,0,1:T(8,128)}, u32[]{:S(2)}) copy-start(f32[64,4,256]{2,0,1:T(8,128)} %get-tuple-element.6) | copy-start | bytes 786436
  143.8 3.4 %collective-permute-start.14 = (f32[256,128]{0,1:T(8,128)S(1)}, f32[256,128]{0,1:T(8,128)S(1)}, u32[]{:S(2)}, u32[]{:S(2)}) collective-permute-start(f32[256,128]{0,1:T(8,128)S(1)} %get-tuple-element.8), channel_id=1, source_target_pairs={{0,128},{128,0},{256,384},{384,256},{512,640},{640,512},{768,896},... | collective-permute-start | bytes 393224 | tf_op jit(solution)/shard_map/ppermute | solution.py:8
  150.3 5.6 %collective-permute-start.16 = (f32[256,128]{0,1:T(8,128)S(1)}, f32[256,128]{0,1:T(8,128)S(1)}, u32[]{:S(2)}, u32[]{:S(2)}) collective-permute-start(f32[256,128]{0,1:T(8,128)S(1)} %get-tuple-element.14), channel_id=1, source_target_pairs={{0,128},{128,0},{256,384},{384,256},{512,640},{640,512},{768,896},... | collective-permute-start | bytes 393224 | tf_op jit(solution)/shard_map/ppermute | solution.py:8
  152.6 9.3 %collective-permute-start.18 = (f32[256,256]{0,1:T(8,128)S(1)}, f32[256,256]{0,1:T(8,128)S(1)}, u32[]{:S(2)}, u32[]{:S(2)}) collective-permute-start(f32[256,256]{0,1:T(8,128)S(1)} %copy.146), channel_id=1, source_target_pairs={{0,256},{128,384},{256,0},{384,128},{512,768},{640,896},{768,512},... | collective-permute-start | bytes 786440 | tf_op jit(solution)/shard_map/ppermute | solution.py:8
  155.9 8.8 %collective-permute-start.17 = (f32[256,128]{0,1:T(8,128)S(1)}, f32[256,128]{0,1:T(8,128)S(1)}, u32[]{:S(2)}, u32[]{:S(2)}) collective-permute-start(f32[256,128]{0,1:T(8,128)S(1)} %get-tuple-element.18), channel_id=1, source_target_pairs={{0,256},{128,384},{256,0},{384,128},{512,768},{640,896},{768,512},... | collective-permute-start | bytes 393224 | tf_op jit(solution)/shard_map/ppermute | solution.py:8
  165.9 5.7 %collective-permute-start.19 = (f32[256,128]{0,1:T(8,128)S(1)}, f32[256,128]{0,1:T(8,128)S(1)}, u32[]{:S(2)}, u32[]{:S(2)}) collective-permute-start(f32[256,128]{0,1:T(8,128)S(1)} %get-tuple-element.12), channel_id=1, source_target_pairs={{0,256},{128,384},{256,0},{384,128},{512,768},{640,896},{768,512},... | collective-permute-start | bytes 393224 | tf_op jit(solution)/shard_map/ppermute | solution.py:8

commit v2 on v1

v2 whole, which is shorter than its diff:
```python
import jax
import jax.numpy as jnp
from jax import lax
from jax.sharding import PartitionSpec as P


def swapped(shard, axis, stride):
    return lax.ppermute(shard, axis, [(i, i ^ 1 << stride) for i in range(lax.axis_size(axis))])


def unit_lower(piece):
    rows = lax.broadcasted_iota(jnp.int32, piece.shape, 0)
    cols = lax.broadcasted_iota(jnp.int32, piece.shape, 1)
    return jnp.where(
        rows < cols, jnp.float32(0.0), jnp.where(rows == cols, jnp.float32(1.0), piece)
    )


def inner(left, right):
    return lax.dot_general(
        left,
        right,
        (((0,), (0,)), ((), ())),
        precision=lax.Precision.HIGHEST,
        preferred_element_type=jnp.float32,
    )


def matmul(left, right):
    return jnp.dot(left, right, precision=lax.Precision.HIGHEST, preferred_element_type=jnp.float32)


def doubling_gather(shard, axis, orders):
    n = lax.axis_size(axis)
    bits = n.bit_length() - 1
    me = lax.axis_index(axis)
    width = shard.shape[1] // len(orders)
    bufs = [shard[:, j * width:(j + 1) * width] for j in range(len(orders))]
    held = [[] for _ in orders]
    for step in range(bits):
        received = [
            lax.ppermute(buf, axis, [(i, i ^ 1 << order[step]) for i in range(n)])
            for buf, order in zip(bufs, orders)
        ]
        for j, (got, order) in enumerate(zip(received, orders)):
            bit = order[step]
            low = (me >> bit) & 1 == 0
            pos = sum(1 for b in held[j] if b > bit)
            bufs[j] = jnp.stack([jnp.where(low, bufs[j], got), jnp.where(low, got, bufs[j])], axis=pos)
            held[j].insert(pos, bit)
    return [buf.reshape((n,) + shard.shape[:1] + (width,)) for buf in bufs]


def combine(top_rows, refl_mine, level):
    lower_side = lax.axis_index("row") // 2**level % 2 == 0
    width = top_rows.shape[0]
    incoming = swapped(jnp.concatenate([top_rows, refl_mine], axis=0), "row", level)
    partner_top, partner_refl = incoming[:width], incoming[width:]
    refl_y = jnp.where(lower_side, refl_mine, partner_refl)
    refl_t = jnp.triu(jnp.where(lower_side, partner_refl, refl_mine))
    lower_top = jnp.where(lower_side, top_rows, partner_top)
    upper_top = jnp.where(lower_side, partner_top, top_rows)
    coeffs = inner(refl_t, lower_top + inner(refl_y, upper_top))
    return jnp.where(lower_side, lower_top - coeffs, upper_top - matmul(refl_y, coeffs))


def local(trailing, leaf_v, leaf_t, tree_y, tree_t):
    width = leaf_v.shape[1]
    n_col = lax.axis_size("col")
    col = lax.axis_index("col")
    row = lax.axis_index("row")
    tree_depth = tree_y.shape[0] * n_col // width
    shard_level = col * tree_y.shape[0] // width
    tree_mine = jnp.where((row >> shard_level) & 1 == 0, tree_y, tree_t)
    packed = jnp.concatenate([leaf_v, leaf_t, tree_mine], axis=0)
    bits = n_col.bit_length() - 1
    high = list(range(bits - 3, -1, -1))
    orders = (high + [bits - 1, bits - 2], high[:3] + [bits - 1, bits - 2] + high[3:])
    pieces = doubling_gather(packed, "col", orders)
    nv, nt = leaf_v.shape[0], leaf_t.shape[0]

    def joined(lo, hi):
        return jnp.concatenate([p[:, lo:hi] for p in pieces], axis=2).reshape(-1, width)

    v_rows = unit_lower(joined(0, nv))
    t_leaf = joined(nv, nv + nt)
    tree_rows = joined(nv + nt, packed.shape[0])
    coeffs = inner(jnp.triu(t_leaf), inner(v_rows, trailing))
    updated = trailing - matmul(v_rows, coeffs)
    top_rows = updated[:width]
    for level in range(tree_depth):
        top_rows = combine(top_rows, tree_rows[level * width:(level + 1) * width], level)
    return lax.dynamic_update_slice(updated, top_rows, (0, 0))


def solution(mesh):
    in_specs = (
        P("row", "col"),
        P(("row", "col"), None),
        P(("row", "col"), None),
        P(("row", "col"), None),
        P(("row", "col"), None),
    )
    out_specs = P("row", "col")
    return jax.shard_map(local, mesh=mesh, in_specs=in_specs, out_specs=out_specs, check_vma=False)
```

time: 176 us -> 169 us (0.960)
  starting transfers between devices: 101 us -> 111 us
  local copies, waits for them, and re-layouts: 17 us -> 10 us
  waiting for transfers between devices: 34.5 us -> 28.3 us
  other arithmetic: 11.4 us -> 6.91 us
  matrix products: 8.77 us -> 10.7 us
    ppermute x14, starting transfers between devices: 79.4 us -> 99.3 us  [doubling_gather(): lax.ppermute(buf, axis, [(i, i ^ 1 << order[step]) for i in range(n)])]
    ppermute x6 -> x2, starting transfers between devices: 21.6 us -> 12.1 us  [swapped(): lax.ppermute(shard, axis, [(i, i ^ 1 << stride) for i in range(lax.axis_s...]
    ppermute x14, waiting for transfers between devices: 24.1 us -> 15.1 us  [doubling_gather(): lax.ppermute(buf, axis, [(i, i ^ 1 << order[step]) for i in range(n)])]
    slice x4 -> x8, local copies, waits for them, and re-layouts: 4.25 us -> 0.19 us  [the longest x6 0.17 us: joined(): p[:, lo:hi]]
    another operation x0 -> x8, local copies, waits for them, and re-layouts: none -> 2.78 us  [doubling_gather(): jnp.stack([jnp.where(low, bufs[j], got), jnp.where(low, got, bufs[j])], a...]
    ppermute x6 -> x2, waiting for transfers between devices: 10.4 us -> 13.2 us  [swapped(): lax.ppermute(shard, axis, [(i, i ^ 1 << stride) for i in range(lax.axis_s...]
    reshape x3 -> x2, local copies, waits for them, and re-layouts: 5.23 us -> 2.62 us  [joined(): jnp.concatenate([p[:, lo:hi] for p in pieces], axis=2).reshape(-1, width)]
    another operation x31 -> x28, other arithmetic: 6.98 us -> 4.53 us  [doubling_gather(): jnp.stack([jnp.where(low, bufs[j], got), jnp.where(low, got, bufs[j])], a...]
  transfers between devices with their start and end apart: 20 -> 16, of which waited for: 11 -> 11; matrix products, arithmetic and copies ran while one was open for 14% -> 3% of each run, Pallas kernels for 0% -> 0%
where the time goes in v2:
time: 169 us; the launch traced here: 168 us
  starting transfers between devices  111 us (66%)
  waiting for transfers between devices  28.3 us (17%)
  matrix products  10.7 us (6%)
  local copies, waits for them, and re-layouts  10 us (6%)
  other arithmetic  6.91 us (4%)
    ppermute x14, starting transfers between devices, doubling_gather(): lax.ppermute(buf, axis, [(i, i ^ 1 << order[step]) for i in range(n)])  99.3 us
    ppermute x14, waiting for transfers between devices, doubling_gather(): lax.ppermute(buf, axis, [(i, i ^ 1 << order[step]) for i in range(n)])  15.1 us
    ppermute x2, waiting for transfers between devices, swapped(): lax.ppermute(shard, axis, [(i, i ^ 1 << stride) for i in range(lax.axis_s...  13.2 us
    ppermute x2, starting transfers between devices, swapped(): lax.ppermute(shard, axis, [(i, i ^ 1 << stride) for i in range(lax.axis_s...  12.1 us
    dot_general x6, matrix products, inner(): lax.dot_general(left, right, (((0,), (0,)), ((), ())), precision=lax.Prec...  6.78 us
    another operation x28, other arithmetic, doubling_gather(): jnp.stack([jnp.where(low, bufs[j], got), jnp.where(low, got, bufs[j])], a...  4.53 us
    dot_general x3, matrix products, matmul(): jnp.dot(left, right, precision=lax.Precision.HIGHEST, preferred_element_t...  3.9 us
  transfers between devices with their start and end apart: 16, of which 11 were waited for; matrix products, arithmetic and copies ran while one was open for 3% of the time, Pallas kernels for 0%

profile of v2, /device:TPU:1, one launch (start us, length us, event | category | flops | bytes accessed | tf_op | source)
XLA Modules:
  0.0 168.1 jit_solution(8454397855550205983)
XLA Ops:
  0.0 0.7 broadcast_select_fusion.1
  0.7 0.7 pad_maximum_fusion.17
  1.4 29.5 %collective-permute-start = (f32[18,128]{1,0:T(8,128)S(1)}, f32[18,128]{1,0:T(8,128)S(1)}, u32[]{:S(2)}, u32[]{:S(2)}) collective-permute-start(f32[18,128]{1,0:T(8,128)S(1)} %slice.68), channel_id=1, source_target_pairs={{0,16},{1,17},{2,18},{3,19},{4,20},{5,21},{6,22},{7,23},{8,24},{9,... | collective-permute-start | bytes 27656 | tf_op jit(solution)/shard_map/ppermute | solution.py:42
  31.0 1.1 collective-permute-done
  32.2 21.6 %collective-permute-start.7 = (f32[18,128]{1,0:T(8,128)S(1)}, f32[18,128]{1,0:T(8,128)S(1)}, u32[]{:S(2)}, u32[]{:S(2)}) collective-permute-start(f32[18,128]{1,0:T(8,128)S(1)} %get-tuple-element.35), channel_id=1, source_target_pairs={{0,16},{1,17},{2,18},{3,19},{4,20},{5,21},{6,22},{7,23},{8,24},{9,... | collective-permute-start | bytes 27656 | tf_op jit(solution)/shard_map/ppermute | solution.py:42
  53.8 5.8 %collective-permute-start.1 = (f32[2,18,128]{2,0,1:T(2,128)S(1)}, f32[2,18,128]{2,0,1:T(2,128)S(1)}, u32[]{:S(2)}, u32[]{:S(2)}) collective-permute-start(f32[2,18,128]{2,0,1:T(2,128)S(1)} %pad_maximum_fusion.18), channel_id=1, source_target_pairs={{0,8},{1,9},{2,10},{3,11},{4,12},{5,13},{6,14},{7,15},{8,0},{9,1},... | collective-permute-start | bytes 55304 | tf_op jit(solution)/shard_map/ppermute | solution.py:42
  59.7 8.2 %collective-permute-start.8 = (f32[2,18,128]{2,0,1:T(2,128)S(1)}, f32[2,18,128]{2,0,1:T(2,128)S(1)}, u32[]{:S(2)}, u32[]{:S(2)}) collective-permute-start(f32[2,18,128]{2,0,1:T(2,128)S(1)} %pad_maximum_fusion.19), channel_id=1, source_target_pairs={{0,8},{1,9},{2,10},{3,11},{4,12},{5,13},{6,14},{7,15},{8,0},{9,1},... | collective-permute-start | bytes 55304 | tf_op jit(solution)/shard_map/ppermute | solution.py:42
  68.0 4.4 %collective-permute-start.2 = (f32[2,2,18,128]{3,0,2,1:T(2,128)S(1)}, f32[2,2,18,128]{3,0,2,1:T(2,128)S(1)}, u32[]{:S(2)}, u32[]{:S(2)}) collective-permute-start(f32[2,2,18,128]{3,0,2,1:T(2,128)S(1)} %pad_maximum_fusion.15), channel_id=1, source_target_pairs={{0,4},{1,5},{2,6},{3,7},{4,0},{5,1},{6,2},{7,3},{8,12},{9,13},{10,... | collective-permute-start | bytes 110600 | tf_op jit(solution)/shard_map/ppermute | solution.py:42
  72.4 0.6 collective-permute-done.8
  73.0 4.2 %collective-permute-start.9 = (f32[2,2,18,128]{3,0,2,1:T(2,128)S(1)}, f32[2,2,18,128]{3,0,2,1:T(2,128)S(1)}, u32[]{:S(2)}, u32[]{:S(2)}) collective-permute-start(f32[2,2,18,128]{3,0,2,1:T(2,128)S(1)} %pad_maximum_fusion.16), channel_id=1, source_target_pairs={{0,4},{1,5},{2,6},{3,7},{4,0},{5,1},{6,2},{7,3},{8,12},{9,13},{10,... | collective-permute-start | bytes 110600 | tf_op jit(solution)/shard_map/ppermute | solution.py:42
  77.3 0.8 collective-permute-done.2
  78.1 2.7 %collective-permute-start.3 = (f32[2,2,2,18,128]{4,0,3,1,2:T(2,128)S(1)}, f32[2,2,2,18,128]{4,0,3,1,2:T(2,128)S(1)}, u32[]{:S(2)}, u32[]{:S(2)}) collective-permute-start(f32[2,2,2,18,128]{4,0,3,1,2:T(2,128)S(1)} %pad_maximum_fusion.13), channel_id=1, source_target_pairs={{0,2},{1,3},{2,0},{3,1},{4,6},{5,7},{6,4},{7,5},{8,10},{9,11},{10,... | collective-permute-start | bytes 221192 | tf_op jit(solution)/shard_map/ppermute | solution.py:42
  80.8 0.8 collective-permute-done.9
  81.7 4.7 %collective-permute-start.10 = (f32[2,2,2,18,128]{4,0,3,1,2:T(2,128)S(1)}, f32[2,2,2,18,128]{4,0,3,1,2:T(2,128)S(1)}, u32[]{:S(2)}, u32[]{:S(2)}) collective-permute-start(f32[2,2,2,18,128]{4,0,3,1,2:T(2,128)S(1)} %pad_maximum_fusion.14), channel_id=1, source_target_pairs={{0,64},{1,65},{2,66},{3,67},{4,68},{5,69},{6,70},{7,71},{8,72},{9,... | collective-permute-start | bytes 221192 | tf_op jit(solution)/shard_map/ppermute | solution.py:42
  86.5 2.9 %collective-permute-start.4 = (f32[2,2,2,2,18,128]{5,0,4,1,2,3:T(2,128)S(1)}, f32[2,2,2,2,18,128]{5,0,4,1,2,3:T(2,128)S(1)}, u32[]{:S(2)}, u32[]{:S(2)}) collective-permute-start(f32[2,2,2,2,18,128]{5,0,4,1,2,3:T(2,128)S(1)} %pad_maximum_fusion.11), channel_id=1, source_target_pairs={{0,1},{1,0},{2,3},{3,2},{4,5},{5,4},{6,7},{7,6},{8,9},{9,8},{10,11... | collective-permute-start | bytes 442376 | tf_op jit(solution)/shard_map/ppermute | solution.py:42
  89.6 2.2 %collective-permute-start.11 = (f32[2,2,2,2,18,128]{5,1,4,2,3,0:T(2,128)S(1)}, f32[2,2,2,2,18,128]{5,1,4,2,3,0:T(2,128)S(1)}, u32[]{:S(2)}, u32[]{:S(2)}) collective-permute-start(f32[2,2,2,2,18,128]{5,1,4,2,3,0:T(2,128)S(1)} %pad_maximum_fusion.12), channel_id=1, source_target_pairs={{0,32},{1,33},{2,34},{3,35},{4,36},{5,37},{6,38},{7,39},{8,40},{9,... | collective-permute-start | bytes 442376 | tf_op jit(solution)/shard_map/ppermute | solution.py:42
  91.9 0.6 collective-permute-done.4
  92.4 0.1 select_bitcast_fusion.11
  92.5 0.1 pad_maximum_fusion.7
  92.7 3.5 %collective-permute-start.5 = (f32[2,2,2,2,2,18,128]{6,0,5,1,2,3,4:T(2,128)S(1)}, f32[2,2,2,2,2,18,128]{6,0,5,1,2,3,4:T(2,128)S(1)}, u32[]{:S(2)}, u32[]{:S(2)}) collective-permute-start(f32[2,2,2,2,2,18,128]{6,0,5,1,2,3,4:T(2,128)S(1)} %pad_maximum_fusion.7), channel_id=1, source_target_pairs={{0,64},{1,65},{2,66},{3,67},{4,68},{5,69},{6,70},{7,71},{8,72},{9,... | collective-permute-start | bytes 884744 | tf_op jit(solution)/shard_map/ppermute | solution.py:42
  96.2 0.1 select_bitcast_fusion.9
  96.4 0.1 pad_maximum_fusion.8
  96.5 4.4 %collective-permute-start.12 = (f32[2,2,2,2,2,18,128]{6,2,5,3,4,0,1:T(2,128)S(1)}, f32[2,2,2,2,2,18,128]{6,2,5,3,4,0,1:T(2,128)S(1)}, u32[]{:S(2)}, u32[]{:S(2)}) collective-permute-start(f32[2,2,2,2,2,18,128]{6,2,5,3,4,0,1:T(2,128)S(1)} %pad_maximum_fusion.8), channel_id=1, source_target_pairs={{0,2},{1,3},{2,0},{3,1},{4,6},{5,7},{6,4},{7,5},{8,10},{9,11},{10,... | collective-permute-start | bytes 884744 | tf_op jit(solution)/shard_map/ppermute | solution.py:42
  100.9 1.1 collective-permute-done.5
  102.0 0.2 select_bitcast_fusion.7
  102.2 0.3 pad_maximum_fusion.3
  102.5 0.5 copy.88
  103.0 2.7 %collective-permute-start.6 = (f32[2,2,2,2,2,2,18,128]{7,5,6,4,3,2,1,0:T(2,128)S(1)}, f32[2,2,2,2,2,2,18,128]{7,5,6,4,3,2,1,0:T(2,128)S(1)}, u32[]{:S(2)}, u32[]{:S(2)}) collective-permute-start(f32[2,2,2,2,2,2,18,128]{7,5,6,4,3,2,1,0:T(2,128)S(1)} %copy.88), channel_id=1, source_target_pairs={{0,32},{1,33},{2,34},{3,35},{4,36},{5,37},{6,38},{7,39},{8,40},{9,... | collective-permute-start | bytes 1769480 | tf_op jit(solution)/shard_map/ppermute | solution.py:42
  105.7 2.8 %collective-permute-done.12 = f32[2,2,2,2,2,18,128]{6,2,5,3,4,0,1:T(2,128)S(1)} collective-permute-done((f32[2,2,2,2,2,18,128]{6,2,5,3,4,0,1:T(2,128)S(1)}, f32[2,2,2,2,2,18,128]{6,2,5,3,4,0,1:T(2,128)S(1)}, u32[]{:S(2)}, u32[]{:S(2)}) %collective-permute-start.12) | collective-permute-done | bytes 294944 | tf_op jit(solution)/shard_map/ppermute | solution.py:42
  108.5 0.2 select_bitcast_fusion.5
  108.7 0.3 pad_maximum_fusion.4
  109.0 0.5 copy.94
  109.5 2.5 %collective-permute-start.13 = (f32[2,2,2,2,2,2,18,128]{7,5,6,4,3,2,1,0:T(2,128)S(1)}, f32[2,2,2,2,2,2,18,128]{7,5,6,4,3,2,1,0:T(2,128)S(1)}, u32[]{:S(2)}, u32[]{:S(2)}) collective-permute-start(f32[2,2,2,2,2,2,18,128]{7,5,6,4,3,2,1,0:T(2,128)S(1)} %copy.94), channel_id=1, source_target_pairs={{0,1},{1,0},{2,3},{3,2},{4,5},{5,4},{6,7},{7,6},{8,9},{9,8},{10,11... | collective-permute-start | bytes 1769480 | tf_op jit(solution)/shard_map/ppermute | solution.py:42
  112.0 2.0 %collective-permute-done.6 = f32[2,2,2,2,2,2,18,128]{7,5,6,4,3,2,1,0:T(2,128)S(1)} collective-permute-done((f32[2,2,2,2,2,2,18,128]{7,5,6,4,3,2,1,0:T(2,128)S(1)}, f32[2,2,2,2,2,2,18,128]{7,5,6,4,3,2,1,0:T(2,128)S(1)}, u32[]{:S(2)}, u32[]{:S(2)}) %collective-permute-start.6) | collective-permute-done | bytes 589856 | tf_op jit(solution)/shard_map/ppermute | solution.py:42
  114.0 0.7 select_bitcast_fusion.3
  114.8 0.6 pad_maximum_fusion.1
  115.4 0.9 copy.91
  116.4 5.3 %collective-permute-done.13 = f32[2,2,2,2,2,2,18,128]{7,5,6,4,3,2,1,0:T(2,128)S(1)} collective-permute-done((f32[2,2,2,2,2,2,18,128]{7,5,6,4,3,2,1,0:T(2,128)S(1)}, f32[2,2,2,2,2,2,18,128]{7,5,6,4,3,2,1,0:T(2,128)S(1)}, u32[]{:S(2)}, u32[]{:S(2)}) %collective-permute-start.13) | collective-permute-done | bytes 589856 | tf_op jit(solution)/shard_map/ppermute | solution.py:42
  121.7 0.5 select_bitcast_fusion.1
  122.2 0.6 pad_maximum_fusion.2
  122.9 0.9 copy.97
  123.9 0.2 copy.99
  124.1 0.9 reshape.18
  125.0 0.7 pad_maximum_fusion.9
  125.8 0.2 copy.100
  126.0 0.1 pad_maximum_fusion
  126.1 2.3 %copy.98 = f32[128,12,256]{2,1,0:T(8,128)} copy(f32[128,12,256]{2,0,1:T(8,128)S(1)} %pad_maximum_fusion) | data formatting | bytes 3145728 | tf_op jit(solution)/shard_map/concatenate | solution.py:83
  128.4 1.7 %reshape.17 = f32[1536,256]{1,0:T(8,128)S(1)} reshape(f32[128,12,256]{2,1,0:T(8,128)} %copy.98) | data formatting | bytes 3145728 | tf_op jit(solution)/shard_map/reshape | solution.py:83
  130.2 0.3 copy-done
  130.5 2.5 %fusion = f32[256,256]{1,0:T(8,128)S(1)} fusion(f32[1536,256]{1,0:T(8,128)S(1)} %copy-done, f32[1536,256]{1,0:T(8,128)S(1)} %reshape.17), kind=kOutput, calls=%fused_computation.5 | convolution fusion | flops 1209532416 | bytes 3407872 | tf_op jit(solution)/shard_map/dot_general | solution.py:20
  133.0 0.7 fusion.12
  133.7 1.4 convolution_subtract_fusion
  135.2 1.1 copy-done.1
  136.4 9.4 %collective-permute-start.14 = (f32[512,256]{1,0:T(8,128)S(1)}, f32[512,256]{1,0:T(8,128)S(1)}, u32[]{:S(2)}, u32[]{:S(2)}) collective-permute-start(f32[512,256]{1,0:T(8,128)S(1)} %pad_maximum_fusion.5), channel_id=1, source_target_pairs={{0,128},{128,0},{256,384},{384,256},{512,640},{640,512},{768,896},... | collective-permute-start | bytes 1572872 | tf_op jit(solution)/shard_map/ppermute | solution.py:8
  145.8 0.2 copy.101
  146.0 1.0 collective-permute-done.14
  147.0 1.6 convolution_add_fusion.1
  148.7 0.7 fusion.9
  149.3 1.3 subtract_select_fusion
  150.7 2.8 %collective-permute-start.15 = (f32[512,256]{1,0:T(8,128)S(1)}, f32[512,256]{1,0:T(8,128)S(1)}, u32[]{:S(2)}, u32[]{:S(2)}) collective-permute-start(f32[512,256]{1,0:T(8,128)S(1)} %pad_maximum_fusion.6), channel_id=1, source_target_pairs={{0,256},{128,384},{256,0},{384,128},{512,768},{640,896},{768,512},... | collective-permute-start | bytes 1572872 | tf_op jit(solution)/shard_map/ppermute | solution.py:8
  153.5 12.2 %collective-permute-done.15 = f32[512,256]{1,0:T(8,128)S(1)} collective-permute-done((f32[512,256]{1,0:T(8,128)S(1)}, f32[512,256]{1,0:T(8,128)S(1)}, u32[]{:S(2)}, u32[]{:S(2)}) %collective-permute-start.15) | collective-permute-done | bytes 524320 | tf_op jit(solution)/shard_map/ppermute | solution.py:8
  165.7 0.6 convolution_add_fusion
  166.3 0.7 fusion.6
  167.0 1.1 select_dynamic-update-slice_fusion
  (45 shorter events, 1.1 us)
Async XLA Ops:
  1.4 30.7 %collective-permute-start = (f32[18,128]{1,0:T(8,128)S(1)}, f32[18,128]{1,0:T(8,128)S(1)}, u32[]{:S(2)}, u32[]{:S(2)}) collective-permute-start(f32[18,128]{1,0:T(8,128)S(1)} %slice.68), channel_id=1, source_target_pairs={{0,16},{1,17},{2,18},{3,19},{4,20},{5,21},{6,22},{7,23},{8,24},{9,... | collective-permute-start | bytes 27656 | tf_op jit(solution)/shard_map/ppermute | solution.py:42
  32.2 27.5 %collective-permute-start.7 = (f32[18,128]{1,0:T(8,128)S(1)}, f32[18,128]{1,0:T(8,128)S(1)}, u32[]{:S(2)}, u32[]{:S(2)}) collective-permute-start(f32[18,128]{1,0:T(8,128)S(1)} %get-tuple-element.35), channel_id=1, source_target_pairs={{0,16},{1,17},{2,18},{3,19},{4,20},{5,21},{6,22},{7,23},{8,24},{9,... | collective-permute-start | bytes 27656 | tf_op jit(solution)/shard_map/ppermute | solution.py:42
  53.8 14.1 %collective-permute-start.1 = (f32[2,18,128]{2,0,1:T(2,128)S(1)}, f32[2,18,128]{2,0,1:T(2,128)S(1)}, u32[]{:S(2)}, u32[]{:S(2)}) collective-permute-start(f32[2,18,128]{2,0,1:T(2,128)S(1)} %pad_maximum_fusion.18), channel_id=1, source_target_pairs={{0,8},{1,9},{2,10},{3,11},{4,12},{5,13},{6,14},{7,15},{8,0},{9,1},... | collective-permute-start | bytes 55304 | tf_op jit(solution)/shard_map/ppermute | solution.py:42
  59.7 13.2 %collective-permute-start.8 = (f32[2,18,128]{2,0,1:T(2,128)S(1)}, f32[2,18,128]{2,0,1:T(2,128)S(1)}, u32[]{:S(2)}, u32[]{:S(2)}) collective-permute-start(f32[2,18,128]{2,0,1:T(2,128)S(1)} %pad_maximum_fusion.19), channel_id=1, source_target_pairs={{0,8},{1,9},{2,10},{3,11},{4,12},{5,13},{6,14},{7,15},{8,0},{9,1},... | collective-permute-start | bytes 55304 | tf_op jit(solution)/shard_map/ppermute | solution.py:42
  68.0 10.1 %collective-permute-start.2 = (f32[2,2,18,128]{3,0,2,1:T(2,128)S(1)}, f32[2,2,18,128]{3,0,2,1:T(2,128)S(1)}, u32[]{:S(2)}, u32[]{:S(2)}) collective-permute-start(f32[2,2,18,128]{3,0,2,1:T(2,128)S(1)} %pad_maximum_fusion.15), channel_id=1, source_target_pairs={{0,4},{1,5},{2,6},{3,7},{4,0},{5,1},{6,2},{7,3},{8,12},{9,13},{10,... | collective-permute-start | bytes 110600 | tf_op jit(solution)/shard_map/ppermute | solution.py:42
  73.0 8.6 %collective-permute-start.9 = (f32[2,2,18,128]{3,0,2,1:T(2,128)S(1)}, f32[2,2,18,128]{3,0,2,1:T(2,128)S(1)}, u32[]{:S(2)}, u32[]{:S(2)}) collective-permute-start(f32[2,2,18,128]{3,0,2,1:T(2,128)S(1)} %pad_maximum_fusion.16), channel_id=1, source_target_pairs={{0,4},{1,5},{2,6},{3,7},{4,0},{5,1},{6,2},{7,3},{8,12},{9,13},{10,... | collective-permute-start | bytes 110600 | tf_op jit(solution)/shard_map/ppermute | solution.py:42
  78.1 8.2 %collective-permute-start.3 = (f32[2,2,2,18,128]{4,0,3,1,2:T(2,128)S(1)}, f32[2,2,2,18,128]{4,0,3,1,2:T(2,128)S(1)}, u32[]{:S(2)}, u32[]{:S(2)}) collective-permute-start(f32[2,2,2,18,128]{4,0,3,1,2:T(2,128)S(1)} %pad_maximum_fusion.13), channel_id=1, source_target_pairs={{0,2},{1,3},{2,0},{3,1},{4,6},{5,7},{6,4},{7,5},{8,10},{9,11},{10,... | collective-permute-start | bytes 221192 | tf_op jit(solution)/shard_map/ppermute | solution.py:42
  81.7 7.8 %collective-permute-start.10 = (f32[2,2,2,18,128]{4,0,3,1,2:T(2,128)S(1)}, f32[2,2,2,18,128]{4,0,3,1,2:T(2,128)S(1)}, u32[]{:S(2)}, u32[]{:S(2)}) collective-permute-start(f32[2,2,2,18,128]{4,0,3,1,2:T(2,128)S(1)} %pad_maximum_fusion.14), channel_id=1, source_target_pairs={{0,64},{1,65},{2,66},{3,67},{4,68},{5,69},{6,70},{7,71},{8,72},{9,... | collective-permute-start | bytes 221192 | tf_op jit(solution)/shard_map/ppermute | solution.py:42
  86.5 5.9 %collective-permute-start.4 = (f32[2,2,2,2,18,128]{5,0,4,1,2,3:T(2,128)S(1)}, f32[2,2,2,2,18,128]{5,0,4,1,2,3:T(2,128)S(1)}, u32[]{:S(2)}, u32[]{:S(2)}) collective-permute-start(f32[2,2,2,2,18,128]{5,0,4,1,2,3:T(2,128)S(1)} %pad_maximum_fusion.11), channel_id=1, source_target_pairs={{0,1},{1,0},{2,3},{3,2},{4,5},{5,4},{6,7},{7,6},{8,9},{9,8},{10,11... | collective-permute-start | bytes 442376 | tf_op jit(solution)/shard_map/ppermute | solution.py:42
  89.6 6.6 %collective-permute-start.11 = (f32[2,2,2,2,18,128]{5,1,4,2,3,0:T(2,128)S(1)}, f32[2,2,2,2,18,128]{5,1,4,2,3,0:T(2,128)S(1)}, u32[]{:S(2)}, u32[]{:S(2)}) collective-permute-start(f32[2,2,2,2,18,128]{5,1,4,2,3,0:T(2,128)S(1)} %pad_maximum_fusion.12), channel_id=1, source_target_pairs={{0,32},{1,33},{2,34},{3,35},{4,36},{5,37},{6,38},{7,39},{8,40},{9,... | collective-permute-start | bytes 442376 | tf_op jit(solution)/shard_map/ppermute | solution.py:42
  92.7 9.3 %collective-permute-start.5 = (f32[2,2,2,2,2,18,128]{6,0,5,1,2,3,4:T(2,128)S(1)}, f32[2,2,2,2,2,18,128]{6,0,5,1,2,3,4:T(2,128)S(1)}, u32[]{:S(2)}, u32[]{:S(2)}) collective-permute-start(f32[2,2,2,2,2,18,128]{6,0,5,1,2,3,4:T(2,128)S(1)} %pad_maximum_fusion.7), channel_id=1, source_target_pairs={{0,64},{1,65},{2,66},{3,67},{4,68},{5,69},{6,70},{7,71},{8,72},{9,... | collective-permute-start | bytes 884744 | tf_op jit(solution)/shard_map/ppermute | solution.py:42
  96.5 12.0 %collective-permute-start.12 = (f32[2,2,2,2,2,18,128]{6,2,5,3,4,0,1:T(2,128)S(1)}, f32[2,2,2,2,2,18,128]{6,2,5,3,4,0,1:T(2,128)S(1)}, u32[]{:S(2)}, u32[]{:S(2)}) collective-permute-start(f32[2,2,2,2,2,18,128]{6,2,5,3,4,0,1:T(2,128)S(1)} %pad_maximum_fusion.8), channel_id=1, source_target_pairs={{0,2},{1,3},{2,0},{3,1},{4,6},{5,7},{6,4},{7,5},{8,10},{9,11},{10,... | collective-permute-start | bytes 884744 | tf_op jit(solution)/shard_map/ppermute | solution.py:42
  103.0 11.0 %collective-permute-start.6 = (f32[2,2,2,2,2,2,18,128]{7,5,6,4,3,2,1,0:T(2,128)S(1)}, f32[2,2,2,2,2,2,18,128]{7,5,6,4,3,2,1,0:T(2,128)S(1)}, u32[]{:S(2)}, u32[]{:S(2)}) collective-permute-start(f32[2,2,2,2,2,2,18,128]{7,5,6,4,3,2,1,0:T(2,128)S(1)} %copy.88), channel_id=1, source_target_pairs={{0,32},{1,33},{2,34},{3,35},{4,36},{5,37},{6,38},{7,39},{8,40},{9,... | collective-permute-start | bytes 1769480 | tf_op jit(solution)/shard_map/ppermute | solution.py:42
  109.5 12.2 %collective-permute-start.13 = (f32[2,2,2,2,2,2,18,128]{7,5,6,4,3,2,1,0:T(2,128)S(1)}, f32[2,2,2,2,2,2,18,128]{7,5,6,4,3,2,1,0:T(2,128)S(1)}, u32[]{:S(2)}, u32[]{:S(2)}) collective-permute-start(f32[2,2,2,2,2,2,18,128]{7,5,6,4,3,2,1,0:T(2,128)S(1)} %copy.94), channel_id=1, source_target_pairs={{0,1},{1,0},{2,3},{3,2},{4,5},{5,4},{6,7},{7,6},{8,9},{9,8},{10,11... | collective-permute-start | bytes 1769480 | tf_op jit(solution)/shard_map/ppermute | solution.py:42
  128.4 2.0 %copy-start = (f32[1536,256]{1,0:T(8,128)S(1)}, f32[1536,256]{1,0:T(8,128)}, u32[]{:S(2)}) copy-start(f32[1536,256]{1,0:T(8,128)} %param.5) | copy-start | bytes 4718596
  130.5 2.6 %copy-start.2 = (f32[256,256]{1,0:T(8,128)S(1)}, f32[256,256]{1,0:T(8,128)}, u32[]{:S(2)}) copy-start(f32[256,256]{1,0:T(8,128)} %reshape.18) | copy-start | bytes 786436
  135.2 1.1 copy-start.1
  136.3 9.4 %copy-start.3 = (f32[64,4,256]{2,0,1:T(8,128)S(1)}, f32[64,4,256]{2,0,1:T(8,128)}, u32[]{:S(2)}) copy-start(f32[64,4,256]{2,0,1:T(8,128)} %get-tuple-element.13) | copy-start | bytes 786436
  136.4 10.7 %collective-permute-start.14 = (f32[512,256]{1,0:T(8,128)S(1)}, f32[512,256]{1,0:T(8,128)S(1)}, u32[]{:S(2)}, u32[]{:S(2)}) collective-permute-start(f32[512,256]{1,0:T(8,128)S(1)} %pad_maximum_fusion.5), channel_id=1, source_target_pairs={{0,128},{128,0},{256,384},{384,256},{512,640},{640,512},{768,896},... | collective-permute-start | bytes 1572872 | tf_op jit(solution)/shard_map/ppermute | solution.py:8
  150.7 15.0 %collective-permute-start.15 = (f32[512,256]{1,0:T(8,128)S(1)}, f32[512,256]{1,0:T(8,128)S(1)}, u32[]{:S(2)}, u32[]{:S(2)}) collective-permute-start(f32[512,256]{1,0:T(8,128)S(1)} %pad_maximum_fusion.6), channel_id=1, source_target_pairs={{0,256},{128,384},{256,0},{384,128},{512,768},{640,896},{768,512},... | collective-permute-start | bytes 1572872 | tf_op jit(solution)/shard_map/ppermute | solution.py:8

commit v3 on v2

--- a/solution.py
+++ b/solution.py
@@ -30,32 +30,36 @@
     return jnp.dot(left, right, precision=lax.Precision.HIGHEST, preferred_element_type=jnp.float32)
 
 
-def doubling_gather(shard, axis, orders):
+def doubling_gather(shard, axis, shared, orders):
     n = lax.axis_size(axis)
-    bits = n.bit_length() - 1
     me = lax.axis_index(axis)
+
+    def step(buf, held, bit):
+        got = lax.ppermute(buf, axis, [(i, i ^ 1 << bit) for i in range(n)])
+        low = (me >> bit) & 1 == 0
+        pos = sum(1 for b in held if b > bit)
+        return jnp.stack([jnp.where(low, buf, got), jnp.where(low, got, buf)], axis=pos), held[:pos] + [bit] + held[pos:]
+
+    buf, held = shard, []
+    for bit in shared:
+        buf, held = step(buf, held, bit)
     width = shard.shape[1] // len(orders)
-    bufs = [shard[:, j * width:(j + 1) * width] for j in range(len(orders))]
-    held = [[] for _ in orders]
-    for step in range(bits):
-        received = [
-            lax.ppermute(buf, axis, [(i, i ^ 1 << order[step]) for i in range(n)])
-            for buf, order in zip(bufs, orders)
-        ]
-        for j, (got, order) in enumerate(zip(received, orders)):
-            bit = order[step]
-            low = (me >> bit) & 1 == 0
-            pos = sum(1 for b in held[j] if b > bit)
-            bufs[j] = jnp.stack([jnp.where(low, bufs[j], got), jnp.where(low, got, bufs[j])], axis=pos)
-            held[j].insert(pos, bit)
-    return [buf.reshape((n,) + shard.shape[:1] + (width,)) for buf in bufs]
+    bufs = [buf[..., j * width:(j + 1) * width] for j in range(len(orders))]
+    helds = [held] * len(orders)
+    for k in range(len(orders[0])):
+        for j, order in enumerate(orders):
+            bufs[j], helds[j] = step(bufs[j], helds[j], order[k])
+    return [b.reshape((n,) + shard.shape[:1] + (width,)) for b in bufs]
 
 
-def combine(top_rows, refl_mine, level):
+def combine(top_rows, refl_mine, partner_refl, level):
     lower_side = lax.axis_index("row") // 2**level % 2 == 0
     width = top_rows.shape[0]
-    incoming = swapped(jnp.concatenate([top_rows, refl_mine], axis=0), "row", level)
-    partner_top, partner_refl = incoming[:width], incoming[width:]
+    if partner_refl is None:
+        incoming = swapped(jnp.concatenate([top_rows, refl_mine], axis=0), "row", level)
+        partner_top, partner_refl = incoming[:width], incoming[width:]
+    else:
+        partner_top = swapped(top_rows, "row", level)
     refl_y = jnp.where(lower_side, refl_mine, partner_refl)
     refl_t = jnp.triu(jnp.where(lower_side, partner_refl, refl_mine))
     lower_top = jnp.where(lower_side, top_rows, partner_top)
@@ -74,9 +78,9 @@
     tree_mine = jnp.where((row >> shard_level) & 1 == 0, tree_y, tree_t)
     packed = jnp.concatenate([leaf_v, leaf_t, tree_mine], axis=0)
     bits = n_col.bit_length() - 1
-    high = list(range(bits - 3, -1, -1))
-    orders = (high + [bits - 1, bits - 2], high[:3] + [bits - 1, bits - 2] + high[3:])
-    pieces = doubling_gather(packed, "col", orders)
+    shared = list(range(bits - 3, 1, -1))
+    orders = ([1, 0, bits - 1, bits - 2], [bits - 1, bits - 2, 1, 0])
+    pieces = doubling_gather(packed, "col", shared, orders)
     nv, nt = leaf_v.shape[0], leaf_t.shape[0]
 
     def joined(lo, hi):
@@ -85,11 +89,13 @@
     v_rows = unit_lower(joined(0, nv))
     t_leaf = joined(nv, nv + nt)
     tree_rows = joined(nv + nt, packed.shape[0])
+    refl = [tree_rows[level * width:(level + 1) * width] for level in range(tree_depth)]
+    partner_refl = [None] + [swapped(refl[level], "row", level) for level in range(1, tree_depth)]
     coeffs = inner(jnp.triu(t_leaf), inner(v_rows, trailing))
     updated = trailing - matmul(v_rows, coeffs)
     top_rows = updated[:width]
     for level in range(tree_depth):
-        top_rows = combine(top_rows, tree_rows[level * width:(level + 1) * width], level)
+        top_rows = combine(top_rows, refl[level], partner_refl[level], level)
     return lax.dynamic_update_slice(updated, top_rows, (0, 0))
 
 

time: 169 us -> 150 us (0.89)
  starting transfers between devices: 111 us -> 89.5 us
  waiting for transfers between devices: 28.3 us -> 31.2 us
    ppermute x14 -> x11, starting transfers between devices: 99.3 us -> 73.5 us  [step(): got = lax.ppermute(buf, axis, [(i, i ^ 1 << bit) for i in range(n)])]
    ppermute x14 -> x11, waiting for transfers between devices: 15.1 us -> 23.7 us  [step(): got = lax.ppermute(buf, axis, [(i, i ^ 1 << bit) for i in range(n)])]
    ppermute x2 -> x3, waiting for transfers between devices: 13.2 us -> 7.51 us  [swapped(): lax.ppermute(shard, axis, [(i, i ^ 1 << stride) for i in range(lax.axis_s...]
    ppermute x2 -> x3, starting transfers between devices: 12.1 us -> 16 us  [swapped(): lax.ppermute(shard, axis, [(i, i ^ 1 << stride) for i in range(lax.axis_s...]
    another operation x28 -> x22, other arithmetic: 4.53 us -> 5.24 us  [step(): jnp.stack([jnp.where(low, buf, got), jnp.where(low, got, buf)], axis=pos)]
  transfers between devices with their start and end apart: 16 -> 14, of which waited for: 11 -> 10; matrix products, arithmetic and copies ran while one was open for 3% -> 6% of each run, Pallas kernels for 0% -> 0%
where the time goes in v3:
time: 150 us
  starting transfers between devices  89.5 us (60%)
  waiting for transfers between devices  31.2 us (21%)
  matrix products  10.7 us (7%)
  local copies, waits for them, and re-layouts  10 us (7%)
  other arithmetic  7.59 us (5%)
    ppermute x11, starting transfers between devices, step(): got = lax.ppermute(buf, axis, [(i, i ^ 1 << bit) for i in range(n)])  73.5 us
    ppermute x11, waiting for transfers between devices, step(): got = lax.ppermute(buf, axis, [(i, i ^ 1 << bit) for i in range(n)])  23.7 us
    ppermute x3, starting transfers between devices, swapped(): lax.ppermute(shard, axis, [(i, i ^ 1 << stride) for i in range(lax.axis_s...  16 us
    ppermute x3, waiting for transfers between devices, swapped(): lax.ppermute(shard, axis, [(i, i ^ 1 << stride) for i in range(lax.axis_s...  7.51 us
    dot_general x6, matrix products, inner(): lax.dot_general(left, right, (((0,), (0,)), ((), ())), precision=lax.Prec...  6.79 us
    another operation x22, other arithmetic, step(): jnp.stack([jnp.where(low, buf, got), jnp.where(low, got, buf)], axis=pos)  5.24 us
    dot_general x3, matrix products, matmul(): jnp.dot(left, right, precision=lax.Precision.HIGHEST, preferred_element_t...  3.91 us
  transfers between devices with their start and end apart: 14, of which 10 were waited for; matrix products, arithmetic and copies ran while one was open for 6% of the time, Pallas kernels for 0%

profile of v3, /device:TPU:1, one launch (start us, length us, event | category | flops | bytes accessed | tf_op | source)
XLA Modules:
  0.0 149.7 jit_solution(8554531488439377315)
XLA Ops:
  0.0 0.7 broadcast_select_fusion.9
  0.7 0.7 pad_maximum_fusion.15
  1.4 29.5 %collective-permute-start = (f32[18,256]{1,0:T(8,128)S(1)}, f32[18,256]{1,0:T(8,128)S(1)}, u32[]{:S(2)}, u32[]{:S(2)}) collective-permute-start(f32[18,256]{1,0:T(8,128)S(1)} %pad_maximum_fusion.15), channel_id=1, source_target_pairs={{0,16},{1,17},{2,18},{3,19},{4,20},{5,21},{6,22},{7,23},{8,24},{9,... | collective-permute-start | bytes 55304 | tf_op jit(solution)/shard_map/ppermute | solution.py:38
  31.0 1.3 collective-permute-done
  32.3 0.7 select_bitcast_fusion.20
  33.1 8.4 %collective-permute-start.1 = (f32[2,18,256]{2,0,1:T(2,128)S(1)}, f32[2,18,256]{2,0,1:T(2,128)S(1)}, u32[]{:S(2)}, u32[]{:S(2)}) collective-permute-start(f32[2,18,256]{2,0,1:T(2,128)S(1)} %pad_maximum_fusion.14), channel_id=1, source_target_pairs={{0,8},{1,9},{2,10},{3,11},{4,12},{5,13},{6,14},{7,15},{8,0},{9,1},... | collective-permute-start | bytes 110600 | tf_op jit(solution)/shard_map/ppermute | solution.py:38
  41.5 5.0 %collective-permute-done.1 = f32[2,18,256]{2,0,1:T(2,128)S(1)} collective-permute-done((f32[2,18,256]{2,0,1:T(2,128)S(1)}, f32[2,18,256]{2,0,1:T(2,128)S(1)}, u32[]{:S(2)}, u32[]{:S(2)}) %collective-permute-start.1) | collective-permute-done | bytes 36896 | tf_op jit(solution)/shard_map/ppermute | solution.py:38
  46.6 5.2 %collective-permute-start.2 = (f32[2,2,18,256]{3,0,2,1:T(2,128)S(1)}, f32[2,2,18,256]{3,0,2,1:T(2,128)S(1)}, u32[]{:S(2)}, u32[]{:S(2)}) collective-permute-start(f32[2,2,18,256]{3,0,2,1:T(2,128)S(1)} %pad_maximum_fusion.13), channel_id=1, source_target_pairs={{0,4},{1,5},{2,6},{3,7},{4,0},{5,1},{6,2},{7,3},{8,12},{9,13},{10,... | collective-permute-start | bytes 221192 | tf_op jit(solution)/shard_map/ppermute | solution.py:38
  51.8 4.6 %collective-permute-done.2 = f32[2,2,18,256]{3,0,2,1:T(2,128)S(1)} collective-permute-done((f32[2,2,18,256]{3,0,2,1:T(2,128)S(1)}, f32[2,2,18,256]{3,0,2,1:T(2,128)S(1)}, u32[]{:S(2)}, u32[]{:S(2)}) %collective-permute-start.2) | collective-permute-done | bytes 73760 | tf_op jit(solution)/shard_map/ppermute | solution.py:38
  56.6 4.0 %collective-permute-start.3 = (f32[2,2,2,18,128]{4,0,3,1,2:T(2,128)S(1)}, f32[2,2,2,18,128]{4,0,3,1,2:T(2,128)S(1)}, u32[]{:S(2)}, u32[]{:S(2)}) collective-permute-start(f32[2,2,2,18,128]{4,0,3,1,2:T(2,128)S(1)} %get-tuple-element.21), channel_id=1, source_target_pairs={{0,2},{1,3},{2,0},{3,1},{4,6},{5,7},{6,4},{7,5},{8,10},{9,11},{10,... | collective-permute-start | bytes 221192 | tf_op jit(solution)/shard_map/ppermute | solution.py:38
  60.6 6.3 %collective-permute-start.7 = (f32[2,2,2,18,128]{4,0,3,1,2:T(2,128)S(1)}, f32[2,2,2,18,128]{4,0,3,1,2:T(2,128)S(1)}, u32[]{:S(2)}, u32[]{:S(2)}) collective-permute-start(f32[2,2,2,18,128]{4,0,3,1,2:T(2,128)S(1)} %get-tuple-element.22), channel_id=1, source_target_pairs={{0,64},{1,65},{2,66},{3,67},{4,68},{5,69},{6,70},{7,71},{8,72},{9,... | collective-permute-start | bytes 221192 | tf_op jit(solution)/shard_map/ppermute | solution.py:38
  67.0 4.7 %collective-permute-start.4 = (f32[2,2,2,2,18,128]{5,0,4,1,2,3:T(2,128)S(1)}, f32[2,2,2,2,18,128]{5,0,4,1,2,3:T(2,128)S(1)}, u32[]{:S(2)}, u32[]{:S(2)}) collective-permute-start(f32[2,2,2,2,18,128]{5,0,4,1,2,3:T(2,128)S(1)} %pad_maximum_fusion.10), channel_id=1, source_target_pairs={{0,1},{1,0},{2,3},{3,2},{4,5},{5,4},{6,7},{7,6},{8,9},{9,8},{10,11... | collective-permute-start | bytes 442376 | tf_op jit(solution)/shard_map/ppermute | solution.py:38
  71.9 2.2 %collective-permute-start.8 = (f32[2,2,2,2,18,128]{5,1,4,2,3,0:T(2,128)S(1)}, f32[2,2,2,2,18,128]{5,1,4,2,3,0:T(2,128)S(1)}, u32[]{:S(2)}, u32[]{:S(2)}) collective-permute-start(f32[2,2,2,2,18,128]{5,1,4,2,3,0:T(2,128)S(1)} %pad_maximum_fusion.11), channel_id=1, source_target_pairs={{0,32},{1,33},{2,34},{3,35},{4,36},{5,37},{6,38},{7,39},{8,40},{9,... | collective-permute-start | bytes 442376 | tf_op jit(solution)/shard_map/ppermute | solution.py:38
  74.1 0.4 collective-permute-done.4
  74.5 0.1 select_bitcast_fusion.11
  74.7 0.1 pad_maximum_fusion.6
  74.8 3.2 %collective-permute-start.5 = (f32[2,2,2,2,2,18,128]{6,0,5,1,2,3,4:T(2,128)S(1)}, f32[2,2,2,2,2,18,128]{6,0,5,1,2,3,4:T(2,128)S(1)}, u32[]{:S(2)}, u32[]{:S(2)}) collective-permute-start(f32[2,2,2,2,2,18,128]{6,0,5,1,2,3,4:T(2,128)S(1)} %pad_maximum_fusion.6), channel_id=1, source_target_pairs={{0,64},{1,65},{2,66},{3,67},{4,68},{5,69},{6,70},{7,71},{8,72},{9,... | collective-permute-start | bytes 884744 | tf_op jit(solution)/shard_map/ppermute | solution.py:38
  78.0 0.1 select_bitcast_fusion.9
  78.2 0.1 pad_maximum_fusion.7
  78.3 2.9 %collective-permute-start.9 = (f32[2,2,2,2,2,18,128]{6,2,5,3,4,0,1:T(2,128)S(1)}, f32[2,2,2,2,2,18,128]{6,2,5,3,4,0,1:T(2,128)S(1)}, u32[]{:S(2)}, u32[]{:S(2)}) collective-permute-start(f32[2,2,2,2,2,18,128]{6,2,5,3,4,0,1:T(2,128)S(1)} %pad_maximum_fusion.7), channel_id=1, source_target_pairs={{0,2},{1,3},{2,0},{3,1},{4,6},{5,7},{6,4},{7,5},{8,10},{9,11},{10,... | collective-permute-start | bytes 884744 | tf_op jit(solution)/shard_map/ppermute | solution.py:38
  81.2 3.4 %collective-permute-done.5 = f32[2,2,2,2,2,18,128]{6,0,5,1,2,3,4:T(2,128)S(1)} collective-permute-done((f32[2,2,2,2,2,18,128]{6,0,5,1,2,3,4:T(2,128)S(1)}, f32[2,2,2,2,2,18,128]{6,0,5,1,2,3,4:T(2,128)S(1)}, u32[]{:S(2)}, u32[]{:S(2)}) %collective-permute-start.5) | collective-permute-done | bytes 294944 | tf_op jit(solution)/shard_map/ppermute | solution.py:38
  84.7 0.2 select_bitcast_fusion.7
  84.9 0.3 pad_maximum_fusion.3
  85.2 0.5 copy.80
  85.6 1.9 %collective-permute-start.6 = (f32[2,2,2,2,2,2,18,128]{7,5,6,4,3,2,1,0:T(2,128)S(1)}, f32[2,2,2,2,2,2,18,128]{7,5,6,4,3,2,1,0:T(2,128)S(1)}, u32[]{:S(2)}, u32[]{:S(2)}) collective-permute-start(f32[2,2,2,2,2,2,18,128]{7,5,6,4,3,2,1,0:T(2,128)S(1)} %copy.80), channel_id=1, source_target_pairs={{0,32},{1,33},{2,34},{3,35},{4,36},{5,37},{6,38},{7,39},{8,40},{9,... | collective-permute-start | bytes 1769480 | tf_op jit(solution)/shard_map/ppermute | solution.py:38
  87.6 2.4 %collective-permute-done.9 = f32[2,2,2,2,2,18,128]{6,2,5,3,4,0,1:T(2,128)S(1)} collective-permute-done((f32[2,2,2,2,2,18,128]{6,2,5,3,4,0,1:T(2,128)S(1)}, f32[2,2,2,2,2,18,128]{6,2,5,3,4,0,1:T(2,128)S(1)}, u32[]{:S(2)}, u32[]{:S(2)}) %collective-permute-start.9) | collective-permute-done | bytes 294944 | tf_op jit(solution)/shard_map/ppermute | solution.py:38
  90.0 0.2 select_bitcast_fusion.5
  90.2 0.3 pad_maximum_fusion.4
  90.5 0.5 copy.84
  91.0 5.2 %collective-permute-start.10 = (f32[2,2,2,2,2,2,18,128]{7,5,6,4,3,2,1,0:T(2,128)S(1)}, f32[2,2,2,2,2,2,18,128]{7,5,6,4,3,2,1,0:T(2,128)S(1)}, u32[]{:S(2)}, u32[]{:S(2)}) collective-permute-start(f32[2,2,2,2,2,2,18,128]{7,5,6,4,3,2,1,0:T(2,128)S(1)} %copy.84), channel_id=1, source_target_pairs={{0,1},{1,0},{2,3},{3,2},{4,5},{5,4},{6,7},{7,6},{8,9},{9,8},{10,11... | collective-permute-start | bytes 1769480 | tf_op jit(solution)/shard_map/ppermute | solution.py:38
  96.2 0.5 collective-permute-done.6
  96.7 0.7 select_bitcast_fusion.3
  97.4 0.6 pad_maximum_fusion.1
  98.0 0.9 copy.83
  99.0 6.0 %collective-permute-done.10 = f32[2,2,2,2,2,2,18,128]{7,5,6,4,3,2,1,0:T(2,128)S(1)} collective-permute-done((f32[2,2,2,2,2,2,18,128]{7,5,6,4,3,2,1,0:T(2,128)S(1)}, f32[2,2,2,2,2,2,18,128]{7,5,6,4,3,2,1,0:T(2,128)S(1)}, u32[]{:S(2)}, u32[]{:S(2)}) %collective-permute-start.10) | collective-permute-done | bytes 589856 | tf_op jit(solution)/shard_map/ppermute | solution.py:38
  105.0 0.5 select_bitcast_fusion.1
  105.5 0.6 pad_maximum_fusion.2
  106.1 0.9 copy.87
  107.2 0.7 pad_maximum_fusion.8
  108.0 0.2 copy.90
  108.1 0.1 slice.55
  108.3 0.2 copy.89
  108.5 0.9 reshape.18
  109.4 0.1 pad_maximum_fusion
  109.5 2.3 %copy.88 = f32[128,12,256]{2,1,0:T(8,128)} copy(f32[128,12,256]{2,0,1:T(8,128)S(1)} %pad_maximum_fusion) | data formatting | bytes 3145728 | tf_op jit(solution)/shard_map/concatenate | solution.py:87
  111.8 1.7 %reshape.17 = f32[1536,256]{1,0:T(8,128)S(1)} reshape(f32[128,12,256]{2,1,0:T(8,128)} %copy.88) | data formatting | bytes 3145728 | tf_op jit(solution)/shard_map/reshape | solution.py:87
  113.5 0.3 copy-done
  113.8 2.5 %fusion = f32[256,256]{1,0:T(8,128)S(1)} fusion(f32[1536,256]{1,0:T(8,128)S(1)} %copy-done, f32[1536,256]{1,0:T(8,128)S(1)} %reshape.17), kind=kOutput, calls=%fused_computation.5 | convolution fusion | flops 1209532416 | bytes 3407872 | tf_op jit(solution)/shard_map/dot_general | solution.py:20
  116.4 0.7 fusion.12
  117.0 1.5 convolution_subtract_fusion
  118.5 1.1 copy-done.1
  119.7 7.2 %collective-permute-start.11 = (f32[512,256]{1,0:T(8,128)S(1)}, f32[512,256]{1,0:T(8,128)S(1)}, u32[]{:S(2)}, u32[]{:S(2)}) collective-permute-start(f32[512,256]{1,0:T(8,128)S(1)} %pad_maximum_fusion.5), channel_id=1, source_target_pairs={{0,128},{128,0},{256,384},{384,256},{512,640},{640,512},{768,896},... | collective-permute-start | bytes 1572872 | tf_op jit(solution)/shard_map/ppermute | solution.py:8
  127.0 0.2 copy.91
  127.1 0.1 slice.59
  127.2 6.9 %collective-permute-start.13 = (f32[256,256]{1,0:T(8,128)S(1)}, f32[256,256]{1,0:T(8,128)S(1)}, u32[]{:S(2)}, u32[]{:S(2)}) collective-permute-start(f32[256,256]{1,0:T(8,128)S(1)} %slice.59), channel_id=1, source_target_pairs={{0,256},{128,384},{256,0},{384,128},{512,768},{640,896},{768,512},... | collective-permute-start | bytes 786440 | tf_op jit(solution)/shard_map/ppermute | solution.py:8
  134.1 1.6 %convolution_add_fusion.1 = f32[256,256]{1,0:T(8,128)S(1)} fusion(f32[512,256]{1,0:T(8,128)S(1)} %collective-permute-done.11, pred[]{:T(512)S(6)} %eq.50, f32[256,256]{1,0:T(8,128)S(1)} %slice.55, f32[1536,256]{1,0:T(8,128)} %copy-done.1), kind=kOutput, calls=%fused_computation.11 | convolution fusion | flops 201588736 | bytes 1836544 | tf_op jit(solution)/shard_map/dot_general | solution.py:20
  135.8 0.7 fusion.9
  136.5 1.3 subtract_select_fusion
  137.8 1.9 %collective-permute-start.12 = (f32[256,256]{1,0:T(8,128)S(1)}, f32[256,256]{1,0:T(8,128)S(1)}, u32[]{:S(2)}, u32[]{:S(2)}) collective-permute-start(f32[256,256]{1,0:T(8,128)S(1)} %subtract_select_fusion), channel_id=1, source_target_pairs={{0,256},{128,384},{256,0},{384,128},{512,768},{640,896},{768,512},... | collective-permute-start | bytes 786440 | tf_op jit(solution)/shard_map/ppermute | solution.py:8
  139.8 0.8 collective-permute-done.13
  140.6 6.7 %collective-permute-done.12 = f32[256,256]{1,0:T(8,128)S(1)} collective-permute-done((f32[256,256]{1,0:T(8,128)S(1)}, f32[256,256]{1,0:T(8,128)S(1)}, u32[]{:S(2)}, u32[]{:S(2)}) %collective-permute-start.12) | collective-permute-done | bytes 262176 | tf_op jit(solution)/shard_map/ppermute | solution.py:8
  147.3 0.6 convolution_add_fusion
  147.9 0.7 fusion.6
  148.6 1.1 select_dynamic-update-slice_fusion
  (31 shorter events, 0.8 us)
Async XLA Ops:
  1.4 30.8 %collective-permute-start = (f32[18,256]{1,0:T(8,128)S(1)}, f32[18,256]{1,0:T(8,128)S(1)}, u32[]{:S(2)}, u32[]{:S(2)}) collective-permute-start(f32[18,256]{1,0:T(8,128)S(1)} %pad_maximum_fusion.15), channel_id=1, source_target_pairs={{0,16},{1,17},{2,18},{3,19},{4,20},{5,21},{6,22},{7,23},{8,24},{9,... | collective-permute-start | bytes 55304 | tf_op jit(solution)/shard_map/ppermute | solution.py:38
  33.1 13.4 %collective-permute-start.1 = (f32[2,18,256]{2,0,1:T(2,128)S(1)}, f32[2,18,256]{2,0,1:T(2,128)S(1)}, u32[]{:S(2)}, u32[]{:S(2)}) collective-permute-start(f32[2,18,256]{2,0,1:T(2,128)S(1)} %pad_maximum_fusion.14), channel_id=1, source_target_pairs={{0,8},{1,9},{2,10},{3,11},{4,12},{5,13},{6,14},{7,15},{8,0},{9,1},... | collective-permute-start | bytes 110600 | tf_op jit(solution)/shard_map/ppermute | solution.py:38
  46.6 9.8 %collective-permute-start.2 = (f32[2,2,18,256]{3,0,2,1:T(2,128)S(1)}, f32[2,2,18,256]{3,0,2,1:T(2,128)S(1)}, u32[]{:S(2)}, u32[]{:S(2)}) collective-permute-start(f32[2,2,18,256]{3,0,2,1:T(2,128)S(1)} %pad_maximum_fusion.13), channel_id=1, source_target_pairs={{0,4},{1,5},{2,6},{3,7},{4,0},{5,1},{6,2},{7,3},{8,12},{9,13},{10,... | collective-permute-start | bytes 221192 | tf_op jit(solution)/shard_map/ppermute | solution.py:38
  56.6 10.3 %collective-permute-start.3 = (f32[2,2,2,18,128]{4,0,3,1,2:T(2,128)S(1)}, f32[2,2,2,18,128]{4,0,3,1,2:T(2,128)S(1)}, u32[]{:S(2)}, u32[]{:S(2)}) collective-permute-start(f32[2,2,2,18,128]{4,0,3,1,2:T(2,128)S(1)} %get-tuple-element.21), channel_id=1, source_target_pairs={{0,2},{1,3},{2,0},{3,1},{4,6},{5,7},{6,4},{7,5},{8,10},{9,11},{10,... | collective-permute-start | bytes 221192 | tf_op jit(solution)/shard_map/ppermute | solution.py:38
  60.6 11.2 %collective-permute-start.7 = (f32[2,2,2,18,128]{4,0,3,1,2:T(2,128)S(1)}, f32[2,2,2,18,128]{4,0,3,1,2:T(2,128)S(1)}, u32[]{:S(2)}, u32[]{:S(2)}) collective-permute-start(f32[2,2,2,18,128]{4,0,3,1,2:T(2,128)S(1)} %get-tuple-element.22), channel_id=1, source_target_pairs={{0,64},{1,65},{2,66},{3,67},{4,68},{5,69},{6,70},{7,71},{8,72},{9,... | collective-permute-start | bytes 221192 | tf_op jit(solution)/shard_map/ppermute | solution.py:38
  67.0 7.5 %collective-permute-start.4 = (f32[2,2,2,2,18,128]{5,0,4,1,2,3:T(2,128)S(1)}, f32[2,2,2,2,18,128]{5,0,4,1,2,3:T(2,128)S(1)}, u32[]{:S(2)}, u32[]{:S(2)}) collective-permute-start(f32[2,2,2,2,18,128]{5,0,4,1,2,3:T(2,128)S(1)} %pad_maximum_fusion.10), channel_id=1, source_target_pairs={{0,1},{1,0},{2,3},{3,2},{4,5},{5,4},{6,7},{7,6},{8,9},{9,8},{10,11... | collective-permute-start | bytes 442376 | tf_op jit(solution)/shard_map/ppermute | solution.py:38
  71.9 6.2 %collective-permute-start.8 = (f32[2,2,2,2,18,128]{5,1,4,2,3,0:T(2,128)S(1)}, f32[2,2,2,2,18,128]{5,1,4,2,3,0:T(2,128)S(1)}, u32[]{:S(2)}, u32[]{:S(2)}) collective-permute-start(f32[2,2,2,2,18,128]{5,1,4,2,3,0:T(2,128)S(1)} %pad_maximum_fusion.11), channel_id=1, source_target_pairs={{0,32},{1,33},{2,34},{3,35},{4,36},{5,37},{6,38},{7,39},{8,40},{9,... | collective-permute-start | bytes 442376 | tf_op jit(solution)/shard_map/ppermute | solution.py:38
  74.8 9.9 %collective-permute-start.5 = (f32[2,2,2,2,2,18,128]{6,0,5,1,2,3,4:T(2,128)S(1)}, f32[2,2,2,2,2,18,128]{6,0,5,1,2,3,4:T(2,128)S(1)}, u32[]{:S(2)}, u32[]{:S(2)}) collective-permute-start(f32[2,2,2,2,2,18,128]{6,0,5,1,2,3,4:T(2,128)S(1)} %pad_maximum_fusion.6), channel_id=1, source_target_pairs={{0,64},{1,65},{2,66},{3,67},{4,68},{5,69},{6,70},{7,71},{8,72},{9,... | collective-permute-start | bytes 884744 | tf_op jit(solution)/shard_map/ppermute | solution.py:38
  78.3 11.7 %collective-permute-start.9 = (f32[2,2,2,2,2,18,128]{6,2,5,3,4,0,1:T(2,128)S(1)}, f32[2,2,2,2,2,18,128]{6,2,5,3,4,0,1:T(2,128)S(1)}, u32[]{:S(2)}, u32[]{:S(2)}) collective-permute-start(f32[2,2,2,2,2,18,128]{6,2,5,3,4,0,1:T(2,128)S(1)} %pad_maximum_fusion.7), channel_id=1, source_target_pairs={{0,2},{1,3},{2,0},{3,1},{4,6},{5,7},{6,4},{7,5},{8,10},{9,11},{10,... | collective-permute-start | bytes 884744 | tf_op jit(solution)/shard_map/ppermute | solution.py:38
  85.6 11.0 %collective-permute-start.6 = (f32[2,2,2,2,2,2,18,128]{7,5,6,4,3,2,1,0:T(2,128)S(1)}, f32[2,2,2,2,2,2,18,128]{7,5,6,4,3,2,1,0:T(2,128)S(1)}, u32[]{:S(2)}, u32[]{:S(2)}) collective-permute-start(f32[2,2,2,2,2,2,18,128]{7,5,6,4,3,2,1,0:T(2,128)S(1)} %copy.80), channel_id=1, source_target_pairs={{0,32},{1,33},{2,34},{3,35},{4,36},{5,37},{6,38},{7,39},{8,40},{9,... | collective-permute-start | bytes 1769480 | tf_op jit(solution)/shard_map/ppermute | solution.py:38
  91.0 14.0 %collective-permute-start.10 = (f32[2,2,2,2,2,2,18,128]{7,5,6,4,3,2,1,0:T(2,128)S(1)}, f32[2,2,2,2,2,2,18,128]{7,5,6,4,3,2,1,0:T(2,128)S(1)}, u32[]{:S(2)}, u32[]{:S(2)}) collective-permute-start(f32[2,2,2,2,2,2,18,128]{7,5,6,4,3,2,1,0:T(2,128)S(1)} %copy.84), channel_id=1, source_target_pairs={{0,1},{1,0},{2,3},{3,2},{4,5},{5,4},{6,7},{7,6},{8,9},{9,8},{10,11... | collective-permute-start | bytes 1769480 | tf_op jit(solution)/shard_map/ppermute | solution.py:38
  111.8 2.0 %copy-start = (f32[1536,256]{1,0:T(8,128)S(1)}, f32[1536,256]{1,0:T(8,128)}, u32[]{:S(2)}) copy-start(f32[1536,256]{1,0:T(8,128)} %param.5) | copy-start | bytes 4718596
  113.8 2.6 %copy-start.2 = (f32[256,256]{1,0:T(8,128)S(1)}, f32[256,256]{1,0:T(8,128)}, u32[]{:S(2)}) copy-start(f32[256,256]{1,0:T(8,128)} %reshape.18) | copy-start | bytes 786436
  118.5 1.1 copy-start.1
  119.7 7.3 %copy-start.3 = (f32[64,4,256]{2,0,1:T(8,128)S(1)}, f32[64,4,256]{2,0,1:T(8,128)}, u32[]{:S(2)}) copy-start(f32[64,4,256]{2,0,1:T(8,128)} %get-tuple-element.13) | copy-start | bytes 786436
  119.7 14.4 %collective-permute-start.11 = (f32[512,256]{1,0:T(8,128)S(1)}, f32[512,256]{1,0:T(8,128)S(1)}, u32[]{:S(2)}, u32[]{:S(2)}) collective-permute-start(f32[512,256]{1,0:T(8,128)S(1)} %pad_maximum_fusion.5), channel_id=1, source_target_pairs={{0,128},{128,0},{256,384},{384,256},{512,640},{640,512},{768,896},... | collective-permute-start | bytes 1572872 | tf_op jit(solution)/shard_map/ppermute | solution.py:8
  127.2 13.3 %collective-permute-start.13 = (f32[256,256]{1,0:T(8,128)S(1)}, f32[256,256]{1,0:T(8,128)S(1)}, u32[]{:S(2)}, u32[]{:S(2)}) collective-permute-start(f32[256,256]{1,0:T(8,128)S(1)} %slice.59), channel_id=1, source_target_pairs={{0,256},{128,384},{256,0},{384,128},{512,768},{640,896},{768,512},... | collective-permute-start | bytes 786440 | tf_op jit(solution)/shard_map/ppermute | solution.py:8
  137.8 9.5 %collective-permute-start.12 = (f32[256,256]{1,0:T(8,128)S(1)}, f32[256,256]{1,0:T(8,128)S(1)}, u32[]{:S(2)}, u32[]{:S(2)}) collective-permute-start(f32[256,256]{1,0:T(8,128)S(1)} %subtract_select_fusion), channel_id=1, source_target_pairs={{0,256},{128,384},{256,0},{384,128},{512,768},{640,896},{768,512},... | collective-permute-start | bytes 786440 | tf_op jit(solution)/shard_map/ppermute | solution.py:8

commit v4 on v3

--- a/solution.py
+++ b/solution.py
@@ -76,7 +76,14 @@
     tree_depth = tree_y.shape[0] * n_col // width
     shard_level = col * tree_y.shape[0] // width
     tree_mine = jnp.where((row >> shard_level) & 1 == 0, tree_y, tree_t)
-    packed = jnp.concatenate([leaf_v, leaf_t, tree_mine], axis=0)
+    n_row = lax.axis_size("row")
+    pairs = [
+        (r * n_col + c, (r ^ 1 << (c * tree_y.shape[0] // width)) * n_col + c)
+        for r in range(n_row)
+        for c in range(n_col)
+    ]
+    tree_partner = lax.ppermute(tree_mine, ("row", "col"), pairs)
+    packed = jnp.concatenate([leaf_v, leaf_t, tree_mine, tree_partner], axis=0)
     bits = n_col.bit_length() - 1
     shared = list(range(bits - 3, 1, -1))
     orders = ([1, 0, bits - 1, bits - 2], [bits - 1, bits - 2, 1, 0])
@@ -88,9 +95,11 @@
 
     v_rows = unit_lower(joined(0, nv))
     t_leaf = joined(nv, nv + nt)
-    tree_rows = joined(nv + nt, packed.shape[0])
+    nm = tree_mine.shape[0]
+    tree_rows = joined(nv + nt, nv + nt + nm)
+    tree_rows_partner = joined(nv + nt + nm, packed.shape[0])
     refl = [tree_rows[level * width:(level + 1) * width] for level in range(tree_depth)]
-    partner_refl = [None] + [swapped(refl[level], "row", level) for level in range(1, tree_depth)]
+    partner_refl = [tree_rows_partner[level * width:(level + 1) * width] for level in range(tree_depth)]
     coeffs = inner(jnp.triu(t_leaf), inner(v_rows, trailing))
     updated = trailing - matmul(v_rows, coeffs)
     top_rows = updated[:width]

time: 150 us -> 160 us (1.067)
  waiting for transfers between devices: 31.2 us -> 60.6 us
  starting transfers between devices: 89.5 us -> 65.2 us
  other arithmetic: 7.59 us -> 10.1 us
    ppermute x11, starting transfers between devices: 73.5 us -> 40.2 us  [step(): got = lax.ppermute(buf, axis, [(i, i ^ 1 << bit) for i in range(n)])]
    ppermute x11, waiting for transfers between devices: 23.7 us -> 53.8 us  [step(): got = lax.ppermute(buf, axis, [(i, i ^ 1 << bit) for i in range(n)])]
    ppermute x0 -> x1, starting transfers between devices: none -> 16 us  [local(): tree_partner = lax.ppermute(tree_mine, ('row', 'col'), pairs)]
    ppermute x3 -> x2, starting transfers between devices: 16 us -> 8.92 us  [swapped(): lax.ppermute(shard, axis, [(i, i ^ 1 << stride) for i in range(lax.axis_s...]
    another operation x22, other arithmetic: 5.24 us -> 8.48 us  [step(): jnp.stack([jnp.where(low, buf, got), jnp.where(low, got, buf)], axis=pos)]
    ppermute x3 -> x2, waiting for transfers between devices: 7.51 us -> 5.99 us  [swapped(): lax.ppermute(shard, axis, [(i, i ^ 1 << stride) for i in range(lax.axis_s...]
  transfers between devices with their start and end apart: 14 -> 14, of which waited for: 10 -> 11; matrix products, arithmetic and copies ran while one was open for 6% -> 6% of each run, Pallas kernels for 0% -> 0%
where the time goes in v4:
time: 160 us; the launch traced here: 159 us
  starting transfers between devices  65.2 us (41%)
  waiting for transfers between devices  60.6 us (38%)
  local copies, waits for them, and re-layouts  11.6 us (7%)
  matrix products  10.7 us (7%)
  other arithmetic  10.1 us (6%)
    ppermute x11, waiting for transfers between devices, step(): got = lax.ppermute(buf, axis, [(i, i ^ 1 << bit) for i in range(n)])  53.8 us
    ppermute x11, starting transfers between devices, step(): got = lax.ppermute(buf, axis, [(i, i ^ 1 << bit) for i in range(n)])  40.2 us
    ppermute x1, starting transfers between devices, local(): tree_partner = lax.ppermute(tree_mine, ('row', 'col'), pairs)  16 us
    ppermute x2, starting transfers between devices, swapped(): lax.ppermute(shard, axis, [(i, i ^ 1 << stride) for i in range(lax.axis_s...  8.92 us
    another operation x22, other arithmetic, step(): jnp.stack([jnp.where(low, buf, got), jnp.where(low, got, buf)], axis=pos)  8.48 us
    dot_general x6, matrix products, inner(): lax.dot_general(left, right, (((0,), (0,)), ((), ())), precision=lax.Prec...  6.78 us
    ppermute x2, waiting for transfers between devices, swapped(): lax.ppermute(shard, axis, [(i, i ^ 1 << stride) for i in range(lax.axis_s...  5.99 us
    dot_general x3, matrix products, matmul(): jnp.dot(left, right, precision=lax.Precision.HIGHEST, preferred_element_t...  3.91 us
  transfers between devices with their start and end apart: 14, of which 11 were waited for; matrix products, arithmetic and copies ran while one was open for 6% of the time, Pallas kernels for 0%

profile of v4, /device:TPU:1, one launch (start us, length us, event | category | flops | bytes accessed | tf_op | source)
XLA Modules:
  0.0 158.8 jit_solution(11488755534862441603)
XLA Ops:
  0.0 0.7 broadcast_select_fusion.11
  0.7 16.0 %collective-permute-start = (f32[4,256]{1,0:T(4,128)S(1)}, f32[4,256]{1,0:T(4,128)S(1)}, u32[]{:S(2)}, u32[]{:S(2)}) collective-permute-start(f32[4,256]{1,0:T(4,128)S(1)} %broadcast_select_fusion.11), channel_id=1, source_target_pairs={{0,128},{1,129},{2,130},{3,131},{4,132},{5,133},{6,134},{7,135},{8... | collective-permute-start | bytes 12296 | tf_op jit(solution)/shard_map/ppermute | solution.py:85
  16.7 0.8 collective-permute-done
  17.5 0.7 pad_maximum_fusion.15
  18.3 16.1 %collective-permute-start.1 = (f32[22,256]{1,0:T(8,128)S(1)}, f32[22,256]{1,0:T(8,128)S(1)}, u32[]{:S(2)}, u32[]{:S(2)}) collective-permute-start(f32[22,256]{1,0:T(8,128)S(1)} %pad_maximum_fusion.15), channel_id=1, source_target_pairs={{0,16},{1,17},{2,18},{3,19},{4,20},{5,21},{6,22},{7,23},{8,24},{9,... | collective-permute-start | bytes 67592 | tf_op jit(solution)/shard_map/ppermute | solution.py:38
  34.3 6.8 %collective-permute-done.1 = f32[22,256]{1,0:T(8,128)S(1)} collective-permute-done((f32[22,256]{1,0:T(8,128)S(1)}, f32[22,256]{1,0:T(8,128)S(1)}, u32[]{:S(2)}, u32[]{:S(2)}) %collective-permute-start.1) | collective-permute-done | bytes 22560 | tf_op jit(solution)/shard_map/ppermute | solution.py:38
  41.2 0.7 select_bitcast_fusion.20
  42.0 3.4 %collective-permute-start.2 = (f32[2,22,256]{2,0,1:T(2,128)S(1)}, f32[2,22,256]{2,0,1:T(2,128)S(1)}, u32[]{:S(2)}, u32[]{:S(2)}) collective-permute-start(f32[2,22,256]{2,0,1:T(2,128)S(1)} %pad_maximum_fusion.14), channel_id=1, source_target_pairs={{0,8},{1,9},{2,10},{3,11},{4,12},{5,13},{6,14},{7,15},{8,0},{9,1},... | collective-permute-start | bytes 135176 | tf_op jit(solution)/shard_map/ppermute | solution.py:38
  45.4 10.1 %collective-permute-done.2 = f32[2,22,256]{2,0,1:T(2,128)S(1)} collective-permute-done((f32[2,22,256]{2,0,1:T(2,128)S(1)}, f32[2,22,256]{2,0,1:T(2,128)S(1)}, u32[]{:S(2)}, u32[]{:S(2)}) %collective-permute-start.2) | collective-permute-done | bytes 45088 | tf_op jit(solution)/shard_map/ppermute | solution.py:38
  55.6 1.9 %collective-permute-start.3 = (f32[2,2,22,256]{3,0,2,1:T(2,128)S(1)}, f32[2,2,22,256]{3,0,2,1:T(2,128)S(1)}, u32[]{:S(2)}, u32[]{:S(2)}) collective-permute-start(f32[2,2,22,256]{3,0,2,1:T(2,128)S(1)} %pad_maximum_fusion.13), channel_id=1, source_target_pairs={{0,4},{1,5},{2,6},{3,7},{4,0},{5,1},{6,2},{7,3},{8,12},{9,13},{10,... | collective-permute-start | bytes 270344 | tf_op jit(solution)/shard_map/ppermute | solution.py:38
  57.6 9.7 %collective-permute-done.3 = f32[2,2,22,256]{3,0,2,1:T(2,128)S(1)} collective-permute-done((f32[2,2,22,256]{3,0,2,1:T(2,128)S(1)}, f32[2,2,22,256]{3,0,2,1:T(2,128)S(1)}, u32[]{:S(2)}, u32[]{:S(2)}) %collective-permute-start.3) | collective-permute-done | bytes 90144 | tf_op jit(solution)/shard_map/ppermute | solution.py:38
  67.5 1.9 %collective-permute-start.4 = (f32[2,2,2,22,128]{4,0,3,1,2:T(2,128)S(1)}, f32[2,2,2,22,128]{4,0,3,1,2:T(2,128)S(1)}, u32[]{:S(2)}, u32[]{:S(2)}) collective-permute-start(f32[2,2,2,22,128]{4,0,3,1,2:T(2,128)S(1)} %get-tuple-element.27), channel_id=1, source_target_pairs={{0,2},{1,3},{2,0},{3,1},{4,6},{5,7},{6,4},{7,5},{8,10},{9,11},{10,... | collective-permute-start | bytes 270344 | tf_op jit(solution)/shard_map/ppermute | solution.py:38
  69.4 1.9 %collective-permute-start.8 = (f32[2,2,2,22,128]{4,0,3,1,2:T(2,128)S(1)}, f32[2,2,2,22,128]{4,0,3,1,2:T(2,128)S(1)}, u32[]{:S(2)}, u32[]{:S(2)}) collective-permute-start(f32[2,2,2,22,128]{4,0,3,1,2:T(2,128)S(1)} %get-tuple-element.28), channel_id=1, source_target_pairs={{0,64},{1,65},{2,66},{3,67},{4,68},{5,69},{6,70},{7,71},{8,72},{9,... | collective-permute-start | bytes 270344 | tf_op jit(solution)/shard_map/ppermute | solution.py:38
  71.3 3.4 %collective-permute-done.4 = f32[2,2,2,22,128]{4,0,3,1,2:T(2,128)S(1)} collective-permute-done((f32[2,2,2,22,128]{4,0,3,1,2:T(2,128)S(1)}, f32[2,2,2,22,128]{4,0,3,1,2:T(2,128)S(1)}, u32[]{:S(2)}, u32[]{:S(2)}) %collective-permute-start.4) | collective-permute-done | bytes 90144 | tf_op jit(solution)/shard_map/ppermute | solution.py:38
  74.9 1.9 %collective-permute-start.5 = (f32[2,2,2,2,22,128]{5,0,4,1,2,3:T(2,128)S(1)}, f32[2,2,2,2,22,128]{5,0,4,1,2,3:T(2,128)S(1)}, u32[]{:S(2)}, u32[]{:S(2)}) collective-permute-start(f32[2,2,2,2,22,128]{5,0,4,1,2,3:T(2,128)S(1)} %pad_maximum_fusion.10), channel_id=1, source_target_pairs={{0,1},{1,0},{2,3},{3,2},{4,5},{5,4},{6,7},{7,6},{8,9},{9,8},{10,11... | collective-permute-start | bytes 540680 | tf_op jit(solution)/shard_map/ppermute | solution.py:38
  77.0 2.5 %collective-permute-start.9 = (f32[2,2,2,2,22,128]{5,1,4,2,3,0:T(2,128)S(1)}, f32[2,2,2,2,22,128]{5,1,4,2,3,0:T(2,128)S(1)}, u32[]{:S(2)}, u32[]{:S(2)}) collective-permute-start(f32[2,2,2,2,22,128]{5,1,4,2,3,0:T(2,128)S(1)} %pad_maximum_fusion.11), channel_id=1, source_target_pairs={{0,32},{1,33},{2,34},{3,35},{4,36},{5,37},{6,38},{7,39},{8,40},{9,... | collective-permute-start | bytes 540680 | tf_op jit(solution)/shard_map/ppermute | solution.py:38
  79.5 1.7 %collective-permute-done.5 = f32[2,2,2,2,22,128]{5,0,4,1,2,3:T(2,128)S(1)} collective-permute-done((f32[2,2,2,2,22,128]{5,0,4,1,2,3:T(2,128)S(1)}, f32[2,2,2,2,22,128]{5,0,4,1,2,3:T(2,128)S(1)}, u32[]{:S(2)}, u32[]{:S(2)}) %collective-permute-start.5) | collective-permute-done | bytes 180256 | tf_op jit(solution)/shard_map/ppermute | solution.py:38
  81.1 0.2 select_bitcast_fusion.11
  81.3 0.2 pad_maximum_fusion.5
  81.5 2.8 %collective-permute-start.6 = (f32[2,2,2,2,2,22,128]{6,0,5,1,2,3,4:T(2,128)S(1)}, f32[2,2,2,2,2,22,128]{6,0,5,1,2,3,4:T(2,128)S(1)}, u32[]{:S(2)}, u32[]{:S(2)}) collective-permute-start(f32[2,2,2,2,2,22,128]{6,0,5,1,2,3,4:T(2,128)S(1)} %pad_maximum_fusion.5), channel_id=1, source_target_pairs={{0,64},{1,65},{2,66},{3,67},{4,68},{5,69},{6,70},{7,71},{8,72},{9,... | collective-permute-start | bytes 1081352 | tf_op jit(solution)/shard_map/ppermute | solution.py:38
  84.3 0.2 select_bitcast_fusion.9
  84.4 0.2 pad_maximum_fusion.6
  84.6 3.8 %collective-permute-start.10 = (f32[2,2,2,2,2,22,128]{6,2,5,3,4,0,1:T(2,128)S(1)}, f32[2,2,2,2,2,22,128]{6,2,5,3,4,0,1:T(2,128)S(1)}, u32[]{:S(2)}, u32[]{:S(2)}) collective-permute-start(f32[2,2,2,2,2,22,128]{6,2,5,3,4,0,1:T(2,128)S(1)} %pad_maximum_fusion.6), channel_id=1, source_target_pairs={{0,2},{1,3},{2,0},{3,1},{4,6},{5,7},{6,4},{7,5},{8,10},{9,11},{10,... | collective-permute-start | bytes 1081352 | tf_op jit(solution)/shard_map/ppermute | solution.py:38
  88.5 6.5 %collective-permute-done.6 = f32[2,2,2,2,2,22,128]{6,0,5,1,2,3,4:T(2,128)S(1)} collective-permute-done((f32[2,2,2,2,2,22,128]{6,0,5,1,2,3,4:T(2,128)S(1)}, f32[2,2,2,2,2,22,128]{6,0,5,1,2,3,4:T(2,128)S(1)}, u32[]{:S(2)}, u32[]{:S(2)}) %collective-permute-start.6) | collective-permute-done | bytes 360480 | tf_op jit(solution)/shard_map/ppermute | solution.py:38
  95.0 0.3 select_bitcast_fusion.7
  95.3 0.3 pad_maximum_fusion.3
  95.6 0.6 copy.93
  96.2 1.9 %collective-permute-start.7 = (f32[2,2,2,2,2,2,22,128]{7,5,6,4,3,2,1,0:T(2,128)S(1)}, f32[2,2,2,2,2,2,22,128]{7,5,6,4,3,2,1,0:T(2,128)}, u32[]{:S(2)}, u32[]{:S(2)}) collective-permute-start(f32[2,2,2,2,2,2,22,128]{7,5,6,4,3,2,1,0:T(2,128)S(1)} %copy.93), channel_id=1, source_target_pairs={{0,32},{1,33},{2,34},{3,35},{4,36},{5,37},{6,38},{7,39},{8,40},{9,... | collective-permute-start | bytes 2162696 | tf_op jit(solution)/shard_map/ppermute | solution.py:38
  98.1 4.9 %collective-permute-done.10 = f32[2,2,2,2,2,22,128]{6,2,5,3,4,0,1:T(2,128)S(1)} collective-permute-done((f32[2,2,2,2,2,22,128]{6,2,5,3,4,0,1:T(2,128)S(1)}, f32[2,2,2,2,2,22,128]{6,2,5,3,4,0,1:T(2,128)S(1)}, u32[]{:S(2)}, u32[]{:S(2)}) %collective-permute-start.10) | collective-permute-done | bytes 360480 | tf_op jit(solution)/shard_map/ppermute | solution.py:38
  103.0 0.3 select_bitcast_fusion.5
  103.3 0.3 pad_maximum_fusion.4
  103.6 0.6 copy.97
  104.2 2.1 %collective-permute-start.11 = (f32[2,2,2,2,2,2,22,128]{7,5,6,4,3,2,1,0:T(2,128)S(1)}, f32[2,2,2,2,2,2,22,128]{7,5,6,4,3,2,1,0:T(2,128)}, u32[]{:S(2)}, u32[]{:S(2)}) collective-permute-start(f32[2,2,2,2,2,2,22,128]{7,5,6,4,3,2,1,0:T(2,128)S(1)} %copy.97), channel_id=1, source_target_pairs={{0,1},{1,0},{2,3},{3,2},{4,5},{5,4},{6,7},{7,6},{8,9},{9,8},{10,11... | collective-permute-start | bytes 2162696 | tf_op jit(solution)/shard_map/ppermute | solution.py:38
  106.3 7.0 %collective-permute-done.7 = f32[2,2,2,2,2,2,22,128]{7,5,6,4,3,2,1,0:T(2,128)} collective-permute-done((f32[2,2,2,2,2,2,22,128]{7,5,6,4,3,2,1,0:T(2,128)S(1)}, f32[2,2,2,2,2,2,22,128]{7,5,6,4,3,2,1,0:T(2,128)}, u32[]{:S(2)}, u32[]{:S(2)}) %collective-permute-start.7) | collective-permute-done | bytes 720928 | tf_op jit(solution)/shard_map/ppermute | solution.py:38
  113.3 2.0 %select_bitcast_fusion.3 = (f32[2,1,2,2,2,2,2,22,128]{8,2,7,3,4,5,6,0,1:T(2,128)S(1)}, f32[2,1,2,2,2,2,2,22,128]{8,2,7,3,4,5,6,0,1:T(2,128)S(1)}) fusion(pred[]{:T(512)S(6)} %eq.41, f32[2,2,2,2,2,2,22,128]{7,5,6,4,3,2,1,0:T(2,128)} %collective-permute-done.7, f32[1,2,2,2,2,2,22,128]{7,1,6,2,3,4,5,0:T(2,128)S(1)} %get-tuple-element.18, ...), kind=kLoop, calls=%fused_computation.21 | loop fusion | flops 540672 | bytes 2883585 | tf_op jit(solution)/shard_map/stack | solution.py:41
  115.3 0.7 pad_maximum_fusion.1
  116.1 1.1 copy.96
  117.3 3.6 %collective-permute-done.11 = f32[2,2,2,2,2,2,22,128]{7,5,6,4,3,2,1,0:T(2,128)} collective-permute-done((f32[2,2,2,2,2,2,22,128]{7,5,6,4,3,2,1,0:T(2,128)S(1)}, f32[2,2,2,2,2,2,22,128]{7,5,6,4,3,2,1,0:T(2,128)}, u32[]{:S(2)}, u32[]{:S(2)}) %collective-permute-start.11) | collective-permute-done | bytes 720928 | tf_op jit(solution)/shard_map/ppermute | solution.py:38
  120.9 1.8 %select_bitcast_fusion.1 = (f32[2,2,2,2,2,2,1,22,128]{8,2,7,3,4,0,1,5,6:T(2,128)S(1)}, f32[2,2,2,2,2,2,1,22,128]{8,2,7,3,4,0,1,5,6:T(2,128)S(1)}) fusion(pred[]{:T(512)S(6)} %eq.43, f32[2,2,2,2,2,2,22,128]{7,5,6,4,3,2,1,0:T(2,128)} %collective-permute-done.11, f32[2,2,2,2,2,1,22,128]{7,2,6,3,4,0,1,5:T(2,128)S(1)} %get-tuple-element.20, ...), kind=kLoop, calls=%fused_computation.19 | loop fusion | flops 540672 | bytes 2883585 | tf_op jit(solution)/shard_map/stack | solution.py:41
  122.7 0.7 pad_maximum_fusion.2
  123.5 1.1 copy.100
  124.6 1.1 copy-done.2
  125.8 0.2 copy.102
  126.0 0.2 reshape.29
  126.3 2.3 %copy.101 = f32[128,12,256]{2,1,0:T(8,128)} copy(f32[128,12,256]{2,0,1:T(8,128)S(1)} %pad_maximum_fusion) | data formatting | bytes 3145728 | tf_op jit(solution)/shard_map/concatenate | solution.py:94
  128.6 1.7 %reshape.28 = f32[1536,256]{1,0:T(8,128)S(1)} reshape(f32[128,12,256]{2,1,0:T(8,128)} %copy.101) | data formatting | bytes 3145728 | tf_op jit(solution)/shard_map/reshape | solution.py:94
  130.3 0.3 copy-done
  130.6 2.5 %fusion = f32[256,256]{1,0:T(8,128)S(1)} fusion(f32[1536,256]{1,0:T(8,128)S(1)} %copy-done, f32[1536,256]{1,0:T(8,128)S(1)} %reshape.28), kind=kOutput, calls=%fused_computation.7 | convolution fusion | flops 1209532416 | bytes 3407872 | tf_op jit(solution)/shard_map/dot_general | solution.py:20
  133.2 0.7 fusion.11
  133.9 1.5 convolution_subtract_fusion
  135.4 5.7 %collective-permute-start.12 = (f32[256,256]{1,0:T(8,128)S(1)}, f32[256,256]{1,0:T(8,128)S(1)}, u32[]{:S(2)}, u32[]{:S(2)}) collective-permute-start(f32[256,256]{1,0:T(8,128)S(1)} %slice.70), channel_id=1, source_target_pairs={{0,128},{128,0},{256,384},{384,256},{512,640},{640,512},{768,896},... | collective-permute-start | bytes 786440 | tf_op jit(solution)/shard_map/ppermute | solution.py:8
  141.1 1.3 fusion.28
  142.5 0.2 copy.104
  142.7 0.2 copy.103
  143.0 1.6 %convolution_add_fusion.1 = f32[256,256]{1,0:T(8,128)S(1)} fusion(f32[256,256]{1,0:T(8,128)S(1)} %select_n.280, f32[256,256]{1,0:T(8,128)S(1)} %collective-permute-done.12, pred[]{:T(512)S(6)} %eq.50, f32[1536,256]{1,0:T(8,128)} %copy-done.3), kind=kOutput, calls=%fused_computation.11 | convolution fusion | flops 201523200 | bytes 1573888 | tf_op jit(solution)/shard_map/dot_general | solution.py:20
  144.7 0.7 fusion.9
  145.3 1.3 subtract_select_fusion
  146.7 3.2 %collective-permute-start.13 = (f32[256,256]{1,0:T(8,128)S(1)}, f32[256,256]{1,0:T(8,128)S(1)}, u32[]{:S(2)}, u32[]{:S(2)}) collective-permute-start(f32[256,256]{1,0:T(8,128)S(1)} %subtract_select_fusion), channel_id=1, source_target_pairs={{0,256},{128,384},{256,0},{384,128},{512,768},{640,896},{768,512},... | collective-permute-start | bytes 786440 | tf_op jit(solution)/shard_map/ppermute | solution.py:8
  149.9 0.2 copy.106
  150.2 0.2 copy.105
  150.5 6.0 %collective-permute-done.13 = f32[256,256]{1,0:T(8,128)S(1)} collective-permute-done((f32[256,256]{1,0:T(8,128)S(1)}, f32[256,256]{1,0:T(8,128)S(1)}, u32[]{:S(2)}, u32[]{:S(2)}) %collective-permute-start.13) | collective-permute-done | bytes 262176 | tf_op jit(solution)/shard_map/ppermute | solution.py:8
  156.4 0.6 convolution_add_fusion
  157.1 0.7 fusion.7
  157.7 1.1 select_dynamic-update-slice_fusion
  (33 shorter events, 1.4 us)
Async XLA Ops:
  0.7 16.8 %collective-permute-start = (f32[4,256]{1,0:T(4,128)S(1)}, f32[4,256]{1,0:T(4,128)S(1)}, u32[]{:S(2)}, u32[]{:S(2)}) collective-permute-start(f32[4,256]{1,0:T(4,128)S(1)} %broadcast_select_fusion.11), channel_id=1, source_target_pairs={{0,128},{1,129},{2,130},{3,131},{4,132},{5,133},{6,134},{7,135},{8... | collective-permute-start | bytes 12296 | tf_op jit(solution)/shard_map/ppermute | solution.py:85
  18.3 22.9 %collective-permute-start.1 = (f32[22,256]{1,0:T(8,128)S(1)}, f32[22,256]{1,0:T(8,128)S(1)}, u32[]{:S(2)}, u32[]{:S(2)}) collective-permute-start(f32[22,256]{1,0:T(8,128)S(1)} %pad_maximum_fusion.15), channel_id=1, source_target_pairs={{0,16},{1,17},{2,18},{3,19},{4,20},{5,21},{6,22},{7,23},{8,24},{9,... | collective-permute-start | bytes 67592 | tf_op jit(solution)/shard_map/ppermute | solution.py:38
  42.0 13.5 %collective-permute-start.2 = (f32[2,22,256]{2,0,1:T(2,128)S(1)}, f32[2,22,256]{2,0,1:T(2,128)S(1)}, u32[]{:S(2)}, u32[]{:S(2)}) collective-permute-start(f32[2,22,256]{2,0,1:T(2,128)S(1)} %pad_maximum_fusion.14), channel_id=1, source_target_pairs={{0,8},{1,9},{2,10},{3,11},{4,12},{5,13},{6,14},{7,15},{8,0},{9,1},... | collective-permute-start | bytes 135176 | tf_op jit(solution)/shard_map/ppermute | solution.py:38
  55.6 11.7 %collective-permute-start.3 = (f32[2,2,22,256]{3,0,2,1:T(2,128)S(1)}, f32[2,2,22,256]{3,0,2,1:T(2,128)S(1)}, u32[]{:S(2)}, u32[]{:S(2)}) collective-permute-start(f32[2,2,22,256]{3,0,2,1:T(2,128)S(1)} %pad_maximum_fusion.13), channel_id=1, source_target_pairs={{0,4},{1,5},{2,6},{3,7},{4,0},{5,1},{6,2},{7,3},{8,12},{9,13},{10,... | collective-permute-start | bytes 270344 | tf_op jit(solution)/shard_map/ppermute | solution.py:38
  67.5 7.3 %collective-permute-start.4 = (f32[2,2,2,22,128]{4,0,3,1,2:T(2,128)S(1)}, f32[2,2,2,22,128]{4,0,3,1,2:T(2,128)S(1)}, u32[]{:S(2)}, u32[]{:S(2)}) collective-permute-start(f32[2,2,2,22,128]{4,0,3,1,2:T(2,128)S(1)} %get-tuple-element.27), channel_id=1, source_target_pairs={{0,2},{1,3},{2,0},{3,1},{4,6},{5,7},{6,4},{7,5},{8,10},{9,11},{10,... | collective-permute-start | bytes 270344 | tf_op jit(solution)/shard_map/ppermute | solution.py:38
  69.4 7.4 %collective-permute-start.8 = (f32[2,2,2,22,128]{4,0,3,1,2:T(2,128)S(1)}, f32[2,2,2,22,128]{4,0,3,1,2:T(2,128)S(1)}, u32[]{:S(2)}, u32[]{:S(2)}) collective-permute-start(f32[2,2,2,22,128]{4,0,3,1,2:T(2,128)S(1)} %get-tuple-element.28), channel_id=1, source_target_pairs={{0,64},{1,65},{2,66},{3,67},{4,68},{5,69},{6,70},{7,71},{8,72},{9,... | collective-permute-start | bytes 270344 | tf_op jit(solution)/shard_map/ppermute | solution.py:38
  74.9 6.2 %collective-permute-start.5 = (f32[2,2,2,2,22,128]{5,0,4,1,2,3:T(2,128)S(1)}, f32[2,2,2,2,22,128]{5,0,4,1,2,3:T(2,128)S(1)}, u32[]{:S(2)}, u32[]{:S(2)}) collective-permute-start(f32[2,2,2,2,22,128]{5,0,4,1,2,3:T(2,128)S(1)} %pad_maximum_fusion.10), channel_id=1, source_target_pairs={{0,1},{1,0},{2,3},{3,2},{4,5},{5,4},{6,7},{7,6},{8,9},{9,8},{10,11... | collective-permute-start | bytes 540680 | tf_op jit(solution)/shard_map/ppermute | solution.py:38
  77.0 7.3 %collective-permute-start.9 = (f32[2,2,2,2,22,128]{5,1,4,2,3,0:T(2,128)S(1)}, f32[2,2,2,2,22,128]{5,1,4,2,3,0:T(2,128)S(1)}, u32[]{:S(2)}, u32[]{:S(2)}) collective-permute-start(f32[2,2,2,2,22,128]{5,1,4,2,3,0:T(2,128)S(1)} %pad_maximum_fusion.11), channel_id=1, source_target_pairs={{0,32},{1,33},{2,34},{3,35},{4,36},{5,37},{6,38},{7,39},{8,40},{9,... | collective-permute-start | bytes 540680 | tf_op jit(solution)/shard_map/ppermute | solution.py:38
  81.5 13.5 %collective-permute-start.6 = (f32[2,2,2,2,2,22,128]{6,0,5,1,2,3,4:T(2,128)S(1)}, f32[2,2,2,2,2,22,128]{6,0,5,1,2,3,4:T(2,128)S(1)}, u32[]{:S(2)}, u32[]{:S(2)}) collective-permute-start(f32[2,2,2,2,2,22,128]{6,0,5,1,2,3,4:T(2,128)S(1)} %pad_maximum_fusion.5), channel_id=1, source_target_pairs={{0,64},{1,65},{2,66},{3,67},{4,68},{5,69},{6,70},{7,71},{8,72},{9,... | collective-permute-start | bytes 1081352 | tf_op jit(solution)/shard_map/ppermute | solution.py:38
  84.6 18.4 %collective-permute-start.10 = (f32[2,2,2,2,2,22,128]{6,2,5,3,4,0,1:T(2,128)S(1)}, f32[2,2,2,2,2,22,128]{6,2,5,3,4,0,1:T(2,128)S(1)}, u32[]{:S(2)}, u32[]{:S(2)}) collective-permute-start(f32[2,2,2,2,2,22,128]{6,2,5,3,4,0,1:T(2,128)S(1)} %pad_maximum_fusion.6), channel_id=1, source_target_pairs={{0,2},{1,3},{2,0},{3,1},{4,6},{5,7},{6,4},{7,5},{8,10},{9,11},{10,... | collective-permute-start | bytes 1081352 | tf_op jit(solution)/shard_map/ppermute | solution.py:38
  96.2 17.1 %collective-permute-start.7 = (f32[2,2,2,2,2,2,22,128]{7,5,6,4,3,2,1,0:T(2,128)S(1)}, f32[2,2,2,2,2,2,22,128]{7,5,6,4,3,2,1,0:T(2,128)}, u32[]{:S(2)}, u32[]{:S(2)}) collective-permute-start(f32[2,2,2,2,2,2,22,128]{7,5,6,4,3,2,1,0:T(2,128)S(1)} %copy.93), channel_id=1, source_target_pairs={{0,32},{1,33},{2,34},{3,35},{4,36},{5,37},{6,38},{7,39},{8,40},{9,... | collective-permute-start | bytes 2162696 | tf_op jit(solution)/shard_map/ppermute | solution.py:38
  104.2 16.7 %collective-permute-start.11 = (f32[2,2,2,2,2,2,22,128]{7,5,6,4,3,2,1,0:T(2,128)S(1)}, f32[2,2,2,2,2,2,22,128]{7,5,6,4,3,2,1,0:T(2,128)}, u32[]{:S(2)}, u32[]{:S(2)}) collective-permute-start(f32[2,2,2,2,2,2,22,128]{7,5,6,4,3,2,1,0:T(2,128)S(1)} %copy.97), channel_id=1, source_target_pairs={{0,1},{1,0},{2,3},{3,2},{4,5},{5,4},{6,7},{7,6},{8,9},{9,8},{10,11... | collective-permute-start | bytes 2162696 | tf_op jit(solution)/shard_map/ppermute | solution.py:38
  117.2 5.5 %copy-start.1 = (f32[2,2,2,2,2,2,2,22,128]{8,6,5,4,3,2,1,0,7:T(2,128)}, f32[2,2,2,2,2,2,2,22,128]{8,6,5,4,3,2,1,0,7:T(2,128)S(1)}, u32[]{:S(2)}) copy-start(f32[2,2,2,2,2,2,2,22,128]{8,6,5,4,3,2,1,0,7:T(2,128)S(1)} %copy.96) | copy-start | bytes 4325380
  124.6 1.1 copy-start.2
  128.6 2.0 %copy-start = (f32[1536,256]{1,0:T(8,128)S(1)}, f32[1536,256]{1,0:T(8,128)}, u32[]{:S(2)}) copy-start(f32[1536,256]{1,0:T(8,128)} %param.5) | copy-start | bytes 4718596
  135.3 7.1 %copy-start.3 = (f32[1536,256]{1,0:T(8,128)}, f32[1536,256]{1,0:T(8,128)S(1)}, u32[]{:S(2)}) copy-start(f32[1536,256]{1,0:T(8,128)S(1)} %convolution_subtract_fusion) | copy-start | bytes 4718596
  135.4 7.7 %collective-permute-start.12 = (f32[256,256]{1,0:T(8,128)S(1)}, f32[256,256]{1,0:T(8,128)S(1)}, u32[]{:S(2)}, u32[]{:S(2)}) collective-permute-start(f32[256,256]{1,0:T(8,128)S(1)} %slice.70), channel_id=1, source_target_pairs={{0,128},{128,0},{256,384},{384,256},{512,640},{640,512},{768,896},... | collective-permute-start | bytes 786440 | tf_op jit(solution)/shard_map/ppermute | solution.py:8
  146.7 9.7 %collective-permute-start.13 = (f32[256,256]{1,0:T(8,128)S(1)}, f32[256,256]{1,0:T(8,128)S(1)}, u32[]{:S(2)}, u32[]{:S(2)}) collective-permute-start(f32[256,256]{1,0:T(8,128)S(1)} %subtract_select_fusion), channel_id=1, source_target_pairs={{0,256},{128,384},{256,0},{384,128},{512,768},{640,896},{768,512},... | collective-permute-start | bytes 786440 | tf_op jit(solution)/shard_map/ppermute | solution.py:8

commit v5 on v3

--- a/solution.py
+++ b/solution.py
@@ -1,3 +1,5 @@
+import functools
+
 import jax
 import jax.numpy as jnp
 from jax import lax
@@ -30,12 +32,13 @@
     return jnp.dot(left, right, precision=lax.Precision.HIGHEST, preferred_element_type=jnp.float32)
 
 
-def doubling_gather(shard, axis, shared, orders):
+def doubling_gather(shard, axis, label, shared, orders):
     n = lax.axis_size(axis)
-    me = lax.axis_index(axis)
+    unlabel = {label(i): i for i in range(n)}
+    me = label(lax.axis_index(axis))
 
     def step(buf, held, bit):
-        got = lax.ppermute(buf, axis, [(i, i ^ 1 << bit) for i in range(n)])
+        got = lax.ppermute(buf, axis, [(i, unlabel[label(i) ^ 1 << bit]) for i in range(n)])
         low = (me >> bit) & 1 == 0
         pos = sum(1 for b in held if b > bit)
         return jnp.stack([jnp.where(low, buf, got), jnp.where(low, got, buf)], axis=pos), held[:pos] + [bit] + held[pos:]
@@ -68,7 +71,7 @@
     return jnp.where(lower_side, lower_top - coeffs, upper_top - matmul(refl_y, coeffs))
 
 
-def local(trailing, leaf_v, leaf_t, tree_y, tree_t):
+def local(z_len, trailing, leaf_v, leaf_t, tree_y, tree_t):
     width = leaf_v.shape[1]
     n_col = lax.axis_size("col")
     col = lax.axis_index("col")
@@ -78,13 +81,25 @@
     tree_mine = jnp.where((row >> shard_level) & 1 == 0, tree_y, tree_t)
     packed = jnp.concatenate([leaf_v, leaf_t, tree_mine], axis=0)
     bits = n_col.bit_length() - 1
-    shared = list(range(bits - 3, 1, -1))
-    orders = ([1, 0, bits - 1, bits - 2], [bits - 1, bits - 2, 1, 0])
-    pieces = doubling_gather(packed, "col", shared, orders)
+    z_bits = z_len.bit_length() - 1
+    n_x = n_col // z_len
+
+    def label(i):
+        x = i >> z_bits
+        return (x ^ x >> 1) << z_bits | i & (z_len - 1)
+
+    shared = list(range(z_bits - 1, 0, -1))
+    orders = ([0] + list(range(bits - 1, z_bits - 1, -1)), list(range(bits - 1, z_bits - 1, -1)) + [0])
+    pieces = doubling_gather(packed, "col", label, shared, orders)
     nv, nt = leaf_v.shape[0], leaf_t.shape[0]
+    x_order = [x ^ x >> 1 for x in range(n_x)]
 
     def joined(lo, hi):
-        return jnp.concatenate([p[:, lo:hi] for p in pieces], axis=2).reshape(-1, width)
+        parts = []
+        for p in pieces:
+            groups = p[:, lo:hi].reshape(n_x, z_len, hi - lo, p.shape[2])
+            parts.append(jnp.concatenate([groups[g][None] for g in x_order], axis=0))
+        return jnp.concatenate(parts, axis=3).reshape(-1, width)
 
     v_rows = unit_lower(joined(0, nv))
     t_leaf = joined(nv, nv + nt)
@@ -108,4 +123,5 @@
         P(("row", "col"), None),
     )
     out_specs = P("row", "col")
-    return jax.shard_map(local, mesh=mesh, in_specs=in_specs, out_specs=out_specs, check_vma=False)
+    z_len = len({d.coords[2] for d in mesh.devices[0].flat})
+    return jax.shard_map(functools.partial(local, z_len), mesh=mesh, in_specs=in_specs, out_specs=out_specs, check_vma=False)

time: 150 us -> 146 us (0.973)
  starting transfers between devices: 89.5 us -> 77.6 us
  waiting for transfers between devices: 31.2 us -> 38.4 us
    ppermute x11 -> x10, waiting for transfers between devices: 23.7 us -> 32.1 us  [step(): lax.ppermute(buf, axis, [(i, unlabel[label(i) ^ 1 << bit]) for i in range...]
    ppermute x11 -> x10, starting transfers between devices: 73.5 us -> 66.6 us  [step(): lax.ppermute(buf, axis, [(i, unlabel[label(i) ^ 1 << bit]) for i in range...]
    ppermute x3, starting transfers between devices: 16 us -> 11 us  [swapped(): lax.ppermute(shard, axis, [(i, i ^ 1 << stride) for i in range(lax.axis_s...]
    another operation x22 -> x20, other arithmetic: 5.24 us -> 5.22 us  [step(): jnp.stack([jnp.where(low, buf, got), jnp.where(low, got, buf)], axis=pos)]
  transfers between devices with their start and end apart: 14 -> 13, of which waited for: 10 -> 8; matrix products, arithmetic and copies ran while one was open for 6% -> 6% of each run, Pallas kernels for 0% -> 0%
where the time goes in v5:
time: 146 us; the launch traced here: 145 us
  starting transfers between devices  77.6 us (53%)
  waiting for transfers between devices  38.4 us (26%)
  local copies, waits for them, and re-layouts  10.7 us (7%)
  matrix products  10.7 us (7%)
  other arithmetic  6.87 us (5%)
    ppermute x10, starting transfers between devices, step(): lax.ppermute(buf, axis, [(i, unlabel[label(i) ^ 1 << bit]) for i in range...  66.6 us
    ppermute x10, waiting for transfers between devices, step(): lax.ppermute(buf, axis, [(i, unlabel[label(i) ^ 1 << bit]) for i in range...  32.1 us
    ppermute x3, starting transfers between devices, swapped(): lax.ppermute(shard, axis, [(i, i ^ 1 << stride) for i in range(lax.axis_s...  11 us
    dot_general x6, matrix products, inner(): lax.dot_general(left, right, (((0,), (0,)), ((), ())), precision=lax.Prec...  6.78 us
    ppermute x3, waiting for transfers between devices, swapped(): lax.ppermute(shard, axis, [(i, i ^ 1 << stride) for i in range(lax.axis_s...  6.36 us
    another operation x20, other arithmetic, step(): jnp.stack([jnp.where(low, buf, got), jnp.where(low, got, buf)], axis=pos)  5.22 us
    dot_general x3, matrix products, matmul(): jnp.dot(left, right, precision=lax.Precision.HIGHEST, preferred_element_t...  3.91 us
  transfers between devices with their start and end apart: 13, of which 8 were waited for; matrix products, arithmetic and copies ran while one was open for 6% of the time, Pallas kernels for 0%

profile of v5, /device:TPU:1, one launch (start us, length us, event | category | flops | bytes accessed | tf_op | source)
XLA Modules:
  0.0 144.9 jit_solution(10861475158758081608)
XLA Ops:
  0.0 0.7 broadcast_select_fusion.9
  0.7 0.7 pad_maximum_fusion.11
  1.4 29.5 %collective-permute-start = (f32[18,256]{1,0:T(8,128)S(1)}, f32[18,256]{1,0:T(8,128)S(1)}, u32[]{:S(2)}, u32[]{:S(2)}) collective-permute-start(f32[18,256]{1,0:T(8,128)S(1)} %pad_maximum_fusion.11), channel_id=1, source_target_pairs={{0,16},{1,17},{2,18},{3,19},{4,20},{5,21},{6,22},{7,23},{8,24},{9,... | collective-permute-start | bytes 55304 | tf_op jit(solution)/shard_map/ppermute | solution.py:41
  31.0 1.3 collective-permute-done
  32.3 0.7 select_bitcast_fusion.18
  33.1 8.4 %collective-permute-start.1 = (f32[2,18,256]{2,0,1:T(2,128)S(1)}, f32[2,18,256]{2,0,1:T(2,128)S(1)}, u32[]{:S(2)}, u32[]{:S(2)}) collective-permute-start(f32[2,18,256]{2,0,1:T(2,128)S(1)} %pad_maximum_fusion.10), channel_id=1, source_target_pairs={{0,8},{1,9},{2,10},{3,11},{4,12},{5,13},{6,14},{7,15},{8,0},{9,1},... | collective-permute-start | bytes 110600 | tf_op jit(solution)/shard_map/ppermute | solution.py:41
  41.5 5.0 %collective-permute-done.1 = f32[2,18,256]{2,0,1:T(2,128)S(1)} collective-permute-done((f32[2,18,256]{2,0,1:T(2,128)S(1)}, f32[2,18,256]{2,0,1:T(2,128)S(1)}, u32[]{:S(2)}, u32[]{:S(2)}) %collective-permute-start.1) | collective-permute-done | bytes 36896 | tf_op jit(solution)/shard_map/ppermute | solution.py:41
  46.6 5.2 %collective-permute-start.2 = (f32[2,2,18,256]{3,0,2,1:T(2,128)S(1)}, f32[2,2,18,256]{3,0,2,1:T(2,128)S(1)}, u32[]{:S(2)}, u32[]{:S(2)}) collective-permute-start(f32[2,2,18,256]{3,0,2,1:T(2,128)S(1)} %pad_maximum_fusion.9), channel_id=1, source_target_pairs={{0,4},{1,5},{2,6},{3,7},{4,0},{5,1},{6,2},{7,3},{8,12},{9,13},{10,... | collective-permute-start | bytes 221192 | tf_op jit(solution)/shard_map/ppermute | solution.py:41
  51.8 4.6 %collective-permute-done.2 = f32[2,2,18,256]{3,0,2,1:T(2,128)S(1)} collective-permute-done((f32[2,2,18,256]{3,0,2,1:T(2,128)S(1)}, f32[2,2,18,256]{3,0,2,1:T(2,128)S(1)}, u32[]{:S(2)}, u32[]{:S(2)}) %collective-permute-start.2) | collective-permute-done | bytes 73760 | tf_op jit(solution)/shard_map/ppermute | solution.py:41
  56.6 4.0 %collective-permute-start.3 = (f32[2,2,2,18,256]{4,0,3,1,2:T(2,128)S(1)}, f32[2,2,2,18,256]{4,0,3,1,2:T(2,128)S(1)}, u32[]{:S(2)}, u32[]{:S(2)}) collective-permute-start(f32[2,2,2,18,256]{4,0,3,1,2:T(2,128)S(1)} %pad_maximum_fusion.8), channel_id=1, source_target_pairs={{0,2},{1,3},{2,0},{3,1},{4,6},{5,7},{6,4},{7,5},{8,10},{9,11},{10,... | collective-permute-start | bytes 442376 | tf_op jit(solution)/shard_map/ppermute | solution.py:41
  60.5 3.5 %collective-permute-done.3 = f32[2,2,2,18,256]{4,0,3,1,2:T(2,128)S(1)} collective-permute-done((f32[2,2,2,18,256]{4,0,3,1,2:T(2,128)S(1)}, f32[2,2,2,18,256]{4,0,3,1,2:T(2,128)S(1)}, u32[]{:S(2)}, u32[]{:S(2)}) %collective-permute-start.3) | collective-permute-done | bytes 147488 | tf_op jit(solution)/shard_map/ppermute | solution.py:41
  64.1 0.1 select_bitcast_fusion.13
  64.2 0.1 fusion.14
  64.4 5.3 %collective-permute-start.4 = (f32[2,2,2,2,18,128]{5,0,4,1,2,3:T(2,128)S(1)}, f32[2,2,2,2,18,128]{5,0,4,1,2,3:T(2,128)S(1)}, u32[]{:S(2)}, u32[]{:S(2)}) collective-permute-start(f32[2,2,2,2,18,128]{5,0,4,1,2,3:T(2,128)S(1)} %get-tuple-element.41), channel_id=1, source_target_pairs={{0,1},{1,0},{2,3},{3,2},{4,5},{5,4},{6,7},{7,6},{8,9},{9,8},{10,11... | collective-permute-start | bytes 442376 | tf_op jit(solution)/shard_map/ppermute | solution.py:41
  69.7 5.9 %collective-permute-start.7 = (f32[2,2,2,2,18,128]{5,0,4,1,2,3:T(2,128)S(1)}, f32[2,2,2,2,18,128]{5,0,4,1,2,3:T(2,128)S(1)}, u32[]{:S(2)}, u32[]{:S(2)}) collective-permute-start(f32[2,2,2,2,18,128]{5,0,4,1,2,3:T(2,128)S(1)} %get-tuple-element.42), channel_id=1, source_target_pairs={{0,96},{1,97},{2,98},{3,99},{4,100},{5,101},{6,102},{7,103},{8,104... | collective-permute-start | bytes 442376 | tf_op jit(solution)/shard_map/ppermute | solution.py:41
  75.6 0.1 select_bitcast_fusion.11
  75.7 0.1 pad_maximum_fusion.5
  75.8 2.5 %collective-permute-start.5 = (f32[2,2,2,2,2,18,128]{6,0,5,1,2,3,4:T(2,128)S(1)}, f32[2,2,2,2,2,18,128]{6,0,5,1,2,3,4:T(2,128)S(1)}, u32[]{:S(2)}, u32[]{:S(2)}) collective-permute-start(f32[2,2,2,2,2,18,128]{6,0,5,1,2,3,4:T(2,128)S(1)} %pad_maximum_fusion.5), channel_id=1, source_target_pairs={{0,96},{1,97},{2,98},{3,99},{4,100},{5,101},{6,102},{7,103},{8,104... | collective-permute-start | bytes 884744 | tf_op jit(solution)/shard_map/ppermute | solution.py:41
  78.3 0.1 select_bitcast_fusion.9
  78.4 0.1 pad_maximum_fusion.6
  78.6 1.9 %collective-permute-start.8 = (f32[2,2,2,2,2,18,128]{6,1,5,2,3,4,0:T(2,128)S(1)}, f32[2,2,2,2,2,18,128]{6,1,5,2,3,4,0:T(2,128)S(1)}, u32[]{:S(2)}, u32[]{:S(2)}) collective-permute-start(f32[2,2,2,2,2,18,128]{6,1,5,2,3,4,0:T(2,128)S(1)} %pad_maximum_fusion.6), channel_id=1, source_target_pairs={{0,32},{1,33},{2,34},{3,35},{4,36},{5,37},{6,38},{7,39},{8,40},{9,... | collective-permute-start | bytes 884744 | tf_op jit(solution)/shard_map/ppermute | solution.py:41
  80.5 5.6 %collective-permute-done.5 = f32[2,2,2,2,2,18,128]{6,0,5,1,2,3,4:T(2,128)S(1)} collective-permute-done((f32[2,2,2,2,2,18,128]{6,0,5,1,2,3,4:T(2,128)S(1)}, f32[2,2,2,2,2,18,128]{6,0,5,1,2,3,4:T(2,128)S(1)}, u32[]{:S(2)}, u32[]{:S(2)}) %collective-permute-start.5) | collective-permute-done | bytes 294944 | tf_op jit(solution)/shard_map/ppermute | solution.py:41
  86.1 0.2 select_bitcast_fusion.7
  86.3 0.3 pad_maximum_fusion.2
  86.6 0.5 copy.80
  87.0 1.9 %collective-permute-start.6 = (f32[2,2,2,2,2,2,18,128]{7,5,6,4,3,2,1,0:T(2,128)S(1)}, f32[2,2,2,2,2,2,18,128]{7,5,6,4,3,2,1,0:T(2,128)S(1)}, u32[]{:S(2)}, u32[]{:S(2)}) collective-permute-start(f32[2,2,2,2,2,2,18,128]{7,5,6,4,3,2,1,0:T(2,128)S(1)} %copy.80), channel_id=1, source_target_pairs={{0,32},{1,33},{2,34},{3,35},{4,36},{5,37},{6,38},{7,39},{8,40},{9,... | collective-permute-start | bytes 1769480 | tf_op jit(solution)/shard_map/ppermute | solution.py:41
  89.0 0.2 select_bitcast_fusion.5
  89.2 0.3 pad_maximum_fusion.3
  89.5 0.3 copy.84
  89.8 2.1 %collective-permute-start.9 = (f32[2,2,2,2,2,2,18,128]{7,5,6,4,3,2,1,0:T(2,128)S(1)}, f32[2,2,2,2,2,2,18,128]{7,5,6,4,3,2,1,0:T(2,128)S(1)}, u32[]{:S(2)}, u32[]{:S(2)}) collective-permute-start(f32[2,2,2,2,2,2,18,128]{7,5,6,4,3,2,1,0:T(2,128)S(1)} %copy.84), channel_id=1, source_target_pairs={{0,1},{1,0},{2,3},{3,2},{4,5},{5,4},{6,7},{7,6},{8,9},{9,8},{10,11... | collective-permute-start | bytes 1769480 | tf_op jit(solution)/shard_map/ppermute | solution.py:41
  91.9 12.0 %collective-permute-done.6 = f32[2,2,2,2,2,2,18,128]{7,5,6,4,3,2,1,0:T(2,128)S(1)} collective-permute-done((f32[2,2,2,2,2,2,18,128]{7,5,6,4,3,2,1,0:T(2,128)S(1)}, f32[2,2,2,2,2,2,18,128]{7,5,6,4,3,2,1,0:T(2,128)S(1)}, u32[]{:S(2)}, u32[]{:S(2)}) %collective-permute-start.6) | collective-permute-done | bytes 589856 | tf_op jit(solution)/shard_map/ppermute | solution.py:41
  103.9 0.7 select_bitcast_fusion.3
  104.7 0.6 pad_maximum_fusion
  105.3 0.9 copy.83
  106.2 0.5 select_bitcast_fusion.1
  106.8 0.6 pad_maximum_fusion.1
  107.4 0.9 copy.87
  108.4 0.2 slice_bitcast_fusion.3
  108.6 0.7 fusion.31
  109.3 0.2 copy.90
  109.5 0.1 slice.253
  109.6 0.2 copy.89
  109.8 0.9 reshape.48
  110.7 0.1 maximum_maximum_fusion
  110.8 2.3 %copy.88 = f32[4,32,12,256]{3,2,1,0:T(8,128)} copy(f32[4,32,12,256]{3,1,2,0:T(8,128)S(1)} %maximum_maximum_fusion) | data formatting | bytes 3145728 | tf_op jit(solution)/shard_map/concatenate | solution.py:102
  113.1 1.7 %reshape.47 = f32[1536,256]{1,0:T(8,128)S(1)} reshape(f32[4,32,12,256]{3,2,1,0:T(8,128)} %copy.88) | data formatting | bytes 3145728 | tf_op jit(solution)/shard_map/reshape | solution.py:102
  114.9 0.3 copy-done
  115.2 2.5 %fusion = f32[256,256]{1,0:T(8,128)S(1)} fusion(f32[1536,256]{1,0:T(8,128)S(1)} %copy-done, f32[1536,256]{1,0:T(8,128)S(1)} %reshape.47), kind=kOutput, calls=%fused_computation.5 | convolution fusion | flops 1209532416 | bytes 3407872 | tf_op jit(solution)/shard_map/dot_general | solution.py:22
  117.7 0.7 fusion.11
  118.4 1.5 %convolution_subtract_fusion = f32[1536,256]{1,0:T(8,128)S(1)} fusion(f32[1536,256]{1,0:T(8,128)S(1)} %copy-done, f32[256,256]{1,0:T(8,128)S(1)} %fusion.11, f32[1536,256]{1,0:T(8,128)S(1)} %reshape.47), kind=kOutput, calls=%fused_computation | convolution fusion | flops 1209925632 | bytes 4980736 | tf_op jit(solution)/shard_map/dot_general | solution.py:32
  119.9 1.1 copy-done.1
  121.1 5.5 %collective-permute-start.10 = (f32[512,256]{1,0:T(8,128)S(1)}, f32[512,256]{1,0:T(8,128)S(1)}, u32[]{:S(2)}, u32[]{:S(2)}) collective-permute-start(f32[512,256]{1,0:T(8,128)S(1)} %pad_maximum_fusion.4), channel_id=1, source_target_pairs={{0,128},{128,0},{256,384},{384,256},{512,640},{640,512},{768,896},... | collective-permute-start | bytes 1572872 | tf_op jit(solution)/shard_map/ppermute | solution.py:10
  126.6 0.2 copy.91
  126.8 0.1 slice.257
  126.9 2.1 %collective-permute-start.12 = (f32[256,256]{1,0:T(8,128)S(1)}, f32[256,256]{1,0:T(8,128)S(1)}, u32[]{:S(2)}, u32[]{:S(2)}) collective-permute-start(f32[256,256]{1,0:T(8,128)S(1)} %slice.257), channel_id=1, source_target_pairs={{0,256},{128,384},{256,0},{384,128},{512,768},{640,896},{768,512},... | collective-permute-start | bytes 786440 | tf_op jit(solution)/shard_map/ppermute | solution.py:10
  129.0 1.6 %convolution_add_fusion.1 = f32[256,256]{1,0:T(8,128)S(1)} fusion(f32[512,256]{1,0:T(8,128)S(1)} %collective-permute-done.10, pred[]{:T(512)S(6)} %eq.49, f32[256,256]{1,0:T(8,128)S(1)} %slice.253, f32[1536,256]{1,0:T(8,128)} %copy-done.1), kind=kOutput, calls=%fused_computation.11 | convolution fusion | flops 201588736 | bytes 1836544 | tf_op jit(solution)/shard_map/dot_general | solution.py:22
  130.7 0.7 fusion.8
  131.3 1.3 subtract_select_fusion
  132.7 3.4 %collective-permute-start.11 = (f32[256,256]{1,0:T(8,128)S(1)}, f32[256,256]{1,0:T(8,128)S(1)}, u32[]{:S(2)}, u32[]{:S(2)}) collective-permute-start(f32[256,256]{1,0:T(8,128)S(1)} %subtract_select_fusion), channel_id=1, source_target_pairs={{0,256},{128,384},{256,0},{384,128},{512,768},{640,896},{768,512},... | collective-permute-start | bytes 786440 | tf_op jit(solution)/shard_map/ppermute | solution.py:10
  136.1 0.5 collective-permute-done.12
  136.6 5.8 %collective-permute-done.11 = f32[256,256]{1,0:T(8,128)S(1)} collective-permute-done((f32[256,256]{1,0:T(8,128)S(1)}, f32[256,256]{1,0:T(8,128)S(1)}, u32[]{:S(2)}, u32[]{:S(2)}) %collective-permute-start.11) | collective-permute-done | bytes 262176 | tf_op jit(solution)/shard_map/ppermute | solution.py:10
  142.4 0.6 convolution_add_fusion
  143.1 0.7 fusion.5
  143.7 1.1 select_dynamic-update-slice_fusion
  (25 shorter events, 0.5 us)
Async XLA Ops:
  1.4 30.8 %collective-permute-start = (f32[18,256]{1,0:T(8,128)S(1)}, f32[18,256]{1,0:T(8,128)S(1)}, u32[]{:S(2)}, u32[]{:S(2)}) collective-permute-start(f32[18,256]{1,0:T(8,128)S(1)} %pad_maximum_fusion.11), channel_id=1, source_target_pairs={{0,16},{1,17},{2,18},{3,19},{4,20},{5,21},{6,22},{7,23},{8,24},{9,... | collective-permute-start | bytes 55304 | tf_op jit(solution)/shard_map/ppermute | solution.py:41
  33.1 13.4 %collective-permute-start.1 = (f32[2,18,256]{2,0,1:T(2,128)S(1)}, f32[2,18,256]{2,0,1:T(2,128)S(1)}, u32[]{:S(2)}, u32[]{:S(2)}) collective-permute-start(f32[2,18,256]{2,0,1:T(2,128)S(1)} %pad_maximum_fusion.10), channel_id=1, source_target_pairs={{0,8},{1,9},{2,10},{3,11},{4,12},{5,13},{6,14},{7,15},{8,0},{9,1},... | collective-permute-start | bytes 110600 | tf_op jit(solution)/shard_map/ppermute | solution.py:41
  46.6 9.8 %collective-permute-start.2 = (f32[2,2,18,256]{3,0,2,1:T(2,128)S(1)}, f32[2,2,18,256]{3,0,2,1:T(2,128)S(1)}, u32[]{:S(2)}, u32[]{:S(2)}) collective-permute-start(f32[2,2,18,256]{3,0,2,1:T(2,128)S(1)} %pad_maximum_fusion.9), channel_id=1, source_target_pairs={{0,4},{1,5},{2,6},{3,7},{4,0},{5,1},{6,2},{7,3},{8,12},{9,13},{10,... | collective-permute-start | bytes 221192 | tf_op jit(solution)/shard_map/ppermute | solution.py:41
  56.6 7.5 %collective-permute-start.3 = (f32[2,2,2,18,256]{4,0,3,1,2:T(2,128)S(1)}, f32[2,2,2,18,256]{4,0,3,1,2:T(2,128)S(1)}, u32[]{:S(2)}, u32[]{:S(2)}) collective-permute-start(f32[2,2,2,18,256]{4,0,3,1,2:T(2,128)S(1)} %pad_maximum_fusion.8), channel_id=1, source_target_pairs={{0,2},{1,3},{2,0},{3,1},{4,6},{5,7},{6,4},{7,5},{8,10},{9,11},{10,... | collective-permute-start | bytes 442376 | tf_op jit(solution)/shard_map/ppermute | solution.py:41
  64.4 11.2 %collective-permute-start.4 = (f32[2,2,2,2,18,128]{5,0,4,1,2,3:T(2,128)S(1)}, f32[2,2,2,2,18,128]{5,0,4,1,2,3:T(2,128)S(1)}, u32[]{:S(2)}, u32[]{:S(2)}) collective-permute-start(f32[2,2,2,2,18,128]{5,0,4,1,2,3:T(2,128)S(1)} %get-tuple-element.41), channel_id=1, source_target_pairs={{0,1},{1,0},{2,3},{3,2},{4,5},{5,4},{6,7},{7,6},{8,9},{9,8},{10,11... | collective-permute-start | bytes 442376 | tf_op jit(solution)/shard_map/ppermute | solution.py:41
  69.7 8.6 %collective-permute-start.7 = (f32[2,2,2,2,18,128]{5,0,4,1,2,3:T(2,128)S(1)}, f32[2,2,2,2,18,128]{5,0,4,1,2,3:T(2,128)S(1)}, u32[]{:S(2)}, u32[]{:S(2)}) collective-permute-start(f32[2,2,2,2,18,128]{5,0,4,1,2,3:T(2,128)S(1)} %get-tuple-element.42), channel_id=1, source_target_pairs={{0,96},{1,97},{2,98},{3,99},{4,100},{5,101},{6,102},{7,103},{8,104... | collective-permute-start | bytes 442376 | tf_op jit(solution)/shard_map/ppermute | solution.py:41
  75.8 10.3 %collective-permute-start.5 = (f32[2,2,2,2,2,18,128]{6,0,5,1,2,3,4:T(2,128)S(1)}, f32[2,2,2,2,2,18,128]{6,0,5,1,2,3,4:T(2,128)S(1)}, u32[]{:S(2)}, u32[]{:S(2)}) collective-permute-start(f32[2,2,2,2,2,18,128]{6,0,5,1,2,3,4:T(2,128)S(1)} %pad_maximum_fusion.5), channel_id=1, source_target_pairs={{0,96},{1,97},{2,98},{3,99},{4,100},{5,101},{6,102},{7,103},{8,104... | collective-permute-start | bytes 884744 | tf_op jit(solution)/shard_map/ppermute | solution.py:41
  78.6 10.4 %collective-permute-start.8 = (f32[2,2,2,2,2,18,128]{6,1,5,2,3,4,0:T(2,128)S(1)}, f32[2,2,2,2,2,18,128]{6,1,5,2,3,4,0:T(2,128)S(1)}, u32[]{:S(2)}, u32[]{:S(2)}) collective-permute-start(f32[2,2,2,2,2,18,128]{6,1,5,2,3,4,0:T(2,128)S(1)} %pad_maximum_fusion.6), channel_id=1, source_target_pairs={{0,32},{1,33},{2,34},{3,35},{4,36},{5,37},{6,38},{7,39},{8,40},{9,... | collective-permute-start | bytes 884744 | tf_op jit(solution)/shard_map/ppermute | solution.py:41
  87.0 16.9 %collective-permute-start.6 = (f32[2,2,2,2,2,2,18,128]{7,5,6,4,3,2,1,0:T(2,128)S(1)}, f32[2,2,2,2,2,2,18,128]{7,5,6,4,3,2,1,0:T(2,128)S(1)}, u32[]{:S(2)}, u32[]{:S(2)}) collective-permute-start(f32[2,2,2,2,2,2,18,128]{7,5,6,4,3,2,1,0:T(2,128)S(1)} %copy.80), channel_id=1, source_target_pairs={{0,32},{1,33},{2,34},{3,35},{4,36},{5,37},{6,38},{7,39},{8,40},{9,... | collective-permute-start | bytes 1769480 | tf_op jit(solution)/shard_map/ppermute | solution.py:41
  89.8 16.4 %collective-permute-start.9 = (f32[2,2,2,2,2,2,18,128]{7,5,6,4,3,2,1,0:T(2,128)S(1)}, f32[2,2,2,2,2,2,18,128]{7,5,6,4,3,2,1,0:T(2,128)S(1)}, u32[]{:S(2)}, u32[]{:S(2)}) collective-permute-start(f32[2,2,2,2,2,2,18,128]{7,5,6,4,3,2,1,0:T(2,128)S(1)} %copy.84), channel_id=1, source_target_pairs={{0,1},{1,0},{2,3},{3,2},{4,5},{5,4},{6,7},{7,6},{8,9},{9,8},{10,11... | collective-permute-start | bytes 1769480 | tf_op jit(solution)/shard_map/ppermute | solution.py:41
  113.1 2.0 %copy-start = (f32[1536,256]{1,0:T(8,128)S(1)}, f32[1536,256]{1,0:T(8,128)}, u32[]{:S(2)}) copy-start(f32[1536,256]{1,0:T(8,128)} %param.5) | copy-start | bytes 4718596
  115.2 2.6 %copy-start.2 = (f32[256,256]{1,0:T(8,128)S(1)}, f32[256,256]{1,0:T(8,128)}, u32[]{:S(2)}) copy-start(f32[256,256]{1,0:T(8,128)} %reshape.48) | copy-start | bytes 786436
  119.9 1.1 copy-start.1
  121.0 5.6 %copy-start.3 = (f32[2,32,4,256]{3,1,2,0:T(8,128)S(1)}, f32[2,32,4,256]{3,1,2,0:T(8,128)}, u32[]{:S(2)}) copy-start(f32[2,32,4,256]{3,1,2,0:T(8,128)} %get-tuple-element.37) | copy-start | bytes 786436
  121.1 7.9 %collective-permute-start.10 = (f32[512,256]{1,0:T(8,128)S(1)}, f32[512,256]{1,0:T(8,128)S(1)}, u32[]{:S(2)}, u32[]{:S(2)}) collective-permute-start(f32[512,256]{1,0:T(8,128)S(1)} %pad_maximum_fusion.4), channel_id=1, source_target_pairs={{0,128},{128,0},{256,384},{384,256},{512,640},{640,512},{768,896},... | collective-permute-start | bytes 1572872 | tf_op jit(solution)/shard_map/ppermute | solution.py:10
  126.9 9.7 %collective-permute-start.12 = (f32[256,256]{1,0:T(8,128)S(1)}, f32[256,256]{1,0:T(8,128)S(1)}, u32[]{:S(2)}, u32[]{:S(2)}) collective-permute-start(f32[256,256]{1,0:T(8,128)S(1)} %slice.257), channel_id=1, source_target_pairs={{0,256},{128,384},{256,0},{384,128},{512,768},{640,896},{768,512},... | collective-permute-start | bytes 786440 | tf_op jit(solution)/shard_map/ppermute | solution.py:10
  132.7 9.7 %collective-permute-start.11 = (f32[256,256]{1,0:T(8,128)S(1)}, f32[256,256]{1,0:T(8,128)S(1)}, u32[]{:S(2)}, u32[]{:S(2)}) collective-permute-start(f32[256,256]{1,0:T(8,128)S(1)} %subtract_select_fusion), channel_id=1, source_target_pairs={{0,256},{128,384},{256,0},{384,128},{512,768},{640,896},{768,512},... | collective-permute-start | bytes 786440 | tf_op jit(solution)/shard_map/ppermute | solution.py:10

commit v6 on v5

--- a/solution.py
+++ b/solution.py
@@ -23,13 +23,13 @@
         left,
         right,
         (((0,), (0,)), ((), ())),
-        precision=lax.Precision.HIGHEST,
+        precision=lax.Precision.HIGH,
         preferred_element_type=jnp.float32,
     )
 
 
 def matmul(left, right):
-    return jnp.dot(left, right, precision=lax.Precision.HIGHEST, preferred_element_type=jnp.float32)
+    return jnp.dot(left, right, precision=lax.Precision.HIGH, preferred_element_type=jnp.float32)
 
 
 def doubling_gather(shard, axis, label, shared, orders):

time: 146 us -> 143 us (0.979)
  matrix products: 10.7 us -> 7.58 us
    dot_general x6, matrix products: 6.78 us -> 4.55 us  [inner(): lax.dot_general(left, right, (((0,), (0,)), ((), ())), precision=lax.Prec...]
where the time goes in v6:
time: 143 us; the launch traced here: 142 us
  starting transfers between devices  77.4 us (54%)
  waiting for transfers between devices  38.9 us (27%)
  local copies, waits for them, and re-layouts  10.7 us (7%)
  matrix products  7.58 us (5%)
  other arithmetic  6.87 us (5%)
    ppermute x10, starting transfers between devices, step(): lax.ppermute(buf, axis, [(i, unlabel[label(i) ^ 1 << bit]) for i in range...  66.6 us
    ppermute x10, waiting for transfers between devices, step(): lax.ppermute(buf, axis, [(i, unlabel[label(i) ^ 1 << bit]) for i in range...  32.1 us
    ppermute x3, starting transfers between devices, swapped(): lax.ppermute(shard, axis, [(i, i ^ 1 << stride) for i in range(lax.axis_s...  10.8 us
    ppermute x3, waiting for transfers between devices, swapped(): lax.ppermute(shard, axis, [(i, i ^ 1 << stride) for i in range(lax.axis_s...  6.89 us
    another operation x20, other arithmetic, step(): jnp.stack([jnp.where(low, buf, got), jnp.where(low, got, buf)], axis=pos)  5.22 us
    dot_general x6, matrix products, inner(): lax.dot_general(left, right, (((0,), (0,)), ((), ())), precision=lax.Prec...  4.55 us
    dot_general x3, matrix products, matmul(): jnp.dot(left, right, precision=lax.Precision.HIGH, preferred_element_type...  3.03 us
  transfers between devices with their start and end apart: 13, of which 8 were waited for; matrix products, arithmetic and copies ran while one was open for 6% of the time, Pallas kernels for 0%

profile of v6, /device:TPU:1, one launch (start us, length us, event | category | flops | bytes accessed | tf_op | source)
XLA Modules:
  0.0 142.1 jit_solution(4031072711905614707)
XLA Ops:
  0.0 0.7 broadcast_select_fusion.9
  0.7 0.7 pad_maximum_fusion.11
  1.4 29.5 %collective-permute-start = (f32[18,256]{1,0:T(8,128)S(1)}, f32[18,256]{1,0:T(8,128)S(1)}, u32[]{:S(2)}, u32[]{:S(2)}) collective-permute-start(f32[18,256]{1,0:T(8,128)S(1)} %pad_maximum_fusion.11), channel_id=1, source_target_pairs={{0,16},{1,17},{2,18},{3,19},{4,20},{5,21},{6,22},{7,23},{8,24},{9,... | collective-permute-start | bytes 55304 | tf_op jit(solution)/shard_map/ppermute | solution.py:41
  31.0 1.3 collective-permute-done
  32.3 0.7 select_bitcast_fusion.18
  33.1 8.4 %collective-permute-start.1 = (f32[2,18,256]{2,0,1:T(2,128)S(1)}, f32[2,18,256]{2,0,1:T(2,128)S(1)}, u32[]{:S(2)}, u32[]{:S(2)}) collective-permute-start(f32[2,18,256]{2,0,1:T(2,128)S(1)} %pad_maximum_fusion.10), channel_id=1, source_target_pairs={{0,8},{1,9},{2,10},{3,11},{4,12},{5,13},{6,14},{7,15},{8,0},{9,1},... | collective-permute-start | bytes 110600 | tf_op jit(solution)/shard_map/ppermute | solution.py:41
  41.5 5.0 %collective-permute-done.1 = f32[2,18,256]{2,0,1:T(2,128)S(1)} collective-permute-done((f32[2,18,256]{2,0,1:T(2,128)S(1)}, f32[2,18,256]{2,0,1:T(2,128)S(1)}, u32[]{:S(2)}, u32[]{:S(2)}) %collective-permute-start.1) | collective-permute-done | bytes 36896 | tf_op jit(solution)/shard_map/ppermute | solution.py:41
  46.6 5.2 %collective-permute-start.2 = (f32[2,2,18,256]{3,0,2,1:T(2,128)S(1)}, f32[2,2,18,256]{3,0,2,1:T(2,128)S(1)}, u32[]{:S(2)}, u32[]{:S(2)}) collective-permute-start(f32[2,2,18,256]{3,0,2,1:T(2,128)S(1)} %pad_maximum_fusion.9), channel_id=1, source_target_pairs={{0,4},{1,5},{2,6},{3,7},{4,0},{5,1},{6,2},{7,3},{8,12},{9,13},{10,... | collective-permute-start | bytes 221192 | tf_op jit(solution)/shard_map/ppermute | solution.py:41
  51.8 4.6 %collective-permute-done.2 = f32[2,2,18,256]{3,0,2,1:T(2,128)S(1)} collective-permute-done((f32[2,2,18,256]{3,0,2,1:T(2,128)S(1)}, f32[2,2,18,256]{3,0,2,1:T(2,128)S(1)}, u32[]{:S(2)}, u32[]{:S(2)}) %collective-permute-start.2) | collective-permute-done | bytes 73760 | tf_op jit(solution)/shard_map/ppermute | solution.py:41
  56.6 4.0 %collective-permute-start.3 = (f32[2,2,2,18,256]{4,0,3,1,2:T(2,128)S(1)}, f32[2,2,2,18,256]{4,0,3,1,2:T(2,128)S(1)}, u32[]{:S(2)}, u32[]{:S(2)}) collective-permute-start(f32[2,2,2,18,256]{4,0,3,1,2:T(2,128)S(1)} %pad_maximum_fusion.8), channel_id=1, source_target_pairs={{0,2},{1,3},{2,0},{3,1},{4,6},{5,7},{6,4},{7,5},{8,10},{9,11},{10,... | collective-permute-start | bytes 442376 | tf_op jit(solution)/shard_map/ppermute | solution.py:41
  60.5 3.5 %collective-permute-done.3 = f32[2,2,2,18,256]{4,0,3,1,2:T(2,128)S(1)} collective-permute-done((f32[2,2,2,18,256]{4,0,3,1,2:T(2,128)S(1)}, f32[2,2,2,18,256]{4,0,3,1,2:T(2,128)S(1)}, u32[]{:S(2)}, u32[]{:S(2)}) %collective-permute-start.3) | collective-permute-done | bytes 147488 | tf_op jit(solution)/shard_map/ppermute | solution.py:41
  64.1 0.1 select_bitcast_fusion.13
  64.2 0.1 fusion.14
  64.4 5.3 %collective-permute-start.4 = (f32[2,2,2,2,18,128]{5,0,4,1,2,3:T(2,128)S(1)}, f32[2,2,2,2,18,128]{5,0,4,1,2,3:T(2,128)S(1)}, u32[]{:S(2)}, u32[]{:S(2)}) collective-permute-start(f32[2,2,2,2,18,128]{5,0,4,1,2,3:T(2,128)S(1)} %get-tuple-element.41), channel_id=1, source_target_pairs={{0,1},{1,0},{2,3},{3,2},{4,5},{5,4},{6,7},{7,6},{8,9},{9,8},{10,11... | collective-permute-start | bytes 442376 | tf_op jit(solution)/shard_map/ppermute | solution.py:41
  69.7 5.9 %collective-permute-start.7 = (f32[2,2,2,2,18,128]{5,0,4,1,2,3:T(2,128)S(1)}, f32[2,2,2,2,18,128]{5,0,4,1,2,3:T(2,128)S(1)}, u32[]{:S(2)}, u32[]{:S(2)}) collective-permute-start(f32[2,2,2,2,18,128]{5,0,4,1,2,3:T(2,128)S(1)} %get-tuple-element.42), channel_id=1, source_target_pairs={{0,96},{1,97},{2,98},{3,99},{4,100},{5,101},{6,102},{7,103},{8,104... | collective-permute-start | bytes 442376 | tf_op jit(solution)/shard_map/ppermute | solution.py:41
  75.6 0.1 select_bitcast_fusion.11
  75.7 0.1 pad_maximum_fusion.5
  75.8 2.5 %collective-permute-start.5 = (f32[2,2,2,2,2,18,128]{6,0,5,1,2,3,4:T(2,128)S(1)}, f32[2,2,2,2,2,18,128]{6,0,5,1,2,3,4:T(2,128)S(1)}, u32[]{:S(2)}, u32[]{:S(2)}) collective-permute-start(f32[2,2,2,2,2,18,128]{6,0,5,1,2,3,4:T(2,128)S(1)} %pad_maximum_fusion.5), channel_id=1, source_target_pairs={{0,96},{1,97},{2,98},{3,99},{4,100},{5,101},{6,102},{7,103},{8,104... | collective-permute-start | bytes 884744 | tf_op jit(solution)/shard_map/ppermute | solution.py:41
  78.3 0.1 select_bitcast_fusion.9
  78.4 0.1 pad_maximum_fusion.6
  78.6 1.9 %collective-permute-start.8 = (f32[2,2,2,2,2,18,128]{6,1,5,2,3,4,0:T(2,128)S(1)}, f32[2,2,2,2,2,18,128]{6,1,5,2,3,4,0:T(2,128)S(1)}, u32[]{:S(2)}, u32[]{:S(2)}) collective-permute-start(f32[2,2,2,2,2,18,128]{6,1,5,2,3,4,0:T(2,128)S(1)} %pad_maximum_fusion.6), channel_id=1, source_target_pairs={{0,32},{1,33},{2,34},{3,35},{4,36},{5,37},{6,38},{7,39},{8,40},{9,... | collective-permute-start | bytes 884744 | tf_op jit(solution)/shard_map/ppermute | solution.py:41
  80.5 5.6 %collective-permute-done.5 = f32[2,2,2,2,2,18,128]{6,0,5,1,2,3,4:T(2,128)S(1)} collective-permute-done((f32[2,2,2,2,2,18,128]{6,0,5,1,2,3,4:T(2,128)S(1)}, f32[2,2,2,2,2,18,128]{6,0,5,1,2,3,4:T(2,128)S(1)}, u32[]{:S(2)}, u32[]{:S(2)}) %collective-permute-start.5) | collective-permute-done | bytes 294944 | tf_op jit(solution)/shard_map/ppermute | solution.py:41
  86.1 0.2 select_bitcast_fusion.7
  86.3 0.3 pad_maximum_fusion.2
  86.6 0.5 copy.80
  87.0 1.9 %collective-permute-start.6 = (f32[2,2,2,2,2,2,18,128]{7,5,6,4,3,2,1,0:T(2,128)S(1)}, f32[2,2,2,2,2,2,18,128]{7,5,6,4,3,2,1,0:T(2,128)S(1)}, u32[]{:S(2)}, u32[]{:S(2)}) collective-permute-start(f32[2,2,2,2,2,2,18,128]{7,5,6,4,3,2,1,0:T(2,128)S(1)} %copy.80), channel_id=1, source_target_pairs={{0,32},{1,33},{2,34},{3,35},{4,36},{5,37},{6,38},{7,39},{8,40},{9,... | collective-permute-start | bytes 1769480 | tf_op jit(solution)/shard_map/ppermute | solution.py:41
  89.0 0.2 select_bitcast_fusion.5
  89.2 0.3 pad_maximum_fusion.3
  89.5 0.3 copy.84
  89.8 2.1 %collective-permute-start.9 = (f32[2,2,2,2,2,2,18,128]{7,5,6,4,3,2,1,0:T(2,128)S(1)}, f32[2,2,2,2,2,2,18,128]{7,5,6,4,3,2,1,0:T(2,128)S(1)}, u32[]{:S(2)}, u32[]{:S(2)}) collective-permute-start(f32[2,2,2,2,2,2,18,128]{7,5,6,4,3,2,1,0:T(2,128)S(1)} %copy.84), channel_id=1, source_target_pairs={{0,1},{1,0},{2,3},{3,2},{4,5},{5,4},{6,7},{7,6},{8,9},{9,8},{10,11... | collective-permute-start | bytes 1769480 | tf_op jit(solution)/shard_map/ppermute | solution.py:41
  91.9 12.0 %collective-permute-done.6 = f32[2,2,2,2,2,2,18,128]{7,5,6,4,3,2,1,0:T(2,128)S(1)} collective-permute-done((f32[2,2,2,2,2,2,18,128]{7,5,6,4,3,2,1,0:T(2,128)S(1)}, f32[2,2,2,2,2,2,18,128]{7,5,6,4,3,2,1,0:T(2,128)S(1)}, u32[]{:S(2)}, u32[]{:S(2)}) %collective-permute-start.6) | collective-permute-done | bytes 589856 | tf_op jit(solution)/shard_map/ppermute | solution.py:41
  103.9 0.7 select_bitcast_fusion.3
  104.7 0.6 pad_maximum_fusion
  105.3 0.9 copy.83
  106.2 0.5 select_bitcast_fusion.1
  106.8 0.6 pad_maximum_fusion.1
  107.4 0.9 copy.87
  108.4 0.2 slice_bitcast_fusion.3
  108.6 0.7 fusion.31
  109.3 0.2 copy.90
  109.5 0.1 slice.253
  109.6 0.2 copy.89
  109.8 0.9 reshape.48
  110.7 0.1 maximum_maximum_fusion
  110.8 2.3 %copy.88 = f32[4,32,12,256]{3,2,1,0:T(8,128)} copy(f32[4,32,12,256]{3,1,2,0:T(8,128)S(1)} %maximum_maximum_fusion) | data formatting | bytes 3145728 | tf_op jit(solution)/shard_map/concatenate | solution.py:102
  113.1 1.7 %reshape.47 = f32[1536,256]{1,0:T(8,128)S(1)} reshape(f32[4,32,12,256]{3,2,1,0:T(8,128)} %copy.88) | data formatting | bytes 3145728 | tf_op jit(solution)/shard_map/reshape | solution.py:102
  114.9 0.3 copy-done
  115.2 1.4 fusion
  116.5 0.5 fusion.11
  117.0 0.8 convolution_subtract_fusion
  117.8 1.1 copy-done.1
  119.0 5.5 %collective-permute-start.10 = (f32[512,256]{1,0:T(8,128)S(1)}, f32[512,256]{1,0:T(8,128)S(1)}, u32[]{:S(2)}, u32[]{:S(2)}) collective-permute-start(f32[512,256]{1,0:T(8,128)S(1)} %pad_maximum_fusion.4), channel_id=1, source_target_pairs={{0,128},{128,0},{256,384},{384,256},{512,640},{640,512},{768,896},... | collective-permute-start | bytes 1572872 | tf_op jit(solution)/shard_map/ppermute | solution.py:10
  124.5 0.2 copy.91
  124.7 0.1 slice.257
  124.8 1.9 %collective-permute-start.12 = (f32[256,256]{1,0:T(8,128)S(1)}, f32[256,256]{1,0:T(8,128)S(1)}, u32[]{:S(2)}, u32[]{:S(2)}) collective-permute-start(f32[256,256]{1,0:T(8,128)S(1)} %slice.257), channel_id=1, source_target_pairs={{0,256},{128,384},{256,0},{384,128},{512,768},{640,896},{768,512},... | collective-permute-start | bytes 786440 | tf_op jit(solution)/shard_map/ppermute | solution.py:10
  126.8 1.4 convolution_add_fusion.1
  128.2 0.5 fusion.8
  128.7 1.2 subtract_select_fusion
  129.9 3.4 %collective-permute-start.11 = (f32[256,256]{1,0:T(8,128)S(1)}, f32[256,256]{1,0:T(8,128)S(1)}, u32[]{:S(2)}, u32[]{:S(2)}) collective-permute-start(f32[256,256]{1,0:T(8,128)S(1)} %subtract_select_fusion), channel_id=1, source_target_pairs={{0,256},{128,384},{256,0},{384,128},{512,768},{640,896},{768,512},... | collective-permute-start | bytes 786440 | tf_op jit(solution)/shard_map/ppermute | solution.py:10
  133.3 1.3 collective-permute-done.12
  134.6 5.6 %collective-permute-done.11 = f32[256,256]{1,0:T(8,128)S(1)} collective-permute-done((f32[256,256]{1,0:T(8,128)S(1)}, f32[256,256]{1,0:T(8,128)S(1)}, u32[]{:S(2)}, u32[]{:S(2)}) %collective-permute-start.11) | collective-permute-done | bytes 262176 | tf_op jit(solution)/shard_map/ppermute | solution.py:10
  140.2 0.4 convolution_add_fusion
  140.6 0.5 fusion.5
  141.0 1.0 select_dynamic-update-slice_fusion
  (25 shorter events, 0.5 us)
Async XLA Ops:
  1.4 30.8 %collective-permute-start = (f32[18,256]{1,0:T(8,128)S(1)}, f32[18,256]{1,0:T(8,128)S(1)}, u32[]{:S(2)}, u32[]{:S(2)}) collective-permute-start(f32[18,256]{1,0:T(8,128)S(1)} %pad_maximum_fusion.11), channel_id=1, source_target_pairs={{0,16},{1,17},{2,18},{3,19},{4,20},{5,21},{6,22},{7,23},{8,24},{9,... | collective-permute-start | bytes 55304 | tf_op jit(solution)/shard_map/ppermute | solution.py:41
  33.1 13.4 %collective-permute-start.1 = (f32[2,18,256]{2,0,1:T(2,128)S(1)}, f32[2,18,256]{2,0,1:T(2,128)S(1)}, u32[]{:S(2)}, u32[]{:S(2)}) collective-permute-start(f32[2,18,256]{2,0,1:T(2,128)S(1)} %pad_maximum_fusion.10), channel_id=1, source_target_pairs={{0,8},{1,9},{2,10},{3,11},{4,12},{5,13},{6,14},{7,15},{8,0},{9,1},... | collective-permute-start | bytes 110600 | tf_op jit(solution)/shard_map/ppermute | solution.py:41
  46.6 9.8 %collective-permute-start.2 = (f32[2,2,18,256]{3,0,2,1:T(2,128)S(1)}, f32[2,2,18,256]{3,0,2,1:T(2,128)S(1)}, u32[]{:S(2)}, u32[]{:S(2)}) collective-permute-start(f32[2,2,18,256]{3,0,2,1:T(2,128)S(1)} %pad_maximum_fusion.9), channel_id=1, source_target_pairs={{0,4},{1,5},{2,6},{3,7},{4,0},{5,1},{6,2},{7,3},{8,12},{9,13},{10,... | collective-permute-start | bytes 221192 | tf_op jit(solution)/shard_map/ppermute | solution.py:41
  56.6 7.5 %collective-permute-start.3 = (f32[2,2,2,18,256]{4,0,3,1,2:T(2,128)S(1)}, f32[2,2,2,18,256]{4,0,3,1,2:T(2,128)S(1)}, u32[]{:S(2)}, u32[]{:S(2)}) collective-permute-start(f32[2,2,2,18,256]{4,0,3,1,2:T(2,128)S(1)} %pad_maximum_fusion.8), channel_id=1, source_target_pairs={{0,2},{1,3},{2,0},{3,1},{4,6},{5,7},{6,4},{7,5},{8,10},{9,11},{10,... | collective-permute-start | bytes 442376 | tf_op jit(solution)/shard_map/ppermute | solution.py:41
  64.4 11.2 %collective-permute-start.4 = (f32[2,2,2,2,18,128]{5,0,4,1,2,3:T(2,128)S(1)}, f32[2,2,2,2,18,128]{5,0,4,1,2,3:T(2,128)S(1)}, u32[]{:S(2)}, u32[]{:S(2)}) collective-permute-start(f32[2,2,2,2,18,128]{5,0,4,1,2,3:T(2,128)S(1)} %get-tuple-element.41), channel_id=1, source_target_pairs={{0,1},{1,0},{2,3},{3,2},{4,5},{5,4},{6,7},{7,6},{8,9},{9,8},{10,11... | collective-permute-start | bytes 442376 | tf_op jit(solution)/shard_map/ppermute | solution.py:41
  69.7 8.6 %collective-permute-start.7 = (f32[2,2,2,2,18,128]{5,0,4,1,2,3:T(2,128)S(1)}, f32[2,2,2,2,18,128]{5,0,4,1,2,3:T(2,128)S(1)}, u32[]{:S(2)}, u32[]{:S(2)}) collective-permute-start(f32[2,2,2,2,18,128]{5,0,4,1,2,3:T(2,128)S(1)} %get-tuple-element.42), channel_id=1, source_target_pairs={{0,96},{1,97},{2,98},{3,99},{4,100},{5,101},{6,102},{7,103},{8,104... | collective-permute-start | bytes 442376 | tf_op jit(solution)/shard_map/ppermute | solution.py:41
  75.8 10.3 %collective-permute-start.5 = (f32[2,2,2,2,2,18,128]{6,0,5,1,2,3,4:T(2,128)S(1)}, f32[2,2,2,2,2,18,128]{6,0,5,1,2,3,4:T(2,128)S(1)}, u32[]{:S(2)}, u32[]{:S(2)}) collective-permute-start(f32[2,2,2,2,2,18,128]{6,0,5,1,2,3,4:T(2,128)S(1)} %pad_maximum_fusion.5), channel_id=1, source_target_pairs={{0,96},{1,97},{2,98},{3,99},{4,100},{5,101},{6,102},{7,103},{8,104... | collective-permute-start | bytes 884744 | tf_op jit(solution)/shard_map/ppermute | solution.py:41
  78.6 10.4 %collective-permute-start.8 = (f32[2,2,2,2,2,18,128]{6,1,5,2,3,4,0:T(2,128)S(1)}, f32[2,2,2,2,2,18,128]{6,1,5,2,3,4,0:T(2,128)S(1)}, u32[]{:S(2)}, u32[]{:S(2)}) collective-permute-start(f32[2,2,2,2,2,18,128]{6,1,5,2,3,4,0:T(2,128)S(1)} %pad_maximum_fusion.6), channel_id=1, source_target_pairs={{0,32},{1,33},{2,34},{3,35},{4,36},{5,37},{6,38},{7,39},{8,40},{9,... | collective-permute-start | bytes 884744 | tf_op jit(solution)/shard_map/ppermute | solution.py:41
  87.0 16.9 %collective-permute-start.6 = (f32[2,2,2,2,2,2,18,128]{7,5,6,4,3,2,1,0:T(2,128)S(1)}, f32[2,2,2,2,2,2,18,128]{7,5,6,4,3,2,1,0:T(2,128)S(1)}, u32[]{:S(2)}, u32[]{:S(2)}) collective-permute-start(f32[2,2,2,2,2,2,18,128]{7,5,6,4,3,2,1,0:T(2,128)S(1)} %copy.80), channel_id=1, source_target_pairs={{0,32},{1,33},{2,34},{3,35},{4,36},{5,37},{6,38},{7,39},{8,40},{9,... | collective-permute-start | bytes 1769480 | tf_op jit(solution)/shard_map/ppermute | solution.py:41
  89.8 16.4 %collective-permute-start.9 = (f32[2,2,2,2,2,2,18,128]{7,5,6,4,3,2,1,0:T(2,128)S(1)}, f32[2,2,2,2,2,2,18,128]{7,5,6,4,3,2,1,0:T(2,128)S(1)}, u32[]{:S(2)}, u32[]{:S(2)}) collective-permute-start(f32[2,2,2,2,2,2,18,128]{7,5,6,4,3,2,1,0:T(2,128)S(1)} %copy.84), channel_id=1, source_target_pairs={{0,1},{1,0},{2,3},{3,2},{4,5},{5,4},{6,7},{7,6},{8,9},{9,8},{10,11... | collective-permute-start | bytes 1769480 | tf_op jit(solution)/shard_map/ppermute | solution.py:41
  113.1 2.0 %copy-start = (f32[1536,256]{1,0:T(8,128)S(1)}, f32[1536,256]{1,0:T(8,128)}, u32[]{:S(2)}) copy-start(f32[1536,256]{1,0:T(8,128)} %param.5) | copy-start | bytes 4718596
  115.2 1.4 copy-start.2
  117.8 1.1 copy-start.1
  119.0 5.6 %copy-start.3 = (f32[2,32,4,256]{3,1,2,0:T(8,128)S(1)}, f32[2,32,4,256]{3,1,2,0:T(8,128)}, u32[]{:S(2)}) copy-start(f32[2,32,4,256]{3,1,2,0:T(8,128)} %get-tuple-element.37) | copy-start | bytes 786436
  119.0 7.7 %collective-permute-start.10 = (f32[512,256]{1,0:T(8,128)S(1)}, f32[512,256]{1,0:T(8,128)S(1)}, u32[]{:S(2)}, u32[]{:S(2)}) collective-permute-start(f32[512,256]{1,0:T(8,128)S(1)} %pad_maximum_fusion.4), channel_id=1, source_target_pairs={{0,128},{128,0},{256,384},{384,256},{512,640},{640,512},{768,896},... | collective-permute-start | bytes 1572872 | tf_op jit(solution)/shard_map/ppermute | solution.py:10
  124.8 9.7 %collective-permute-start.12 = (f32[256,256]{1,0:T(8,128)S(1)}, f32[256,256]{1,0:T(8,128)S(1)}, u32[]{:S(2)}, u32[]{:S(2)}) collective-permute-start(f32[256,256]{1,0:T(8,128)S(1)} %slice.257), channel_id=1, source_target_pairs={{0,256},{128,384},{256,0},{384,128},{512,768},{640,896},{768,512},... | collective-permute-start | bytes 786440 | tf_op jit(solution)/shard_map/ppermute | solution.py:10
  129.9 10.3 %collective-permute-start.11 = (f32[256,256]{1,0:T(8,128)S(1)}, f32[256,256]{1,0:T(8,128)S(1)}, u32[]{:S(2)}, u32[]{:S(2)}) collective-permute-start(f32[256,256]{1,0:T(8,128)S(1)} %subtract_select_fusion), channel_id=1, source_target_pairs={{0,256},{128,384},{256,0},{384,128},{512,768},{640,896},{768,512},... | collective-permute-start | bytes 786440 | tf_op jit(solution)/shard_map/ppermute | solution.py:10

commit v7 on v5

--- a/solution.py
+++ b/solution.py
@@ -49,10 +49,17 @@
     width = shard.shape[1] // len(orders)
     bufs = [buf[..., j * width:(j + 1) * width] for j in range(len(orders))]
     helds = [held] * len(orders)
-    for k in range(len(orders[0])):
+    for k in range(len(orders[0]) - 1):
         for j, order in enumerate(orders):
             bufs[j], helds[j] = step(bufs[j], helds[j], order[k])
-    return [b.reshape((n,) + shard.shape[:1] + (width,)) for b in bufs]
+    pieces = []
+    for buf, held, order in zip(bufs, helds, orders):
+        bit = order[-1]
+        got = lax.ppermute(buf, axis, [(i, unlabel[label(i) ^ 1 << bit]) for i in range(n)])
+        low = (me >> bit) & 1 == 0
+        pos = sum(1 for b in held if b > bit)
+        pieces.append((jnp.where(low, buf, got), jnp.where(low, got, buf), pos))
+    return pieces
 
 
 def combine(top_rows, refl_mine, partner_refl, level):
@@ -96,8 +103,9 @@
 
     def joined(lo, hi):
         parts = []
-        for p in pieces:
-            groups = p[:, lo:hi].reshape(n_x, z_len, hi - lo, p.shape[2])
+        for low_half, high_half, pos in pieces:
+            p = jnp.stack([low_half[..., lo:hi, :], high_half[..., lo:hi, :]], axis=pos)
+            groups = p.reshape(n_x, z_len, hi - lo, p.shape[-1])
             parts.append(jnp.concatenate([groups[g][None] for g in x_order], axis=0))
         return jnp.concatenate(parts, axis=3).reshape(-1, width)
 

time: 146 us -> 149 us (1.021)
    ppermute x0 -> x2, waiting for transfers between devices: none -> 12 us  [doubling_gather(): lax.ppermute(buf, axis, [(i, unlabel[label(i) ^ 1 << bit]) for i in range...]
    ppermute x10 -> x8, waiting for transfers between devices: 32.1 us -> 20.1 us  [step(): lax.ppermute(buf, axis, [(i, unlabel[label(i) ^ 1 << bit]) for i in range...]
    ppermute x10 -> x8, starting transfers between devices: 66.6 us -> 62.6 us  [step(): lax.ppermute(buf, axis, [(i, unlabel[label(i) ^ 1 << bit]) for i in range...]
    ppermute x0 -> x2, starting transfers between devices: none -> 4.02 us  [doubling_gather(): lax.ppermute(buf, axis, [(i, unlabel[label(i) ^ 1 << bit]) for i in range...]
    another operation x20 -> x16, other arithmetic: 5.22 us -> 2.73 us  [step(): jnp.stack([jnp.where(low, buf, got), jnp.where(low, got, buf)], axis=pos)]
    another operation x0 -> x12, local copies, waits for them, and re-layouts: none -> 2.08 us  [joined(): p = jnp.stack([low_half[..., lo:hi, :], high_half[..., lo:hi, :]], axis=pos)]
    another operation x6 -> x4, local copies, waits for them, and re-layouts: 2.62 us -> 0.8 us  [step(): jnp.stack([jnp.where(low, buf, got), jnp.where(low, got, buf)], axis=pos)]
    another operation x0 -> x12, other arithmetic: none -> 1.75 us  [joined(): p = jnp.stack([low_half[..., lo:hi, :], high_half[..., lo:hi, :]], axis=pos)]
  transfers between devices with their start and end apart: 13 -> 13, of which waited for: 8 -> 8; matrix products, arithmetic and copies ran while one was open for 6% -> 5% of each run, Pallas kernels for 0% -> 0%
where the time goes in v7:
time: 149 us; the launch traced here: 148 us
  starting transfers between devices  78.7 us (53%)
  waiting for transfers between devices  38.4 us (26%)
  local copies, waits for them, and re-layouts  11.7 us (8%)
  matrix products  10.7 us (7%)
  other arithmetic  7.44 us (5%)
    ppermute x8, starting transfers between devices, step(): lax.ppermute(buf, axis, [(i, unlabel[label(i) ^ 1 << bit]) for i in range...  62.6 us
    ppermute x8, waiting for transfers between devices, step(): lax.ppermute(buf, axis, [(i, unlabel[label(i) ^ 1 << bit]) for i in range...  20.1 us
    ppermute x3, starting transfers between devices, swapped(): lax.ppermute(shard, axis, [(i, i ^ 1 << stride) for i in range(lax.axis_s...  12.1 us
    ppermute x2, waiting for transfers between devices, doubling_gather(): lax.ppermute(buf, axis, [(i, unlabel[label(i) ^ 1 << bit]) for i in range...  12 us
    dot_general x6, matrix products, inner(): lax.dot_general(left, right, (((0,), (0,)), ((), ())), precision=lax.Prec...  6.78 us
    ppermute x3, waiting for transfers between devices, swapped(): lax.ppermute(shard, axis, [(i, i ^ 1 << stride) for i in range(lax.axis_s...  6.37 us
    ppermute x2, starting transfers between devices, doubling_gather(): lax.ppermute(buf, axis, [(i, unlabel[label(i) ^ 1 << bit]) for i in range...  4.02 us
    dot_general x3, matrix products, matmul(): jnp.dot(left, right, precision=lax.Precision.HIGHEST, preferred_element_t...  3.91 us
  transfers between devices with their start and end apart: 13, of which 8 were waited for; matrix products, arithmetic and copies ran while one was open for 5% of the time, Pallas kernels for 0%

profile of v7, /device:TPU:1, one launch (start us, length us, event | category | flops | bytes accessed | tf_op | source)
XLA Modules:
  0.0 147.8 jit_solution(16967558339773693096)
XLA Ops:
  0.0 0.7 broadcast_select_fusion.13
  0.7 0.7 pad_maximum_fusion.15
  1.4 29.5 %collective-permute-start = (f32[18,256]{1,0:T(8,128)S(1)}, f32[18,256]{1,0:T(8,128)S(1)}, u32[]{:S(2)}, u32[]{:S(2)}) collective-permute-start(f32[18,256]{1,0:T(8,128)S(1)} %pad_maximum_fusion.15), channel_id=1, source_target_pairs={{0,16},{1,17},{2,18},{3,19},{4,20},{5,21},{6,22},{7,23},{8,24},{9,... | collective-permute-start | bytes 55304 | tf_op jit(solution)/shard_map/ppermute | solution.py:41
  31.0 1.3 collective-permute-done
  32.3 0.7 select_bitcast_fusion.14
  33.1 8.4 %collective-permute-start.1 = (f32[2,18,256]{2,0,1:T(2,128)S(1)}, f32[2,18,256]{2,0,1:T(2,128)S(1)}, u32[]{:S(2)}, u32[]{:S(2)}) collective-permute-start(f32[2,18,256]{2,0,1:T(2,128)S(1)} %pad_maximum_fusion.14), channel_id=1, source_target_pairs={{0,8},{1,9},{2,10},{3,11},{4,12},{5,13},{6,14},{7,15},{8,0},{9,1},... | collective-permute-start | bytes 110600 | tf_op jit(solution)/shard_map/ppermute | solution.py:41
  41.5 5.0 %collective-permute-done.1 = f32[2,18,256]{2,0,1:T(2,128)S(1)} collective-permute-done((f32[2,18,256]{2,0,1:T(2,128)S(1)}, f32[2,18,256]{2,0,1:T(2,128)S(1)}, u32[]{:S(2)}, u32[]{:S(2)}) %collective-permute-start.1) | collective-permute-done | bytes 36896 | tf_op jit(solution)/shard_map/ppermute | solution.py:41
  46.6 5.2 %collective-permute-start.2 = (f32[2,2,18,256]{3,0,2,1:T(2,128)S(1)}, f32[2,2,18,256]{3,0,2,1:T(2,128)S(1)}, u32[]{:S(2)}, u32[]{:S(2)}) collective-permute-start(f32[2,2,18,256]{3,0,2,1:T(2,128)S(1)} %pad_maximum_fusion.13), channel_id=1, source_target_pairs={{0,4},{1,5},{2,6},{3,7},{4,0},{5,1},{6,2},{7,3},{8,12},{9,13},{10,... | collective-permute-start | bytes 221192 | tf_op jit(solution)/shard_map/ppermute | solution.py:41
  51.8 4.6 %collective-permute-done.2 = f32[2,2,18,256]{3,0,2,1:T(2,128)S(1)} collective-permute-done((f32[2,2,18,256]{3,0,2,1:T(2,128)S(1)}, f32[2,2,18,256]{3,0,2,1:T(2,128)S(1)}, u32[]{:S(2)}, u32[]{:S(2)}) %collective-permute-start.2) | collective-permute-done | bytes 73760 | tf_op jit(solution)/shard_map/ppermute | solution.py:41
  56.6 4.0 %collective-permute-start.3 = (f32[2,2,2,18,256]{4,0,3,1,2:T(2,128)S(1)}, f32[2,2,2,18,256]{4,0,3,1,2:T(2,128)S(1)}, u32[]{:S(2)}, u32[]{:S(2)}) collective-permute-start(f32[2,2,2,18,256]{4,0,3,1,2:T(2,128)S(1)} %pad_maximum_fusion.10), channel_id=1, source_target_pairs={{0,2},{1,3},{2,0},{3,1},{4,6},{5,7},{6,4},{7,5},{8,10},{9,11},{10,... | collective-permute-start | bytes 442376 | tf_op jit(solution)/shard_map/ppermute | solution.py:41
  60.5 3.5 %collective-permute-done.3 = f32[2,2,2,18,256]{4,0,3,1,2:T(2,128)S(1)} collective-permute-done((f32[2,2,2,18,256]{4,0,3,1,2:T(2,128)S(1)}, f32[2,2,2,18,256]{4,0,3,1,2:T(2,128)S(1)}, u32[]{:S(2)}, u32[]{:S(2)}) %collective-permute-start.3) | collective-permute-done | bytes 147488 | tf_op jit(solution)/shard_map/ppermute | solution.py:41
  64.2 0.1 fusion.16
  64.4 5.3 %collective-permute-start.4 = (f32[2,2,2,2,18,128]{5,0,4,1,2,3:T(2,128)S(1)}, f32[2,2,2,2,18,128]{5,0,4,1,2,3:T(2,128)S(1)}, u32[]{:S(2)}, u32[]{:S(2)}) collective-permute-start(f32[2,2,2,2,18,128]{5,0,4,1,2,3:T(2,128)S(1)} %get-tuple-element.21), channel_id=1, source_target_pairs={{0,1},{1,0},{2,3},{3,2},{4,5},{5,4},{6,7},{7,6},{8,9},{9,8},{10,11... | collective-permute-start | bytes 442376 | tf_op jit(solution)/shard_map/ppermute | solution.py:41
  69.7 5.9 %collective-permute-start.7 = (f32[2,2,2,2,18,128]{5,0,4,1,2,3:T(2,128)S(1)}, f32[2,2,2,2,18,128]{5,0,4,1,2,3:T(2,128)S(1)}, u32[]{:S(2)}, u32[]{:S(2)}) collective-permute-start(f32[2,2,2,2,18,128]{5,0,4,1,2,3:T(2,128)S(1)} %get-tuple-element.22), channel_id=1, source_target_pairs={{0,96},{1,97},{2,98},{3,99},{4,100},{5,101},{6,102},{7,103},{8,104... | collective-permute-start | bytes 442376 | tf_op jit(solution)/shard_map/ppermute | solution.py:41
  75.7 0.1 pad_maximum_fusion.5
  75.8 2.5 %collective-permute-start.5 = (f32[2,2,2,2,2,18,128]{6,0,5,1,2,3,4:T(2,128)S(1)}, f32[2,2,2,2,2,18,128]{6,0,5,1,2,3,4:T(2,128)S(1)}, u32[]{:S(2)}, u32[]{:S(2)}) collective-permute-start(f32[2,2,2,2,2,18,128]{6,0,5,1,2,3,4:T(2,128)S(1)} %pad_maximum_fusion.5), channel_id=1, source_target_pairs={{0,96},{1,97},{2,98},{3,99},{4,100},{5,101},{6,102},{7,103},{8,104... | collective-permute-start | bytes 884744 | tf_op jit(solution)/shard_map/ppermute | solution.py:41
  78.6 1.9 %collective-permute-start.8 = (f32[2,2,2,2,2,18,128]{6,1,5,2,3,4,0:T(2,128)S(1)}, f32[2,2,2,2,2,18,128]{6,1,5,2,3,4,0:T(2,128)S(1)}, u32[]{:S(2)}, u32[]{:S(2)}) collective-permute-start(f32[2,2,2,2,2,18,128]{6,1,5,2,3,4,0:T(2,128)S(1)} %pad_maximum_fusion.6), channel_id=1, source_target_pairs={{0,32},{1,33},{2,34},{3,35},{4,36},{5,37},{6,38},{7,39},{8,40},{9,... | collective-permute-start | bytes 884744 | tf_op jit(solution)/shard_map/ppermute | solution.py:41
  80.5 5.6 %collective-permute-done.5 = f32[2,2,2,2,2,18,128]{6,0,5,1,2,3,4:T(2,128)S(1)} collective-permute-done((f32[2,2,2,2,2,18,128]{6,0,5,1,2,3,4:T(2,128)S(1)}, f32[2,2,2,2,2,18,128]{6,0,5,1,2,3,4:T(2,128)S(1)}, u32[]{:S(2)}, u32[]{:S(2)}) %collective-permute-start.5) | collective-permute-done | bytes 294944 | tf_op jit(solution)/shard_map/ppermute | solution.py:41
  86.1 0.2 select_bitcast_fusion.3
  86.3 0.3 pad_maximum_fusion.2
  86.6 0.5 copy.130
  87.0 1.9 %collective-permute-start.6 = (f32[2,2,2,2,2,2,18,128]{7,5,6,4,3,2,1,0:T(2,128)S(1)}, f32[2,2,2,2,2,2,18,128]{7,5,6,4,3,2,1,0:T(2,128)S(1)}, u32[]{:S(2)}, u32[]{:S(2)}) collective-permute-start(f32[2,2,2,2,2,2,18,128]{7,5,6,4,3,2,1,0:T(2,128)S(1)} %copy.130), channel_id=1, source_target_pairs={{0,32},{1,33},{2,34},{3,35},{4,36},{5,37},{6,38},{7,39},{8,40},{9,... | collective-permute-start | bytes 1769480 | tf_op jit(solution)/shard_map/ppermute | solution.py:58
  89.0 0.2 select_bitcast_fusion.1
  89.2 0.3 pad_maximum_fusion.3
  89.5 0.3 copy.135
  89.8 2.1 %collective-permute-start.9 = (f32[2,2,2,2,2,2,18,128]{7,5,6,4,3,2,1,0:T(2,128)S(1)}, f32[2,2,2,2,2,2,18,128]{7,5,6,4,3,2,1,0:T(2,128)S(1)}, u32[]{:S(2)}, u32[]{:S(2)}) collective-permute-start(f32[2,2,2,2,2,2,18,128]{7,5,6,4,3,2,1,0:T(2,128)S(1)} %copy.135), channel_id=1, source_target_pairs={{0,1},{1,0},{2,3},{3,2},{4,5},{5,4},{6,7},{7,6},{8,9},{9,8},{10,11... | collective-permute-start | bytes 1769480 | tf_op jit(solution)/shard_map/ppermute | solution.py:58
  91.9 12.0 %collective-permute-done.6 = f32[2,2,2,2,2,2,18,128]{7,5,6,4,3,2,1,0:T(2,128)S(1)} collective-permute-done((f32[2,2,2,2,2,2,18,128]{7,5,6,4,3,2,1,0:T(2,128)S(1)}, f32[2,2,2,2,2,2,18,128]{7,5,6,4,3,2,1,0:T(2,128)S(1)}, u32[]{:S(2)}, u32[]{:S(2)}) %collective-permute-start.6) | collective-permute-done | bytes 589856 | tf_op jit(solution)/shard_map/ppermute | solution.py:58
  103.9 0.7 broadcast_select_fusion.3
  104.9 0.5 broadcast_select_fusion.1
  105.5 0.1 pad_maximum_fusion.8
  106.1 0.2 fusion.6
  106.3 0.4 pad_maximum_fusion
  106.8 0.2 fusion.5
  107.0 0.4 pad_maximum_fusion.1
  107.5 0.2 copy.147
  107.7 0.2 copy.149
  108.1 0.7 fusion.39
  108.9 0.2 copy.150
  109.5 0.2 copy.145
  109.7 0.9 reshape.38
  110.6 0.3 copy.133
  110.9 0.6 copy.134
  111.6 0.3 copy.138
  111.9 0.6 copy.139
  112.6 0.1 maximum_maximum_fusion
  112.7 2.3 %copy.140 = f32[4,32,12,256]{3,2,1,0:T(8,128)} copy(f32[4,32,12,256]{3,1,2,0:T(8,128)S(1)} %maximum_maximum_fusion) | data formatting | bytes 3145728 | tf_op jit(solution)/shard_map/concatenate | solution.py:110
  115.0 1.7 %reshape.35 = f32[1536,256]{1,0:T(8,128)S(1)} reshape(f32[4,32,12,256]{3,2,1,0:T(8,128)} %copy.140) | data formatting | bytes 3145728 | tf_op jit(solution)/shard_map/reshape | solution.py:110
  116.7 0.3 copy-done
  117.0 2.5 %fusion = f32[256,256]{1,0:T(8,128)S(1)} fusion(f32[1536,256]{1,0:T(8,128)S(1)} %copy-done, f32[1536,256]{1,0:T(8,128)S(1)} %reshape.35), kind=kOutput, calls=%fused_computation.5 | convolution fusion | flops 1209532416 | bytes 3407872 | tf_op jit(solution)/shard_map/dot_general | solution.py:22
  119.6 0.7 fusion.13
  120.3 1.5 convolution_subtract_fusion
  121.7 1.1 copy-done.1
  122.9 6.8 %collective-permute-start.10 = (f32[512,256]{1,0:T(8,128)S(1)}, f32[512,256]{1,0:T(8,128)S(1)}, u32[]{:S(2)}, u32[]{:S(2)}) collective-permute-start(f32[512,256]{1,0:T(8,128)S(1)} %pad_maximum_fusion.4), channel_id=1, source_target_pairs={{0,128},{128,0},{256,384},{384,256},{512,640},{640,512},{768,896},... | collective-permute-start | bytes 1572872 | tf_op jit(solution)/shard_map/ppermute | solution.py:10
  129.7 0.2 copy.151
  130.0 1.9 %collective-permute-start.12 = (f32[256,256]{1,0:T(8,128)S(1)}, f32[256,256]{1,0:T(8,128)S(1)}, u32[]{:S(2)}, u32[]{:S(2)}) collective-permute-start(f32[256,256]{1,0:T(8,128)S(1)} %slice.191), channel_id=1, source_target_pairs={{0,256},{128,384},{256,0},{384,128},{512,768},{640,896},{768,512},... | collective-permute-start | bytes 786440 | tf_op jit(solution)/shard_map/ppermute | solution.py:10
  131.9 1.6 %convolution_add_fusion.1 = f32[256,256]{1,0:T(8,128)S(1)} fusion(f32[512,256]{1,0:T(8,128)S(1)} %collective-permute-done.10, pred[]{:T(512)S(6)} %eq.49, f32[256,256]{1,0:T(8,128)S(1)} %slice.187, f32[1536,256]{1,0:T(8,128)} %copy-done.1), kind=kOutput, calls=%fused_computation.9 | convolution fusion | flops 201588736 | bytes 1836544 | tf_op jit(solution)/shard_map/dot_general | solution.py:22
  133.6 0.7 fusion.10
  134.3 1.3 subtract_select_fusion
  135.6 3.4 %collective-permute-start.11 = (f32[256,256]{1,0:T(8,128)S(1)}, f32[256,256]{1,0:T(8,128)S(1)}, u32[]{:S(2)}, u32[]{:S(2)}) collective-permute-start(f32[256,256]{1,0:T(8,128)S(1)} %subtract_select_fusion), channel_id=1, source_target_pairs={{0,256},{128,384},{256,0},{384,128},{512,768},{640,896},{768,512},... | collective-permute-start | bytes 786440 | tf_op jit(solution)/shard_map/ppermute | solution.py:10
  139.0 0.7 collective-permute-done.12
  139.7 5.6 %collective-permute-done.11 = f32[256,256]{1,0:T(8,128)S(1)} collective-permute-done((f32[256,256]{1,0:T(8,128)S(1)}, f32[256,256]{1,0:T(8,128)S(1)}, u32[]{:S(2)}, u32[]{:S(2)}) %collective-permute-start.11) | collective-permute-done | bytes 262176 | tf_op jit(solution)/shard_map/ppermute | solution.py:10
  145.4 0.6 convolution_add_fusion
  146.0 0.7 fusion.7
  146.7 1.1 select_dynamic-update-slice_fusion
  (54 shorter events, 2.4 us)
Async XLA Ops:
  1.4 30.8 %collective-permute-start = (f32[18,256]{1,0:T(8,128)S(1)}, f32[18,256]{1,0:T(8,128)S(1)}, u32[]{:S(2)}, u32[]{:S(2)}) collective-permute-start(f32[18,256]{1,0:T(8,128)S(1)} %pad_maximum_fusion.15), channel_id=1, source_target_pairs={{0,16},{1,17},{2,18},{3,19},{4,20},{5,21},{6,22},{7,23},{8,24},{9,... | collective-permute-start | bytes 55304 | tf_op jit(solution)/shard_map/ppermute | solution.py:41
  33.1 13.4 %collective-permute-start.1 = (f32[2,18,256]{2,0,1:T(2,128)S(1)}, f32[2,18,256]{2,0,1:T(2,128)S(1)}, u32[]{:S(2)}, u32[]{:S(2)}) collective-permute-start(f32[2,18,256]{2,0,1:T(2,128)S(1)} %pad_maximum_fusion.14), channel_id=1, source_target_pairs={{0,8},{1,9},{2,10},{3,11},{4,12},{5,13},{6,14},{7,15},{8,0},{9,1},... | collective-permute-start | bytes 110600 | tf_op jit(solution)/shard_map/ppermute | solution.py:41
  46.6 9.8 %collective-permute-start.2 = (f32[2,2,18,256]{3,0,2,1:T(2,128)S(1)}, f32[2,2,18,256]{3,0,2,1:T(2,128)S(1)}, u32[]{:S(2)}, u32[]{:S(2)}) collective-permute-start(f32[2,2,18,256]{3,0,2,1:T(2,128)S(1)} %pad_maximum_fusion.13), channel_id=1, source_target_pairs={{0,4},{1,5},{2,6},{3,7},{4,0},{5,1},{6,2},{7,3},{8,12},{9,13},{10,... | collective-permute-start | bytes 221192 | tf_op jit(solution)/shard_map/ppermute | solution.py:41
  56.6 7.5 %collective-permute-start.3 = (f32[2,2,2,18,256]{4,0,3,1,2:T(2,128)S(1)}, f32[2,2,2,18,256]{4,0,3,1,2:T(2,128)S(1)}, u32[]{:S(2)}, u32[]{:S(2)}) collective-permute-start(f32[2,2,2,18,256]{4,0,3,1,2:T(2,128)S(1)} %pad_maximum_fusion.10), channel_id=1, source_target_pairs={{0,2},{1,3},{2,0},{3,1},{4,6},{5,7},{6,4},{7,5},{8,10},{9,11},{10,... | collective-permute-start | bytes 442376 | tf_op jit(solution)/shard_map/ppermute | solution.py:41
  64.4 11.2 %collective-permute-start.4 = (f32[2,2,2,2,18,128]{5,0,4,1,2,3:T(2,128)S(1)}, f32[2,2,2,2,18,128]{5,0,4,1,2,3:T(2,128)S(1)}, u32[]{:S(2)}, u32[]{:S(2)}) collective-permute-start(f32[2,2,2,2,18,128]{5,0,4,1,2,3:T(2,128)S(1)} %get-tuple-element.21), channel_id=1, source_target_pairs={{0,1},{1,0},{2,3},{3,2},{4,5},{5,4},{6,7},{7,6},{8,9},{9,8},{10,11... | collective-permute-start | bytes 442376 | tf_op jit(solution)/shard_map/ppermute | solution.py:41
  69.7 8.6 %collective-permute-start.7 = (f32[2,2,2,2,18,128]{5,0,4,1,2,3:T(2,128)S(1)}, f32[2,2,2,2,18,128]{5,0,4,1,2,3:T(2,128)S(1)}, u32[]{:S(2)}, u32[]{:S(2)}) collective-permute-start(f32[2,2,2,2,18,128]{5,0,4,1,2,3:T(2,128)S(1)} %get-tuple-element.22), channel_id=1, source_target_pairs={{0,96},{1,97},{2,98},{3,99},{4,100},{5,101},{6,102},{7,103},{8,104... | collective-permute-start | bytes 442376 | tf_op jit(solution)/shard_map/ppermute | solution.py:41
  75.8 10.3 %collective-permute-start.5 = (f32[2,2,2,2,2,18,128]{6,0,5,1,2,3,4:T(2,128)S(1)}, f32[2,2,2,2,2,18,128]{6,0,5,1,2,3,4:T(2,128)S(1)}, u32[]{:S(2)}, u32[]{:S(2)}) collective-permute-start(f32[2,2,2,2,2,18,128]{6,0,5,1,2,3,4:T(2,128)S(1)} %pad_maximum_fusion.5), channel_id=1, source_target_pairs={{0,96},{1,97},{2,98},{3,99},{4,100},{5,101},{6,102},{7,103},{8,104... | collective-permute-start | bytes 884744 | tf_op jit(solution)/shard_map/ppermute | solution.py:41
  78.6 10.4 %collective-permute-start.8 = (f32[2,2,2,2,2,18,128]{6,1,5,2,3,4,0:T(2,128)S(1)}, f32[2,2,2,2,2,18,128]{6,1,5,2,3,4,0:T(2,128)S(1)}, u32[]{:S(2)}, u32[]{:S(2)}) collective-permute-start(f32[2,2,2,2,2,18,128]{6,1,5,2,3,4,0:T(2,128)S(1)} %pad_maximum_fusion.6), channel_id=1, source_target_pairs={{0,32},{1,33},{2,34},{3,35},{4,36},{5,37},{6,38},{7,39},{8,40},{9,... | collective-permute-start | bytes 884744 | tf_op jit(solution)/shard_map/ppermute | solution.py:41
  87.0 16.9 %collective-permute-start.6 = (f32[2,2,2,2,2,2,18,128]{7,5,6,4,3,2,1,0:T(2,128)S(1)}, f32[2,2,2,2,2,2,18,128]{7,5,6,4,3,2,1,0:T(2,128)S(1)}, u32[]{:S(2)}, u32[]{:S(2)}) collective-permute-start(f32[2,2,2,2,2,2,18,128]{7,5,6,4,3,2,1,0:T(2,128)S(1)} %copy.130), channel_id=1, source_target_pairs={{0,32},{1,33},{2,34},{3,35},{4,36},{5,37},{6,38},{7,39},{8,40},{9,... | collective-permute-start | bytes 1769480 | tf_op jit(solution)/shard_map/ppermute | solution.py:58
  89.8 15.1 %collective-permute-start.9 = (f32[2,2,2,2,2,2,18,128]{7,5,6,4,3,2,1,0:T(2,128)S(1)}, f32[2,2,2,2,2,2,18,128]{7,5,6,4,3,2,1,0:T(2,128)S(1)}, u32[]{:S(2)}, u32[]{:S(2)}) collective-permute-start(f32[2,2,2,2,2,2,18,128]{7,5,6,4,3,2,1,0:T(2,128)S(1)} %copy.135), channel_id=1, source_target_pairs={{0,1},{1,0},{2,3},{3,2},{4,5},{5,4},{6,7},{7,6},{8,9},{9,8},{10,11... | collective-permute-start | bytes 1769480 | tf_op jit(solution)/shard_map/ppermute | solution.py:58
  115.0 2.0 %copy-start = (f32[1536,256]{1,0:T(8,128)S(1)}, f32[1536,256]{1,0:T(8,128)}, u32[]{:S(2)}) copy-start(f32[1536,256]{1,0:T(8,128)} %param.5) | copy-start | bytes 4718596
  117.0 2.6 %copy-start.2 = (f32[256,256]{1,0:T(8,128)S(1)}, f32[256,256]{1,0:T(8,128)}, u32[]{:S(2)}) copy-start(f32[256,256]{1,0:T(8,128)} %reshape.38) | copy-start | bytes 786436
  121.7 1.1 copy-start.1
  122.9 6.9 %copy-start.3 = (f32[2,32,4,256]{3,1,2,0:T(8,128)S(1)}, f32[2,32,4,256]{3,1,2,0:T(8,128)}, u32[]{:S(2)}) copy-start(f32[2,32,4,256]{3,1,2,0:T(8,128)} %get-tuple-element.17) | copy-start | bytes 786436
  122.9 9.0 %collective-permute-start.10 = (f32[512,256]{1,0:T(8,128)S(1)}, f32[512,256]{1,0:T(8,128)S(1)}, u32[]{:S(2)}, u32[]{:S(2)}) collective-permute-start(f32[512,256]{1,0:T(8,128)S(1)} %pad_maximum_fusion.4), channel_id=1, source_target_pairs={{0,128},{128,0},{256,384},{384,256},{512,640},{640,512},{768,896},... | collective-permute-start | bytes 1572872 | tf_op jit(solution)/shard_map/ppermute | solution.py:10
  130.0 9.7 %collective-permute-start.12 = (f32[256,256]{1,0:T(8,128)S(1)}, f32[256,256]{1,0:T(8,128)S(1)}, u32[]{:S(2)}, u32[]{:S(2)}) collective-permute-start(f32[256,256]{1,0:T(8,128)S(1)} %slice.191), channel_id=1, source_target_pairs={{0,256},{128,384},{256,0},{384,128},{512,768},{640,896},{768,512},... | collective-permute-start | bytes 786440 | tf_op jit(solution)/shard_map/ppermute | solution.py:10
  135.6 9.8 %collective-permute-start.11 = (f32[256,256]{1,0:T(8,128)S(1)}, f32[256,256]{1,0:T(8,128)S(1)}, u32[]{:S(2)}, u32[]{:S(2)}) collective-permute-start(f32[256,256]{1,0:T(8,128)S(1)} %subtract_select_fusion), channel_id=1, source_target_pairs={{0,256},{128,384},{256,0},{384,128},{512,768},{640,896},{768,512},... | collective-permute-start | bytes 786440 | tf_op jit(solution)/shard_map/ppermute | solution.py:10

commit v8 on v5

--- a/solution.py
+++ b/solution.py
@@ -107,8 +107,8 @@
     refl = [tree_rows[level * width:(level + 1) * width] for level in range(tree_depth)]
     partner_refl = [None] + [swapped(refl[level], "row", level) for level in range(1, tree_depth)]
     coeffs = inner(jnp.triu(t_leaf), inner(v_rows, trailing))
+    top_rows = trailing[:width] - matmul(v_rows[:width], coeffs)
     updated = trailing - matmul(v_rows, coeffs)
-    top_rows = updated[:width]
     for level in range(tree_depth):
         top_rows = combine(top_rows, refl[level], partner_refl[level], level)
     return lax.dynamic_update_slice(updated, top_rows, (0, 0))

time: 146 us -> 152 us (1.041)
  local copies, waits for them, and re-layouts: 10.7 us -> 15.1 us
  matrix products: 10.7 us -> 13.5 us
  waiting for transfers between devices: 38.4 us -> 36 us
    slice x5, local copies, waits for them, and re-layouts: 1.27 us -> 4.56 us  [local(): tree_rows[level * width:(level + 1) * width]]
    ppermute x3, waiting for transfers between devices: 6.36 us -> 3.91 us  [swapped(): lax.ppermute(shard, axis, [(i, i ^ 1 << stride) for i in range(lax.axis_s...]
    dot_general x3 -> x4, matrix products: 3.91 us -> 5.48 us  [matmul(): jnp.dot(left, right, precision=lax.Precision.HIGHEST, preferred_element_t...]
  transfers between devices with their start and end apart: 13 -> 13, of which waited for: 8 -> 7; matrix products, arithmetic and copies ran while one was open for 6% -> 10% of each run, Pallas kernels for 0% -> 0%
where the time goes in v8:
time: 152 us; the launch traced here: 151 us
  starting transfers between devices  77.9 us (51%)
  waiting for transfers between devices  36 us (24%)
  local copies, waits for them, and re-layouts  15.1 us (10%)
  matrix products  13.5 us (9%)
  other arithmetic  7.76 us (5%)
    ppermute x10, starting transfers between devices, step(): lax.ppermute(buf, axis, [(i, unlabel[label(i) ^ 1 << bit]) for i in range...  66.6 us
    ppermute x10, waiting for transfers between devices, step(): lax.ppermute(buf, axis, [(i, unlabel[label(i) ^ 1 << bit]) for i in range...  32.1 us
    ppermute x3, starting transfers between devices, swapped(): lax.ppermute(shard, axis, [(i, i ^ 1 << stride) for i in range(lax.axis_s...  11.2 us
    dot_general x6, matrix products, inner(): lax.dot_general(left, right, (((0,), (0,)), ((), ())), precision=lax.Prec...  7.99 us
    dot_general x4, matrix products, matmul(): jnp.dot(left, right, precision=lax.Precision.HIGHEST, preferred_element_t...  5.48 us
    another operation x20, other arithmetic, step(): jnp.stack([jnp.where(low, buf, got), jnp.where(low, got, buf)], axis=pos)  5.22 us
    slice x5, local copies, waits for them, and re-layouts, local(): tree_rows[level * width:(level + 1) * width]  4.56 us
    ppermute x3, waiting for transfers between devices, swapped(): lax.ppermute(shard, axis, [(i, i ^ 1 << stride) for i in range(lax.axis_s...  3.91 us
  transfers between devices with their start and end apart: 13, of which 7 were waited for; matrix products, arithmetic and copies ran while one was open for 10% of the time, Pallas kernels for 0%

profile of v8, /device:TPU:1, one launch (start us, length us, event | category | flops | bytes accessed | tf_op | source)
XLA Modules:
  0.0 150.8 jit_solution(15475652790395427299)
XLA Ops:
  0.0 0.7 broadcast_select_fusion.9
  0.7 0.7 pad_maximum_fusion.11
  1.4 29.5 %collective-permute-start = (f32[18,256]{1,0:T(8,128)S(1)}, f32[18,256]{1,0:T(8,128)S(1)}, u32[]{:S(2)}, u32[]{:S(2)}) collective-permute-start(f32[18,256]{1,0:T(8,128)S(1)} %pad_maximum_fusion.11), channel_id=1, source_target_pairs={{0,16},{1,17},{2,18},{3,19},{4,20},{5,21},{6,22},{7,23},{8,24},{9,... | collective-permute-start | bytes 55304 | tf_op jit(solution)/shard_map/ppermute | solution.py:41
  31.0 1.3 collective-permute-done
  32.3 0.7 select_bitcast_fusion.18
  33.1 8.4 %collective-permute-start.1 = (f32[2,18,256]{2,0,1:T(2,128)S(1)}, f32[2,18,256]{2,0,1:T(2,128)S(1)}, u32[]{:S(2)}, u32[]{:S(2)}) collective-permute-start(f32[2,18,256]{2,0,1:T(2,128)S(1)} %pad_maximum_fusion.10), channel_id=1, source_target_pairs={{0,8},{1,9},{2,10},{3,11},{4,12},{5,13},{6,14},{7,15},{8,0},{9,1},... | collective-permute-start | bytes 110600 | tf_op jit(solution)/shard_map/ppermute | solution.py:41
  41.5 5.0 %collective-permute-done.1 = f32[2,18,256]{2,0,1:T(2,128)S(1)} collective-permute-done((f32[2,18,256]{2,0,1:T(2,128)S(1)}, f32[2,18,256]{2,0,1:T(2,128)S(1)}, u32[]{:S(2)}, u32[]{:S(2)}) %collective-permute-start.1) | collective-permute-done | bytes 36896 | tf_op jit(solution)/shard_map/ppermute | solution.py:41
  46.6 5.2 %collective-permute-start.2 = (f32[2,2,18,256]{3,0,2,1:T(2,128)S(1)}, f32[2,2,18,256]{3,0,2,1:T(2,128)S(1)}, u32[]{:S(2)}, u32[]{:S(2)}) collective-permute-start(f32[2,2,18,256]{3,0,2,1:T(2,128)S(1)} %pad_maximum_fusion.9), channel_id=1, source_target_pairs={{0,4},{1,5},{2,6},{3,7},{4,0},{5,1},{6,2},{7,3},{8,12},{9,13},{10,... | collective-permute-start | bytes 221192 | tf_op jit(solution)/shard_map/ppermute | solution.py:41
  51.8 4.6 %collective-permute-done.2 = f32[2,2,18,256]{3,0,2,1:T(2,128)S(1)} collective-permute-done((f32[2,2,18,256]{3,0,2,1:T(2,128)S(1)}, f32[2,2,18,256]{3,0,2,1:T(2,128)S(1)}, u32[]{:S(2)}, u32[]{:S(2)}) %collective-permute-start.2) | collective-permute-done | bytes 73760 | tf_op jit(solution)/shard_map/ppermute | solution.py:41
  56.6 4.0 %collective-permute-start.3 = (f32[2,2,2,18,256]{4,0,3,1,2:T(2,128)S(1)}, f32[2,2,2,18,256]{4,0,3,1,2:T(2,128)S(1)}, u32[]{:S(2)}, u32[]{:S(2)}) collective-permute-start(f32[2,2,2,18,256]{4,0,3,1,2:T(2,128)S(1)} %pad_maximum_fusion.8), channel_id=1, source_target_pairs={{0,2},{1,3},{2,0},{3,1},{4,6},{5,7},{6,4},{7,5},{8,10},{9,11},{10,... | collective-permute-start | bytes 442376 | tf_op jit(solution)/shard_map/ppermute | solution.py:41
  60.5 3.5 %collective-permute-done.3 = f32[2,2,2,18,256]{4,0,3,1,2:T(2,128)S(1)} collective-permute-done((f32[2,2,2,18,256]{4,0,3,1,2:T(2,128)S(1)}, f32[2,2,2,18,256]{4,0,3,1,2:T(2,128)S(1)}, u32[]{:S(2)}, u32[]{:S(2)}) %collective-permute-start.3) | collective-permute-done | bytes 147488 | tf_op jit(solution)/shard_map/ppermute | solution.py:41
  64.1 0.1 select_bitcast_fusion.13
  64.2 0.1 fusion.10
  64.4 5.3 %collective-permute-start.4 = (f32[2,2,2,2,18,128]{5,0,4,1,2,3:T(2,128)S(1)}, f32[2,2,2,2,18,128]{5,0,4,1,2,3:T(2,128)S(1)}, u32[]{:S(2)}, u32[]{:S(2)}) collective-permute-start(f32[2,2,2,2,18,128]{5,0,4,1,2,3:T(2,128)S(1)} %get-tuple-element.41), channel_id=1, source_target_pairs={{0,1},{1,0},{2,3},{3,2},{4,5},{5,4},{6,7},{7,6},{8,9},{9,8},{10,11... | collective-permute-start | bytes 442376 | tf_op jit(solution)/shard_map/ppermute | solution.py:41
  69.7 5.9 %collective-permute-start.7 = (f32[2,2,2,2,18,128]{5,0,4,1,2,3:T(2,128)S(1)}, f32[2,2,2,2,18,128]{5,0,4,1,2,3:T(2,128)S(1)}, u32[]{:S(2)}, u32[]{:S(2)}) collective-permute-start(f32[2,2,2,2,18,128]{5,0,4,1,2,3:T(2,128)S(1)} %get-tuple-element.42), channel_id=1, source_target_pairs={{0,96},{1,97},{2,98},{3,99},{4,100},{5,101},{6,102},{7,103},{8,104... | collective-permute-start | bytes 442376 | tf_op jit(solution)/shard_map/ppermute | solution.py:41
  75.6 0.1 select_bitcast_fusion.11
  75.7 0.1 pad_maximum_fusion.5
  75.8 2.5 %collective-permute-start.5 = (f32[2,2,2,2,2,18,128]{6,0,5,1,2,3,4:T(2,128)S(1)}, f32[2,2,2,2,2,18,128]{6,0,5,1,2,3,4:T(2,128)S(1)}, u32[]{:S(2)}, u32[]{:S(2)}) collective-permute-start(f32[2,2,2,2,2,18,128]{6,0,5,1,2,3,4:T(2,128)S(1)} %pad_maximum_fusion.5), channel_id=1, source_target_pairs={{0,96},{1,97},{2,98},{3,99},{4,100},{5,101},{6,102},{7,103},{8,104... | collective-permute-start | bytes 884744 | tf_op jit(solution)/shard_map/ppermute | solution.py:41
  78.4 0.1 pad_maximum_fusion.6
  78.6 1.9 %collective-permute-start.8 = (f32[2,2,2,2,2,18,128]{6,1,5,2,3,4,0:T(2,128)S(1)}, f32[2,2,2,2,2,18,128]{6,1,5,2,3,4,0:T(2,128)S(1)}, u32[]{:S(2)}, u32[]{:S(2)}) collective-permute-start(f32[2,2,2,2,2,18,128]{6,1,5,2,3,4,0:T(2,128)S(1)} %pad_maximum_fusion.6), channel_id=1, source_target_pairs={{0,32},{1,33},{2,34},{3,35},{4,36},{5,37},{6,38},{7,39},{8,40},{9,... | collective-permute-start | bytes 884744 | tf_op jit(solution)/shard_map/ppermute | solution.py:41
  80.5 5.6 %collective-permute-done.5 = f32[2,2,2,2,2,18,128]{6,0,5,1,2,3,4:T(2,128)S(1)} collective-permute-done((f32[2,2,2,2,2,18,128]{6,0,5,1,2,3,4:T(2,128)S(1)}, f32[2,2,2,2,2,18,128]{6,0,5,1,2,3,4:T(2,128)S(1)}, u32[]{:S(2)}, u32[]{:S(2)}) %collective-permute-start.5) | collective-permute-done | bytes 294944 | tf_op jit(solution)/shard_map/ppermute | solution.py:41
  86.1 0.2 select_bitcast_fusion.7
  86.3 0.3 pad_maximum_fusion.2
  86.6 0.5 copy.80
  87.0 1.9 %collective-permute-start.6 = (f32[2,2,2,2,2,2,18,128]{7,5,6,4,3,2,1,0:T(2,128)S(1)}, f32[2,2,2,2,2,2,18,128]{7,5,6,4,3,2,1,0:T(2,128)S(1)}, u32[]{:S(2)}, u32[]{:S(2)}) collective-permute-start(f32[2,2,2,2,2,2,18,128]{7,5,6,4,3,2,1,0:T(2,128)S(1)} %copy.80), channel_id=1, source_target_pairs={{0,32},{1,33},{2,34},{3,35},{4,36},{5,37},{6,38},{7,39},{8,40},{9,... | collective-permute-start | bytes 1769480 | tf_op jit(solution)/shard_map/ppermute | solution.py:41
  89.0 0.2 select_bitcast_fusion.5
  89.2 0.3 pad_maximum_fusion.3
  89.5 0.3 copy.84
  89.8 2.1 %collective-permute-start.9 = (f32[2,2,2,2,2,2,18,128]{7,5,6,4,3,2,1,0:T(2,128)S(1)}, f32[2,2,2,2,2,2,18,128]{7,5,6,4,3,2,1,0:T(2,128)S(1)}, u32[]{:S(2)}, u32[]{:S(2)}) collective-permute-start(f32[2,2,2,2,2,2,18,128]{7,5,6,4,3,2,1,0:T(2,128)S(1)} %copy.84), channel_id=1, source_target_pairs={{0,1},{1,0},{2,3},{3,2},{4,5},{5,4},{6,7},{7,6},{8,9},{9,8},{10,11... | collective-permute-start | bytes 1769480 | tf_op jit(solution)/shard_map/ppermute | solution.py:41
  91.9 12.0 %collective-permute-done.6 = f32[2,2,2,2,2,2,18,128]{7,5,6,4,3,2,1,0:T(2,128)S(1)} collective-permute-done((f32[2,2,2,2,2,2,18,128]{7,5,6,4,3,2,1,0:T(2,128)S(1)}, f32[2,2,2,2,2,2,18,128]{7,5,6,4,3,2,1,0:T(2,128)S(1)}, u32[]{:S(2)}, u32[]{:S(2)}) %collective-permute-start.6) | collective-permute-done | bytes 589856 | tf_op jit(solution)/shard_map/ppermute | solution.py:41
  103.9 0.7 select_bitcast_fusion.3
  104.7 0.6 pad_maximum_fusion
  105.3 0.9 copy.83
  106.2 0.5 select_bitcast_fusion.1
  106.8 0.6 pad_maximum_fusion.1
  107.4 0.9 copy.87
  108.4 0.2 slice_bitcast_fusion.3
  108.6 0.7 fusion.23
  109.3 0.2 copy.90
  109.6 0.2 copy.89
  109.8 0.9 reshape.48
  110.7 0.1 maximum_maximum_fusion
  110.9 2.3 %copy.88 = f32[4,32,12,256]{3,2,1,0:T(8,128)} copy(f32[4,32,12,256]{3,1,2,0:T(8,128)S(1)} %maximum_maximum_fusion) | data formatting | bytes 3145728 | tf_op jit(solution)/shard_map/concatenate | solution.py:102
  113.1 1.6 %reshape.47 = f32[1536,256]{1,0:T(8,128)S(1)} reshape(f32[4,32,12,256]{3,2,1,0:T(8,128)} %copy.88) | data formatting | bytes 3145728 | tf_op jit(solution)/shard_map/reshape | solution.py:102
  114.9 1.3 copy-done
  116.2 2.5 %fusion.22 = f32[256,256]{1,0:T(8,128)S(1)} fusion(f32[1536,256]{1,0:T(8,128)S(1)} %copy-done, f32[1536,256]{1,0:T(8,128)S(1)} %reshape.47), kind=kOutput, calls=%fused_computation.103 | convolution fusion | flops 1209532416 | bytes 3407872 | tf_op jit(solution)/shard_map/dot_general | solution.py:22
  118.7 0.7 fusion.7
  119.4 0.7 copy-done.4
  120.1 0.4 convolution_subtract_fusion.3
  120.5 0.7 copy-done.2
  121.2 0.8 pad_maximum_fusion.4
  122.0 5.5 %collective-permute-start.10 = (f32[512,256]{1,0:T(8,128)}, f32[512,256]{1,0:T(8,128)}, u32[]{:S(2)}, u32[]{:S(2)}) collective-permute-start(f32[512,256]{1,0:T(8,128)} %pad_maximum_fusion.4), channel_id=1, source_target_pairs={{0,128},{128,0},{256,384},{384,256},{512,640},{640,512},{768,896},... | collective-permute-start | bytes 1572872 | tf_op jit(solution)/shard_map/ppermute | solution.py:10
  127.6 1.8 %copy.91 = f32[2,32,4,256]{3,2,1,0:T(4,128)} copy(f32[2,32,4,256]{3,1,2,0:T(8,128)} %get-tuple-element.37) | data formatting | bytes 524288 | tf_op jit(solution)/shard_map/slice | solution.py:107
  129.4 1.7 %slice.261 = f32[256,256]{1,0:T(8,128)} reshape(f32[2,32,4,256]{3,2,1,0:T(4,128)} %copy.91) | data formatting | bytes 524288 | tf_op jit(solution)/shard_map/slice | solution.py:107
  131.1 2.3 %collective-permute-start.12 = (f32[256,256]{1,0:T(8,128)}, f32[256,256]{1,0:T(8,128)S(1)}, u32[]{:S(2)}, u32[]{:S(2)}) collective-permute-start(f32[256,256]{1,0:T(8,128)} %slice.261), channel_id=1, source_target_pairs={{0,256},{128,384},{256,0},{384,128},{512,768},{640,896},{768,512},... | collective-permute-start | bytes 786440 | tf_op jit(solution)/shard_map/ppermute | solution.py:10
  133.4 1.9 %convolution_add_fusion.1 = f32[256,256]{1,0:T(8,128)S(1)} fusion(f32[256,256]{1,0:T(8,128)} %copy-done.2, f32[512,256]{1,0:T(8,128)} %collective-permute-done.10, pred[]{:T(512)S(6)} %eq.49, f32[256,256]{1,0:T(8,128)S(1)} %slice.257), kind=kOutput, calls=%fused_computation.10 | convolution fusion | flops 201588736 | bytes 1836544 | tf_op jit(solution)/shard_map/dot_general | solution.py:22
  135.3 1.6 %fusion.4 = f32[256,256]{1,0:T(8,128)S(1)} fusion(f32[256,256]{1,0:T(8,128)S(1)} %convolution_add_fusion.1, f32[256,256]{1,0:T(8,128)S(1)} %slice.257, f32[512,256]{1,0:T(8,128)} %collective-permute-done.10, s32[256]{0:T(256)S(1)} %iota_add_fusion, pred[]{:T(512)S(6)} %eq.49), kind=kOutput, calls=%fused_computation.35 | convolution fusion | flops 201523200 | bytes 1049601 | tf_op jit(solution)/shard_map/dot_general | solution.py:22
  136.9 1.4 subtract_select_fusion
  138.4 3.5 %collective-permute-start.11 = (f32[256,256]{1,0:T(8,128)S(1)}, f32[256,256]{1,0:T(8,128)S(1)}, u32[]{:S(2)}, u32[]{:S(2)}) collective-permute-start(f32[256,256]{1,0:T(8,128)S(1)} %subtract_select_fusion), channel_id=1, source_target_pairs={{0,256},{128,384},{256,0},{384,128},{512,768},{640,896},{768,512},... | collective-permute-start | bytes 786440 | tf_op jit(solution)/shard_map/ppermute | solution.py:10
  141.9 2.5 %convolution_subtract_fusion = f32[1536,256]{1,0:T(8,128)} fusion(f32[1536,256]{1,0:T(8,128)S(1)} %copy-done, f32[256,256]{1,0:T(8,128)S(1)} %copy-done.5, f32[1536,256]{1,0:T(8,128)S(1)} %reshape.47), kind=kOutput, calls=%fused_computation | convolution fusion | flops 1209925632 | bytes 4980736 | tf_op jit(solution)/shard_map/dot_general | solution.py:32
  144.4 3.9 %collective-permute-done.11 = f32[256,256]{1,0:T(8,128)S(1)} collective-permute-done((f32[256,256]{1,0:T(8,128)S(1)}, f32[256,256]{1,0:T(8,128)S(1)}, u32[]{:S(2)}, u32[]{:S(2)}) %collective-permute-start.11) | collective-permute-done | bytes 262176 | tf_op jit(solution)/shard_map/ppermute | solution.py:10
  148.3 0.6 convolution_add_fusion
  149.0 0.7 fusion.1
  149.6 1.1 select_dynamic-update-slice_fusion
  (32 shorter events, 0.7 us)
Async XLA Ops:
  1.4 30.8 %collective-permute-start = (f32[18,256]{1,0:T(8,128)S(1)}, f32[18,256]{1,0:T(8,128)S(1)}, u32[]{:S(2)}, u32[]{:S(2)}) collective-permute-start(f32[18,256]{1,0:T(8,128)S(1)} %pad_maximum_fusion.11), channel_id=1, source_target_pairs={{0,16},{1,17},{2,18},{3,19},{4,20},{5,21},{6,22},{7,23},{8,24},{9,... | collective-permute-start | bytes 55304 | tf_op jit(solution)/shard_map/ppermute | solution.py:41
  33.1 13.4 %collective-permute-start.1 = (f32[2,18,256]{2,0,1:T(2,128)S(1)}, f32[2,18,256]{2,0,1:T(2,128)S(1)}, u32[]{:S(2)}, u32[]{:S(2)}) collective-permute-start(f32[2,18,256]{2,0,1:T(2,128)S(1)} %pad_maximum_fusion.10), channel_id=1, source_target_pairs={{0,8},{1,9},{2,10},{3,11},{4,12},{5,13},{6,14},{7,15},{8,0},{9,1},... | collective-permute-start | bytes 110600 | tf_op jit(solution)/shard_map/ppermute | solution.py:41
  46.6 9.8 %collective-permute-start.2 = (f32[2,2,18,256]{3,0,2,1:T(2,128)S(1)}, f32[2,2,18,256]{3,0,2,1:T(2,128)S(1)}, u32[]{:S(2)}, u32[]{:S(2)}) collective-permute-start(f32[2,2,18,256]{3,0,2,1:T(2,128)S(1)} %pad_maximum_fusion.9), channel_id=1, source_target_pairs={{0,4},{1,5},{2,6},{3,7},{4,0},{5,1},{6,2},{7,3},{8,12},{9,13},{10,... | collective-permute-start | bytes 221192 | tf_op jit(solution)/shard_map/ppermute | solution.py:41
  56.6 7.5 %collective-permute-start.3 = (f32[2,2,2,18,256]{4,0,3,1,2:T(2,128)S(1)}, f32[2,2,2,18,256]{4,0,3,1,2:T(2,128)S(1)}, u32[]{:S(2)}, u32[]{:S(2)}) collective-permute-start(f32[2,2,2,18,256]{4,0,3,1,2:T(2,128)S(1)} %pad_maximum_fusion.8), channel_id=1, source_target_pairs={{0,2},{1,3},{2,0},{3,1},{4,6},{5,7},{6,4},{7,5},{8,10},{9,11},{10,... | collective-permute-start | bytes 442376 | tf_op jit(solution)/shard_map/ppermute | solution.py:41
  64.4 11.2 %collective-permute-start.4 = (f32[2,2,2,2,18,128]{5,0,4,1,2,3:T(2,128)S(1)}, f32[2,2,2,2,18,128]{5,0,4,1,2,3:T(2,128)S(1)}, u32[]{:S(2)}, u32[]{:S(2)}) collective-permute-start(f32[2,2,2,2,18,128]{5,0,4,1,2,3:T(2,128)S(1)} %get-tuple-element.41), channel_id=1, source_target_pairs={{0,1},{1,0},{2,3},{3,2},{4,5},{5,4},{6,7},{7,6},{8,9},{9,8},{10,11... | collective-permute-start | bytes 442376 | tf_op jit(solution)/shard_map/ppermute | solution.py:41
  69.7 8.6 %collective-permute-start.7 = (f32[2,2,2,2,18,128]{5,0,4,1,2,3:T(2,128)S(1)}, f32[2,2,2,2,18,128]{5,0,4,1,2,3:T(2,128)S(1)}, u32[]{:S(2)}, u32[]{:S(2)}) collective-permute-start(f32[2,2,2,2,18,128]{5,0,4,1,2,3:T(2,128)S(1)} %get-tuple-element.42), channel_id=1, source_target_pairs={{0,96},{1,97},{2,98},{3,99},{4,100},{5,101},{6,102},{7,103},{8,104... | collective-permute-start | bytes 442376 | tf_op jit(solution)/shard_map/ppermute | solution.py:41
  75.8 10.3 %collective-permute-start.5 = (f32[2,2,2,2,2,18,128]{6,0,5,1,2,3,4:T(2,128)S(1)}, f32[2,2,2,2,2,18,128]{6,0,5,1,2,3,4:T(2,128)S(1)}, u32[]{:S(2)}, u32[]{:S(2)}) collective-permute-start(f32[2,2,2,2,2,18,128]{6,0,5,1,2,3,4:T(2,128)S(1)} %pad_maximum_fusion.5), channel_id=1, source_target_pairs={{0,96},{1,97},{2,98},{3,99},{4,100},{5,101},{6,102},{7,103},{8,104... | collective-permute-start | bytes 884744 | tf_op jit(solution)/shard_map/ppermute | solution.py:41
  78.6 10.4 %collective-permute-start.8 = (f32[2,2,2,2,2,18,128]{6,1,5,2,3,4,0:T(2,128)S(1)}, f32[2,2,2,2,2,18,128]{6,1,5,2,3,4,0:T(2,128)S(1)}, u32[]{:S(2)}, u32[]{:S(2)}) collective-permute-start(f32[2,2,2,2,2,18,128]{6,1,5,2,3,4,0:T(2,128)S(1)} %pad_maximum_fusion.6), channel_id=1, source_target_pairs={{0,32},{1,33},{2,34},{3,35},{4,36},{5,37},{6,38},{7,39},{8,40},{9,... | collective-permute-start | bytes 884744 | tf_op jit(solution)/shard_map/ppermute | solution.py:41
  87.0 16.9 %collective-permute-start.6 = (f32[2,2,2,2,2,2,18,128]{7,5,6,4,3,2,1,0:T(2,128)S(1)}, f32[2,2,2,2,2,2,18,128]{7,5,6,4,3,2,1,0:T(2,128)S(1)}, u32[]{:S(2)}, u32[]{:S(2)}) collective-permute-start(f32[2,2,2,2,2,2,18,128]{7,5,6,4,3,2,1,0:T(2,128)S(1)} %copy.80), channel_id=1, source_target_pairs={{0,32},{1,33},{2,34},{3,35},{4,36},{5,37},{6,38},{7,39},{8,40},{9,... | collective-permute-start | bytes 1769480 | tf_op jit(solution)/shard_map/ppermute | solution.py:41
  89.8 16.4 %collective-permute-start.9 = (f32[2,2,2,2,2,2,18,128]{7,5,6,4,3,2,1,0:T(2,128)S(1)}, f32[2,2,2,2,2,2,18,128]{7,5,6,4,3,2,1,0:T(2,128)S(1)}, u32[]{:S(2)}, u32[]{:S(2)}) collective-permute-start(f32[2,2,2,2,2,2,18,128]{7,5,6,4,3,2,1,0:T(2,128)S(1)} %copy.84), channel_id=1, source_target_pairs={{0,1},{1,0},{2,3},{3,2},{4,5},{5,4},{6,7},{7,6},{8,9},{9,8},{10,11... | collective-permute-start | bytes 1769480 | tf_op jit(solution)/shard_map/ppermute | solution.py:41
  114.8 1.4 copy-start
  116.2 2.6 %copy-start.6 = (f32[256,256]{1,0:T(8,128)S(1)}, f32[256,256]{1,0:T(8,128)}, u32[]{:S(2)}) copy-start(f32[256,256]{1,0:T(8,128)} %reshape.48) | copy-start | bytes 786436
  119.4 0.7 copy-start.4
  120.5 0.7 copy-start.2
  122.0 11.3 %collective-permute-start.10 = (f32[512,256]{1,0:T(8,128)}, f32[512,256]{1,0:T(8,128)}, u32[]{:S(2)}, u32[]{:S(2)}) collective-permute-start(f32[512,256]{1,0:T(8,128)} %pad_maximum_fusion.4), channel_id=1, source_target_pairs={{0,128},{128,0},{256,384},{384,256},{512,640},{640,512},{768,896},... | collective-permute-start | bytes 1572872 | tf_op jit(solution)/shard_map/ppermute | solution.py:10
  131.1 5.8 %copy-start.3 = (f32[256,256]{1,0:T(8,128)S(1)}, f32[256,256]{1,0:T(8,128)}, u32[]{:S(2)}) copy-start(f32[256,256]{1,0:T(8,128)} %copy-done.2) | copy-start | bytes 786436
  131.1 10.8 %copy-start.5 = (f32[256,256]{1,0:T(8,128)S(1)}, f32[256,256]{1,0:T(8,128)}, u32[]{:S(2)}) copy-start(f32[256,256]{1,0:T(8,128)} %copy-done.4) | copy-start | bytes 786436
  131.1 13.3 %collective-permute-start.12 = (f32[256,256]{1,0:T(8,128)}, f32[256,256]{1,0:T(8,128)S(1)}, u32[]{:S(2)}, u32[]{:S(2)}) collective-permute-start(f32[256,256]{1,0:T(8,128)} %slice.261), channel_id=1, source_target_pairs={{0,256},{128,384},{256,0},{384,128},{512,768},{640,896},{768,512},... | collective-permute-start | bytes 786440 | tf_op jit(solution)/shard_map/ppermute | solution.py:10
  138.4 10.0 %copy-start.1 = (f32[256,256]{1,0:T(8,128)S(1)}, f32[256,256]{1,0:T(8,128)}, u32[]{:S(2)}) copy-start(f32[256,256]{1,0:T(8,128)} %slice.261) | copy-start | bytes 786436
  138.4 10.0 %collective-permute-start.11 = (f32[256,256]{1,0:T(8,128)S(1)}, f32[256,256]{1,0:T(8,128)S(1)}, u32[]{:S(2)}, u32[]{:S(2)}) collective-permute-start(f32[256,256]{1,0:T(8,128)S(1)} %subtract_select_fusion), channel_id=1, source_target_pairs={{0,256},{128,384},{256,0},{384,128},{512,768},{640,896},{768,512},... | collective-permute-start | bytes 786440 | tf_op jit(solution)/shard_map/ppermute | solution.py:10
